TPU v7x, 256 devices: a whole 4x4x8 slice. The times are simulated.
256 devices in a mesh: dist: 64 (over z, x, core), sky: 4 (over y).
Axes of the slice: x: 4, y: 4, z: 8, core: 2. Of those that a mesh axis runs over, the one named last changes fastest.
Arguments:
- coarse_field: float32 [8, 512, 4096], P(None, 'dist', 'sky'), may hold values from -6 to 6
- excitations: bfloat16 [8, 1024, 16384], P(None, 'dist', 'sky'), may hold values from -6 to 6
- refine_weights: float32 [2, 4, 3, 9], replicated, may hold values from -0.875 to 0.875
- refine_sqrt: bfloat16 [2, 4, 2, 4], replicated, may hold values from -1.5 to 1.5
- halo_index: int32 [9, 4096], P(None, 'sky'), may hold values from 0 to 1279, as said below
- star_extinction: float32 [1024, 16384], P('dist', 'sky'), may hold values from 0 to 3
- star_counts: int32 [1024, 16384], P('dist', 'sky'), may hold values from 0 to 4
Outputs:
- extinction: bfloat16 [8, 1024, 16384], P(None, 'dist', 'sky')
- excitation_grad: float32 [8, 1024, 16384], P(None, 'dist', 'sky')
Inputs may be any that keep to these rules, and one draw needn't show every extreme that they name: halo_index[m, P] names the coarse pixel (P // 1024) * 1024 - 128 + halo_index[m, P], which lies within 128 pixels of P and never outside 0 .. 4095; halo_index[4, P] = 128 + P % 1024.
All inputs are finite; a program needn't handle non-finite values.
Results may differ from a plain program's by a relative error of at most 0.001.
Values sent between devices are 32-bit elements; how exact they have to be, the bound alone decides.
No kernel may reach another device: no remote copies, remote signals or barrier semaphores. Data moves between devices by JAX's collectives and lax.ppermute only.
A program may use at most 128 MiB of HBM per device.

v0:
```python
import jax
import jax.numpy as jnp
from jax import lax
from jax.sharding import PartitionSpec as P

BAND = 128


exact_mode = lax.Precision.HIGHEST


def with_halo(block, sides, width):
    for axis, dim in sides:
        count = lax.axis_size(axis)
        forward = [(i, i + 1) for i in range(count - 1)]
        backward = [(target, source) for source, target in forward]
        low = lax.ppermute(
            lax.slice_in_dim(block, block.shape[dim] - width, None, axis=dim), axis, forward
        )
        high = lax.ppermute(lax.slice_in_dim(block, 0, width, axis=dim), axis, backward)
        block = jnp.concatenate([low, block, high], axis=dim)
    return block


def entering(part, axis, combine, identity, reverse):
    count = lax.axis_size(axis)
    place = lax.axis_index(axis)
    ahead = count - 1 - place if reverse else place
    gathered = lax.all_gather(part, axis)
    state = jnp.zeros_like(part) + jnp.asarray(identity, part.dtype)

    def one(lap, state):
        source = count - 1 - lap if reverse else lap
        return combine(state, lax.dynamic_index_in_dim(gathered, source, 0, False))

    return lax.fori_loop(0, ahead, one, state)


def add_up(earlier, later):
    return earlier + later


def shards(
    coarse_field, excitations, refine_weights, refine_sqrt, halo_index, star_extinction, star_counts
):
    samples, coarse_shells, coarse_pixels = coarse_field.shape
    fine_shells = 2 * coarse_shells
    fine_pixels = 4 * coarse_pixels
    dist_count = lax.axis_size("dist")
    dist_rank = lax.axis_index("dist")
    all_shells = fine_shells * dist_count
    blocked = coarse_field.reshape(samples, coarse_shells, coarse_pixels // BAND, BAND)
    extended = with_halo(blocked, (("dist", 1), ("sky", 2)), 1)
    extended = extended.reshape(samples, coarse_shells + 2, coarse_pixels + 2 * BAND)
    nearby = extended[:, :, halo_index]
    local_part = excitations.reshape(samples, coarse_shells, 2, 4, coarse_pixels)
    refined = jnp.einsum(
        "ksabc,tqab->kstqc", local_part, refine_sqrt, preferred_element_type=jnp.float32
    )
    for offset in range(3):
        refined = refined + jnp.einsum(
            "ksmc,tqm->kstqc",
            nearby[:, offset : offset + coarse_shells],
            refine_weights[:, :, offset, :],
            precision=exact_mode,
        )
    refined = refined.reshape(samples, fine_shells, fine_pixels)
    shells = dist_rank * fine_shells + jnp.arange(fine_shells, dtype=jnp.int32)
    middle = (shells.astype(jnp.float32) + 0.5) / all_shells
    widths = 3.0 * jnp.exp(3.0 * middle - 3.0) / all_shells
    density = jnp.exp(refined) * widths[None, :, None]
    local_cum = jnp.cumsum(density, axis=1)
    totals = local_cum[:, -1, :]
    counts = star_counts.astype(jnp.float32)
    carry_in = entering(totals, "dist", add_up, jnp.zeros_like(totals), False)
    cumulative = local_cum + carry_in[:, None, :]
    misfit = counts[None] * (cumulative - star_extinction[None])
    local_back = jnp.flip(jnp.cumsum(jnp.flip(misfit, 1), axis=1), 1)
    cumulative, local_back = (cumulative, local_back)
    carry_out = entering(local_back[:, 0, :], "dist", add_up, jnp.zeros_like(totals), True)
    back = local_back + carry_out[:, None, :]
    flowing = (density * back).reshape(samples, coarse_shells, 2, 4, coarse_pixels)
    gradient = jnp.einsum(
        "kstqc,tqab->ksabc", flowing, refine_sqrt.astype(jnp.float32), precision=exact_mode
    )
    return (cumulative.astype(jnp.bfloat16), gradient.reshape(samples, fine_shells, fine_pixels))


def solution(mesh):
    placed = (
        P(None, "dist", "sky"),
        P(None, "dist", "sky"),
        P(),
        P(),
        P(None, "sky"),
        P("dist", "sky"),
        P("dist", "sky"),
    )
    return jax.shard_map(
        shards,
        mesh=mesh,
        in_specs=placed,
        out_specs=(P(None, "dist", "sky"), P(None, "dist", "sky")),
        check_vma=False,
    )
```

profile of v0, /device:TPU:1, one launch (start us, length us, event | category | flops | bytes accessed | tf_op | source)
XLA Modules:
  0.0 466.1 jit_solution(4743654503447053561)
XLA Ops:
  7.2 1.0 copy.70
  8.8 4.5 collective-permute-start
  13.3 1.9 collective-permute-start.1
  16.2 1.9 reshape.53
  18.1 1.1 fusion.18
  19.3 3.2 collective-permute-start.2
  22.5 1.3 collective-permute-start.3
  23.9 3.4 collective-permute-done.3
  27.7 3.2 copy.30
  30.9 72.0 %gather_fusion = f32[9216,8,10]{2,1,0:T(8,128)} fusion(f32[8,10,1280]{1,0,2:T(8,128)} %copy.30, s32[9216]{0:T(1024)S(1)} %broadcast_clamp_fusion), kind=kCustom, calls=%fused_computation | custom fusion | bytes 5935104 | tf_op jit(solution)/shard_map/gather | solution.py:55
  102.9 26.7 %copy.32 = f32[9,1024,8,10]{1,0,3,2:T(8,128)} copy(f32[9,1024,8,10]{3,2,1,0:T(8,128)} %bitcast.89) | data formatting | bytes 5898240 | tf_op jit(solution)/shard_map/gather | solution.py:55
  129.6 7.1 %fusion = f32[8,8,1024,2,4]{2,4,1,0,3:T(4,128)S(1)} fusion(f32[8,10,9,1024]{3,2,1,0:T(8,128)} %bitcast.86, f32[2,4,3,9]{3,1,2,0:T(4,128)S(1)} %copy-done.6), kind=kOutput, calls=%fused_computation.4 | convolution fusion | flops 56623104 | bytes 6295552 | tf_op jit(solution)/shard_map/ksmc,tqm->kstqc/dot_general | solution.py:61
  136.8 4.2 fusion.1
  141.0 5.7 %fusion.5 = f32[8,8,2,4,1024]{4,3,1,0,2:T(4,128)S(1)} fusion(f32[2,4,8,8,1024,1]{4,1,5,3,2,0:T(4,128)S(1)} %fusion.18, f32[8,8,1024,2,4]{2,4,1,0,3:T(4,128)S(1)} %fusion, f32[8,8,1024,2,4]{2,4,1,0,3:T(4,128)S(1)} %fusion.1, f32[8,10,9,1024]{3,2,1,0:T(8,128)S(1)} %bitcast.88, f32[2,4,3,9]{3,1,2,0:T(4,128)S(1)} %copy-done.6), kind=kOutput, calls=%fused_computation.12 | convolution fusion | flops 58195968 | bytes 12587008 | tf_op jit(solution)/shard_map/ksmc,tqm->kstqc/dot_general | solution.py:61
  146.6 1.5 copy.50
  148.2 2.7 reshape.65
  151.1 1.3 copy-done.2
  153.2 88.4 %all-gather.5.cloned.1.call-done = f32[512,1,4096]{2,0,1:T(8,128)} async-done(((f32[8,1,4096]{2,0,1:T(8,128)}), f32[512,1,4096]{2,0,1:T(8,128)}) %all-gather.5.cloned.1.call-update) | async-done | bytes 8388624 | tf_op jit(solution)/shard_map/all_gather | solution.py:29
  241.6 1.0 while.22
  241.7 0.9 bitcast_add_fusion.5
  242.6 3.3 subtract_multiply_fusion
  245.9 3.1 rev.7
  249.0 1.7 fusion.25
  250.8 1.3 copy-done.1
  252.8 1.6 copy.37
  254.3 137.1 %all-gather.7.cloned.1.call-done = f32[512,1,4096]{2,0,1:T(8,128)} async-done(((f32[8,1,4096]{2,0,1:T(8,128)}), f32[512,1,4096]{2,0,1:T(8,128)}) %all-gather.7.cloned.1.call-update) | async-done | bytes 8388624 | tf_op jit(solution)/shard_map/all_gather | solution.py:29
  391.4 59.7 %while.23 = (s32[]{:T(128)}, f32[8,4096]{1,0:T(8,128)S(1)}, s32[]{:T(128)}, f32[64,8,4096]{2,1,0:T(8,128)}, s32[]{:T(128)}, /*index=5*/s32[]{:T(128)}, s32[]{:T(128)}, s32[]{:T(128)}) while((s32[]{:T(128)}, f32[8,4096]{1,0:T(8,128)S(1)}, s32[]{:T(128)}, f32[64,8,4096]{2,1,0:T(8,128)}, s32[]{:T(128)}, /*index=5*/s32[]{:T(128)}, s32[]{:T(128)}, ...), condition=%wide.region_5.6_spmd, body=%wide.region_4.5_spmd.sunk | while | flops 32774 | bytes 393351 | solution.py:36
  391.4 0.9 bitcast_add_fusion.6
  392.4 0.9 bitcast_add_fusion.6
  393.3 0.9 bitcast_add_fusion.6
  394.3 0.9 bitcast_add_fusion.6
  395.3 0.9 bitcast_add_fusion.6
  396.2 0.9 bitcast_add_fusion.6
  397.2 0.9 bitcast_add_fusion.6
  398.1 0.9 bitcast_add_fusion.6
  399.1 0.9 bitcast_add_fusion.6
  400.1 0.9 bitcast_add_fusion.6
  401.0 0.9 bitcast_add_fusion.6
  402.0 0.9 bitcast_add_fusion.6
  403.0 0.9 bitcast_add_fusion.6
  403.9 0.9 bitcast_add_fusion.6
  404.9 0.9 bitcast_add_fusion.6
  405.9 0.9 bitcast_add_fusion.6
  406.8 0.9 bitcast_add_fusion.6
  407.8 0.9 bitcast_add_fusion.6
  408.7 0.9 bitcast_add_fusion.6
  409.7 0.9 bitcast_add_fusion.6
  410.7 0.9 bitcast_add_fusion.6
  411.6 0.9 bitcast_add_fusion.6
  412.6 0.9 bitcast_add_fusion.6
  413.6 0.9 bitcast_add_fusion.6
  414.5 0.9 bitcast_add_fusion.6
  415.5 0.9 bitcast_add_fusion.6
  416.4 0.9 bitcast_add_fusion.6
  417.4 0.9 bitcast_add_fusion.6
  418.4 0.9 bitcast_add_fusion.6
  425.1 0.9 bitcast_add_fusion.6
  429.9 0.9 bitcast_add_fusion.6
  436.7 0.9 bitcast_add_fusion.6
  443.4 0.9 bitcast_add_fusion.6
  448.2 0.9 bitcast_add_fusion.6
  451.1 1.9 add_multiply_fusion
  453.0 3.8 fusion.10
  456.8 2.4 reshape.39
  (64 shorter events, 29.9 us)
Async XLA Ops:
  7.2 10.9 %copy-start.5 = (bf16[2,4,2,4]{3,2,1,0:T(2,128)(2,1)S(1)}, bf16[2,4,2,4]{3,2,1,0:T(2,128)(2,1)}, u32[]{:S(2)}) copy-start(bf16[2,4,2,4]{3,2,1,0:T(2,128)(2,1)} %param.14) | copy-start | bytes 388
  7.2 234.4 %all-gather.5.cloned.1.call-start = ((), (), s32[]{:S(2)}) async-start(), calls=%async_computation | async-start | bytes 8519680 | tf_op jit(solution)/shard_map/all_gather | solution.py:29
  8.8 10.3 %collective-permute-start = (f32[8,1,8,128]{3,2,1,0:T(8,128)}, f32[8,1,8,128]{3,2,1,0:T(8,128)S(1)}, u32[]{:S(2)}, u32[]{:S(2)}) collective-permute-start(f32[8,1,8,128]{3,2,1,0:T(8,128)} %get-tuple-element.110), channel_id=1, source_target_pairs={{0,4},{4,8},{8,12},{12,16},{16,20},{20,24},{24,28},{28,32},{32,36}... | collective-permute-start | bytes 98312 | tf_op jit(solution)/shard_map/ppermute | solution.py:17
  13.3 5.9 %collective-permute-start.1 = (f32[8,1,8,128]{3,2,1,0:T(8,128)S(1)}, f32[8,1,8,128]{3,2,1,0:T(8,128)S(1)}, u32[]{:S(2)}, u32[]{:S(2)}) collective-permute-start(f32[8,1,8,128]{3,2,1,0:T(8,128)S(1)} %get-tuple-element.109), channel_id=1, source_target_pairs={{4,0},{8,4},{12,8},{16,12},{20,16},{24,20},{28,24},{32,28},{36,32}... | collective-permute-start | bytes 98312 | tf_op jit(solution)/shard_map/ppermute | solution.py:20
  18.0 1.1 copy-start.3
  19.3 4.5 collective-permute-start.2
  22.5 4.7 %collective-permute-start.3 = (f32[8,10,1,128]{3,2,1,0:T(1,128)S(1)}, f32[8,10,1,128]{3,2,1,0:T(1,128)S(1)}, u32[]{:S(2)}, u32[]{:S(2)}) collective-permute-start(f32[8,10,1,128]{3,2,1,0:T(1,128)S(1)} %get-tuple-element.108), channel_id=1, source_target_pairs={{1,0},{2,1},{3,2},{5,4},{6,5},{7,6},{9,8},{10,9},{11,10},{13,12},{... | collective-permute-start | bytes 122888 | tf_op jit(solution)/shard_map/ppermute | solution.py:20
  102.9 26.7 %copy-start.6 = (f32[2,4,3,9]{3,1,2,0:T(4,128)S(1)}, f32[2,4,3,9]{3,1,2,0:T(4,128)}, u32[]{:S(2)}) copy-start(f32[2,4,3,9]{3,1,2,0:T(4,128)} %param.13) | copy-start | bytes 2596
  129.6 7.1 %copy-start = (f32[9,1024,8,10]{1,0,3,2:T(8,128)S(1)}, f32[9,1024,8,10]{1,0,3,2:T(8,128)}, u32[]{:S(2)}) copy-start(f32[9,1024,8,10]{1,0,3,2:T(8,128)} %copy.32) | copy-start | bytes 8847364
  150.9 2.3 copy-start.4
  151.1 1.3 copy-start.2
  153.1 238.2 %all-gather.7.cloned.1.call-start = ((), (), s32[]{:S(2)}) async-start(), calls=%async_computation.1 | async-start | bytes 8519680 | tf_op jit(solution)/shard_map/all_gather | solution.py:29
  250.8 1.3 copy-start.1
Sparse Core Ops, SparseCore 0:
  153.2 88.3 all-gather.4
  252.9 138.4 all-gather.6
where the time goes:
time: 468 us; the launch traced here: 466 us
  waiting for transfers between devices  229 us (49%)
  local copies, waits for them, and re-layouts  121 us (26%)
  other arithmetic  67.1 us (14%)
  matrix products  21.9 us (5%)
  between operations  14.3 us (3%)
  starting transfers between devices  11 us (2%)
    all_gather x2, waiting for transfers between devices, entering(): gathered = lax.all_gather(part, axis)  225 us
    gather x2, local copies, waits for them, and re-layouts, shards(): nearby = extended[:, :, halo_index]  98.8 us
    add x63, other arithmetic, add_up(): return earlier + later  58.9 us
    dot_general x3, matrix products, shards(): jnp.einsum('ksmc,tqm->kstqc', nearby[:, offset:offset + coarse_shells], r...  17 us
  transfers between devices with their start and end apart: 6, of which 3 were waited for; matrix products, arithmetic and copies ran while one was open for 1% of the time, Pallas kernels for 0%

commit v1 on v0

--- a/solution.py
+++ b/solution.py
@@ -22,22 +22,25 @@
     return block
 
 
-def entering(part, axis, combine, identity, reverse):
+def block_carries(totals, partial, weight, axis):
     count = lax.axis_size(axis)
-    place = lax.axis_index(axis)
-    ahead = count - 1 - place if reverse else place
-    gathered = lax.all_gather(part, axis)
-    state = jnp.zeros_like(part) + jnp.asarray(identity, part.dtype)
-
-    def one(lap, state):
-        source = count - 1 - lap if reverse else lap
-        return combine(state, lax.dynamic_index_in_dim(gathered, source, 0, False))
-
-    return lax.fori_loop(0, ahead, one, state)
-
-
-def add_up(earlier, later):
-    return earlier + later
+    rows, pixels = totals.shape
+    width = pixels // count
+    packed = jnp.concatenate([totals, partial, weight], axis=0)
+    packed = packed.reshape(packed.shape[0], count, width).transpose(1, 0, 2)
+    mine = lax.all_to_all(packed, axis, 0, 0, tiled=True)
+    block_totals = mine[:, :rows]
+    block_partial = mine[:, rows : 2 * rows]
+    block_weight = mine[:, 2 * rows :]
+    zero = jnp.zeros_like(block_totals[:1])
+    ahead = jnp.cumsum(block_totals, axis=0)
+    carry_in = jnp.concatenate([zero, ahead[:-1]], axis=0)
+    block_misfit = block_partial + block_weight * carry_in
+    behind = jnp.flip(jnp.cumsum(jnp.flip(block_misfit, 0), axis=0), 0)
+    carry_out = jnp.concatenate([behind[1:], zero], axis=0)
+    back = lax.all_to_all(jnp.concatenate([carry_in, carry_out], axis=1), axis, 0, 0, tiled=True)
+    back = back.transpose(1, 0, 2).reshape(2 * rows, pixels)
+    return back[:rows], back[rows:]
 
 
 def shards(
@@ -72,12 +75,12 @@
     local_cum = jnp.cumsum(density, axis=1)
     totals = local_cum[:, -1, :]
     counts = star_counts.astype(jnp.float32)
-    carry_in = entering(totals, "dist", add_up, jnp.zeros_like(totals), False)
+    partial = jnp.sum(counts[None] * (local_cum - star_extinction[None]), axis=1)
+    weight = jnp.sum(counts, axis=0, keepdims=True)
+    carry_in, carry_out = block_carries(totals, partial, weight, "dist")
     cumulative = local_cum + carry_in[:, None, :]
     misfit = counts[None] * (cumulative - star_extinction[None])
     local_back = jnp.flip(jnp.cumsum(jnp.flip(misfit, 1), axis=1), 1)
-    cumulative, local_back = (cumulative, local_back)
-    carry_out = entering(local_back[:, 0, :], "dist", add_up, jnp.zeros_like(totals), True)
     back = local_back + carry_out[:, None, :]
     flowing = (density * back).reshape(samples, coarse_shells, 2, 4, coarse_pixels)
     gradient = jnp.einsum(

time: 468 us -> 228 us (0.49)
  waiting for transfers between devices: 229 us -> 2.36 us
  blocking collectives: 0 us -> 45.9 us
  other arithmetic: 67.1 us -> 21.5 us
  between operations: 14.3 us -> 1.01 us
    all_gather x2 -> x0, waiting for transfers between devices: 225 us -> none  [entering(): gathered = lax.all_gather(part, axis)]
    add x63 -> x0, other arithmetic: 58.9 us -> none  [add_up(): return earlier + later]
    all_to_all x0 -> x2, blocking collectives: none -> 45.9 us  [the longest x1 28.1 us: block_carries(): mine = lax.all_to_all(packed, axis, 0, 0, tiled=True)]
    another operation x0 -> x2, other arithmetic: none -> 6.4 us  [the longest x1 6.33 us: block_carries(): behind = jnp.flip(jnp.cumsum(jnp.flip(block_misfit, 0), axis=0), 0)]
  transfers between devices with their start and end apart: 6 -> 4, of which waited for: 3 -> 1; matrix products, arithmetic and copies ran while one was open for 1% -> 2% of each run, Pallas kernels for 0% -> 0%
where the time goes in v1:
time: 228 us; the launch traced here: 227 us
  local copies, waits for them, and re-layouts  123 us (54%)
  blocking collectives  45.9 us (20%)
  matrix products  21.9 us (10%)
  other arithmetic  21.5 us (9%)
  starting transfers between devices  10.9 us (5%)
  waiting for transfers between devices  2.36 us (1%)
    gather x2, local copies, waits for them, and re-layouts, shards(): nearby = extended[:, :, halo_index]  98.6 us
    all_to_all x1, blocking collectives, block_carries(): mine = lax.all_to_all(packed, axis, 0, 0, tiled=True)  28.1 us
    all_to_all x1, blocking collectives, block_carries(): lax.all_to_all(jnp.concatenate([carry_in, carry_out], axis=1), axis, 0, 0...  17.8 us
    dot_general x3, matrix products, shards(): jnp.einsum('ksmc,tqm->kstqc', nearby[:, offset:offset + coarse_shells], r...  17 us
    ppermute x2, starting transfers between devices, with_halo(): lax.ppermute(lax.slice_in_dim(block, block.shape[dim] - width, None, axis...  7.69 us
    unnamed x26, local copies, waits for them, and re-layouts  6.59 us
    another operation x1, other arithmetic, block_carries(): behind = jnp.flip(jnp.cumsum(jnp.flip(block_misfit, 0), axis=0), 0)  6.33 us
  transfers between devices with their start and end apart: 4, of which 1 were waited for; matrix products, arithmetic and copies ran while one was open for 2% of the time, Pallas kernels for 0%

profile of v1, /device:TPU:1, one launch (start us, length us, event | category | flops | bytes accessed | tf_op | source)
XLA Modules:
  0.0 227.0 jit_solution(4066714732629228845)
XLA Ops:
  0.6 1.0 copy.79
  1.6 0.6 fusion.27
  2.3 4.5 %collective-permute-start = (f32[8,1,8,128]{3,2,1,0:T(8,128)}, f32[8,1,8,128]{3,2,1,0:T(8,128)S(1)}, u32[]{:S(2)}, u32[]{:S(2)}) collective-permute-start(f32[8,1,8,128]{3,2,1,0:T(8,128)} %get-tuple-element.15), channel_id=1, source_target_pairs={{0,4},{4,8},{8,12},{12,16},{16,20},{20,24},{24,28},{28,32},{32,36}... | collective-permute-start | bytes 98312 | tf_op jit(solution)/shard_map/ppermute | solution.py:17
  6.8 1.9 collective-permute-start.1
  8.7 0.9 compare_select_fusion
  9.6 1.9 reshape.62
  11.5 0.0 copy-start.4
  11.5 0.0 copy-start.3
  11.5 1.1 fusion.20
  12.6 0.0 copy-done.4
  12.7 0.0 collective-permute-done
  12.7 0.1 constant_dynamic-update-slice_fusion.1
  12.7 0.0 collective-permute-done.1
  12.8 0.1 fusion.26
  12.8 3.2 %collective-permute-start.2 = (f32[8,10,1,128]{3,2,1,0:T(1,128)S(1)}, f32[8,10,1,128]{3,2,1,0:T(1,128)S(1)}, u32[]{:S(2)}, u32[]{:S(2)}) collective-permute-start(f32[8,10,1,128]{3,2,1,0:T(1,128)S(1)} %get-tuple-element.12), channel_id=1, source_target_pairs={{0,1},{1,2},{2,3},{4,5},{5,6},{6,7},{8,9},{9,10},{10,11},{12,13},{... | collective-permute-start | bytes 122888 | tf_op jit(solution)/shard_map/ppermute | solution.py:17
  16.0 1.3 collective-permute-start.3
  17.3 1.0 convert_element_type.15
  18.3 0.1 concatenate.29
  18.4 0.0 collective-permute-done.2
  18.4 2.4 %collective-permute-done.3 = f32[8,10,1,128]{3,2,1,0:T(1,128)S(1)} collective-permute-done((f32[8,10,1,128]{3,2,1,0:T(1,128)S(1)}, f32[8,10,1,128]{3,2,1,0:T(1,128)S(1)}, u32[]{:S(2)}, u32[]{:S(2)}) %collective-permute-start.3) | collective-permute-done | bytes 40992 | tf_op jit(solution)/shard_map/ppermute | solution.py:20
  20.8 0.1 pad_maximum_fusion
  20.9 0.2 copy.78
  21.2 3.2 %copy.35 = f32[8,10,1280]{1,0,2:T(8,128)} copy(f32[8,10,1280]{2,0,1:T(8,128)S(1)} %bitcast.89) | data formatting | bytes 819200 | tf_op jit(solution)/shard_map/reshape | solution.py:57
  24.3 71.9 %gather_fusion = f32[9216,8,10]{2,1,0:T(8,128)} fusion(f32[8,10,1280]{1,0,2:T(8,128)} %copy.35, s32[9216]{0:T(1024)S(1)} %broadcast_clamp_fusion), kind=kCustom, calls=%fused_computation | custom fusion | bytes 5935104 | tf_op jit(solution)/shard_map/gather | solution.py:58
  96.2 26.7 %copy.37 = f32[9,1024,8,10]{1,0,3,2:T(8,128)} copy(f32[9,1024,8,10]{3,2,1,0:T(8,128)} %bitcast.86) | data formatting | bytes 5898240 | tf_op jit(solution)/shard_map/gather | solution.py:58
  122.9 0.0 copy-done.8
  122.9 7.1 %fusion = f32[8,8,1024,2,4]{2,4,1,0,3:T(4,128)S(1)} fusion(f32[8,10,9,1024]{3,2,1,0:T(8,128)} %bitcast.83, f32[2,4,3,9]{3,1,2,0:T(4,128)S(1)} %copy-done.8), kind=kOutput, calls=%fused_computation.2 | convolution fusion | flops 56623104 | bytes 6295552 | tf_op jit(solution)/shard_map/ksmc,tqm->kstqc/dot_general | solution.py:64
  130.1 0.0 copy-done
  130.1 4.2 %fusion.1 = f32[8,8,1024,2,4]{2,4,1,0,3:T(4,128)S(1)} fusion(f32[8,10,9,1024]{3,2,1,0:T(8,128)S(1)} %bitcast.84, f32[2,4,3,9]{3,1,2,0:T(4,128)S(1)} %copy-done.8), kind=kOutput, calls=%fused_computation.4 | convolution fusion | flops 56623104 | bytes 6295552 | tf_op jit(solution)/shard_map/ksmc,tqm->kstqc/dot_general | solution.py:64
  134.3 5.7 %fusion.5 = f32[8,8,2,4,1024]{4,3,1,0,2:T(4,128)S(1)} fusion(f32[2,4,8,8,1024,1]{4,1,5,3,2,0:T(4,128)S(1)} %fusion.20, f32[8,8,1024,2,4]{2,4,1,0,3:T(4,128)S(1)} %fusion, f32[8,8,1024,2,4]{2,4,1,0,3:T(4,128)S(1)} %fusion.1, f32[8,10,9,1024]{3,2,1,0:T(8,128)S(1)} %bitcast.85, f32[2,4,3,9]{3,1,2,0:T(4,128)S(1)} %copy-done.8), kind=kOutput, calls=%fused_computation.10 | convolution fusion | flops 58195968 | bytes 12587008 | tf_op jit(solution)/shard_map/ksmc,tqm->kstqc/dot_general | solution.py:64
  139.9 1.5 copy.59
  141.5 2.7 %reshape.74 = f32[8,16,4096]{2,0,1:T(8,128)S(1)} reshape(f32[8,8,2,4,1024]{4,3,0,2,1:T(4,128)} %copy.59) | data formatting | bytes 4194304 | tf_op jit(solution)/shard_map/exp | solution.py:74
  144.2 0.4 multiply_reduce_fusion
  144.7 0.0 copy-start.1
  144.7 1.3 copy-done.1
  146.0 0.1 concatenate.27
  146.1 0.2 copy.40
  146.3 0.1 concatenate.28
  146.4 0.2 copy.41
  146.5 0.1 maximum_bitcast_fusion
  146.6 1.1 reshape.75
  147.7 28.1 %all_to_all.10 = f32[64,1,1088]{2,1,0:T(1,128)S(1)} all-to-all(f32[64,1,1088]{2,1,0:T(1,128)} %reshape.75), channel_id=1, replica_groups=mesh['dist'=64,'sky'=4] {'dist'}, dimensions={0} | all-to-all | bytes 557056 | tf_op jit(solution)/shard_map/all_to_all | solution.py:31
  175.8 0.6 broadcast.51
  176.4 2.1 reduce
  178.6 1.1 reshape.76
  179.7 0.1 fusion.14
  179.8 0.8 fusion.28
  180.6 6.3 %fusion.29 = f32[64,8,64]{2,1,0:T(8,128)S(1)} fusion(f32[64,8,64]{2,1,0:T(8,128)S(1)} %rev.12), kind=kOutput, calls=%fused_computation.50 | output fusion | flops 2064384 | bytes 262144 | tf_op jit(solution)/shard_map/jit(cumsum)/reduce_window_sum | solution.py:39
  187.0 0.3 reshape.77
  187.3 17.8 %all_to_all.11 = f32[64,1,1024]{2,1,0:T(1,128)S(1)} all-to-all(f32[64,1,1024]{2,1,0:T(1,128)S(1)} %reshape.77), channel_id=1, replica_groups=mesh['dist'=64,'sky'=4] {'dist'}, dimensions={0} | all-to-all | bytes 524288 | tf_op jit(solution)/shard_map/all_to_all | solution.py:41
  205.1 1.3 reduce.1
  206.4 0.1 reshape.78
  206.6 0.7 fusion.25
  207.3 0.1 copy.42
  207.4 0.1 add.73
  207.5 3.3 %subtract_multiply_fusion = (f32[8,16,4096]{2,0,1:T(8,128)}, bf16[8,16,4096]{2,0,1:T(8,128)(2,1)S(1)}) fusion(f32[8,16,4096]{2,0,1:T(8,128)} %copy-done.1, f32[8,4096]{1,0:T(8,128)S(1)} %add.73, f32[16,4096]{1,0:T(8,128)} %param.12, f32[16,4096]{1,0:T(8,128)S(1)} %convert_element_type.15), kind=kLoop, calls=%fused_computation.14 | loop fusion | flops 2097152 | bytes 5898240 | tf_op jit(solution)/shard_map/mul | solution.py:82
  210.8 3.1 %rev.13 = f32[8,16,4096]{2,0,1:T(8,128)} reverse(f32[8,16,4096]{2,0,1:T(8,128)} %get-tuple-element.8), dimensions={1} | reverse | bytes 4194304 | tf_op jit(solution)/shard_map/jit(_flip)/rev | solution.py:83
  214.0 3.1 %fusion.30 = f32[8,16,4096]{2,0,1:T(8,128)} fusion(f32[8,16,4096]{2,0,1:T(8,128)} %rev.13), kind=kOutput, calls=%fused_computation.51 | output fusion | flops 7864320 | bytes 4194304 | tf_op jit(solution)/shard_map/jit(cumsum)/reduce_window_sum | solution.py:83
  217.0 0.1 copy.43
  217.1 0.1 add.76
  217.2 1.9 add_multiply_fusion
  219.2 3.8 %fusion.10 = f32[8,8,2,4,1024]{4,3,2,1,0:T(4,128)S(1)} fusion(f32[8,8,2,4,1024,1]{4,0,3,2,1,5:T(8,128)S(1)} %bitcast.87, bf16[2,4,2,4,1,1]{3,2,1,0,5,4:T(2,128)(2,1)S(1)} %bitcast.94), kind=kOutput, calls=%fused_computation.19 | convolution fusion | flops 50331648 | bytes 4194432 | tf_op jit(solution)/shard_map/kstqc,tqab->ksabc/dot_general | solution.py:86
  223.0 2.4 %reshape.50 = f32[8,16,4096]{2,1,0:T(8,128)} reshape(f32[8,8,2,4,1024]{4,3,2,1,0:T(4,128)S(1)} %fusion.10) | data formatting | bytes 4194304 | tf_op jit(solution)/shard_map/reshape | solution.py:89
  225.4 1.6 copy.46
  (24 shorter events, 0.3 us)
Async XLA Ops:
  0.6 10.8 %copy-start.7 = (bf16[2,4,2,4]{3,2,1,0:T(2,128)(2,1)S(1)}, bf16[2,4,2,4]{3,2,1,0:T(2,128)(2,1)}, u32[]{:S(2)}) copy-start(bf16[2,4,2,4]{3,2,1,0:T(2,128)(2,1)} %param.10) | copy-start | bytes 388
  2.3 10.4 %collective-permute-start = (f32[8,1,8,128]{3,2,1,0:T(8,128)}, f32[8,1,8,128]{3,2,1,0:T(8,128)S(1)}, u32[]{:S(2)}, u32[]{:S(2)}) collective-permute-start(f32[8,1,8,128]{3,2,1,0:T(8,128)} %get-tuple-element.15), channel_id=1, source_target_pairs={{0,4},{4,8},{8,12},{12,16},{16,20},{20,24},{24,28},{28,32},{32,36}... | collective-permute-start | bytes 98312 | tf_op jit(solution)/shard_map/ppermute | solution.py:17
  6.8 6.0 %collective-permute-start.1 = (f32[8,1,8,128]{3,2,1,0:T(8,128)S(1)}, f32[8,1,8,128]{3,2,1,0:T(8,128)S(1)}, u32[]{:S(2)}, u32[]{:S(2)}) collective-permute-start(f32[8,1,8,128]{3,2,1,0:T(8,128)S(1)} %get-tuple-element.14), channel_id=1, source_target_pairs={{4,0},{8,4},{12,8},{16,12},{20,16},{24,20},{28,24},{32,28},{36,32}... | collective-permute-start | bytes 98312 | tf_op jit(solution)/shard_map/ppermute | solution.py:20
  11.5 1.1 copy-start.4
  11.5 1.2 copy-start.3
  12.8 5.6 %collective-permute-start.2 = (f32[8,10,1,128]{3,2,1,0:T(1,128)S(1)}, f32[8,10,1,128]{3,2,1,0:T(1,128)S(1)}, u32[]{:S(2)}, u32[]{:S(2)}) collective-permute-start(f32[8,10,1,128]{3,2,1,0:T(1,128)S(1)} %get-tuple-element.12), channel_id=1, source_target_pairs={{0,1},{1,2},{2,3},{4,5},{5,6},{6,7},{8,9},{9,10},{10,11},{12,13},{... | collective-permute-start | bytes 122888 | tf_op jit(solution)/shard_map/ppermute | solution.py:17
  16.0 4.7 %collective-permute-start.3 = (f32[8,10,1,128]{3,2,1,0:T(1,128)S(1)}, f32[8,10,1,128]{3,2,1,0:T(1,128)S(1)}, u32[]{:S(2)}, u32[]{:S(2)}) collective-permute-start(f32[8,10,1,128]{3,2,1,0:T(1,128)S(1)} %get-tuple-element.13), channel_id=1, source_target_pairs={{1,0},{2,1},{3,2},{5,4},{6,5},{7,6},{9,8},{10,9},{11,10},{13,12},{... | collective-permute-start | bytes 122888 | tf_op jit(solution)/shard_map/ppermute | solution.py:20
  96.2 26.7 %copy-start.8 = (f32[2,4,3,9]{3,1,2,0:T(4,128)S(1)}, f32[2,4,3,9]{3,1,2,0:T(4,128)}, u32[]{:S(2)}) copy-start(f32[2,4,3,9]{3,1,2,0:T(4,128)} %param.9) | copy-start | bytes 2596
  122.9 7.1 %copy-start = (f32[9,1024,8,10]{1,0,3,2:T(8,128)S(1)}, f32[9,1024,8,10]{1,0,3,2:T(8,128)}, u32[]{:S(2)}) copy-start(f32[9,1024,8,10]{1,0,3,2:T(8,128)} %copy.37) | copy-start | bytes 8847364
  141.5 2.7 %copy-start.2 = (f32[16,4096]{1,0:T(8,128)S(1)}, f32[16,4096]{1,0:T(8,128)}, u32[]{:S(2)}) copy-start(f32[16,4096]{1,0:T(8,128)} %param.12) | copy-start | bytes 786436
  144.7 1.3 copy-start.1
  180.5 6.4 %copy-start.6 = (f32[64,8,64]{2,1,0:T(8,128)S(1)}, f32[64,8,64]{2,1,0:T(8,128)}, u32[]{:S(2)}) copy-start(f32[64,8,64]{2,1,0:T(8,128)} %get-tuple-element.16) | copy-start | bytes 393220
  214.0 3.1 %copy-start.5 = (f32[8,64,64]{2,0,1:T(8,128)S(1)}, f32[8,64,64]{2,0,1:T(8,128)}, u32[]{:S(2)}) copy-start(f32[8,64,64]{2,0,1:T(8,128)} %get-tuple-element.10) | copy-start | bytes 393220

commit v2 on v1

--- a/solution.py
+++ b/solution.py
@@ -43,6 +43,34 @@
     return back[:rows], back[rows:]
 
 
+def split_three(values):
+    high = lax.reduce_precision(values, exponent_bits=8, mantissa_bits=7)
+    rest = values - high
+    middle = lax.reduce_precision(rest, exponent_bits=8, mantissa_bits=7)
+    low = rest - middle
+    return jnp.stack([high, middle, low]).astype(jnp.bfloat16)
+
+
+def gather_nearby(extended, halo_index):
+    samples, shells, _ = extended.shape
+    slots, pixels = halo_index.shape
+    blocks = pixels // BAND
+    window = 3 * BAND
+    windows = jnp.stack(
+        [extended[:, :, b * BAND : b * BAND + window] for b in range(blocks)]
+    ).reshape(blocks, samples * shells, window)
+    pieces = split_three(windows).transpose(1, 0, 2, 3).reshape(blocks, 3 * samples * shells, window)
+    starts = (jnp.arange(blocks, dtype=jnp.int32) * BAND)[None, :, None]
+    local = halo_index.reshape(slots, blocks, BAND) - starts
+    spots = jnp.arange(window, dtype=jnp.int32)[None, :, None, None]
+    onehot = (local.transpose(1, 0, 2)[:, None] == spots).astype(jnp.bfloat16)
+    onehot = onehot.reshape(blocks, window, slots * BAND)
+    picked = jnp.einsum("bxw,bwn->bxn", pieces, onehot, preferred_element_type=jnp.float32)
+    picked = picked.reshape(blocks, 3, samples, shells, slots, BAND)
+    picked = (picked[:, 0] + picked[:, 1]) + picked[:, 2]
+    return picked.transpose(1, 2, 3, 0, 4).reshape(samples, shells, slots, pixels)
+
+
 def shards(
     coarse_field, excitations, refine_weights, refine_sqrt, halo_index, star_extinction, star_counts
 ):
@@ -55,7 +83,7 @@
     blocked = coarse_field.reshape(samples, coarse_shells, coarse_pixels // BAND, BAND)
     extended = with_halo(blocked, (("dist", 1), ("sky", 2)), 1)
     extended = extended.reshape(samples, coarse_shells + 2, coarse_pixels + 2 * BAND)
-    nearby = extended[:, :, halo_index]
+    nearby = gather_nearby(extended, halo_index)
     local_part = excitations.reshape(samples, coarse_shells, 2, 4, coarse_pixels)
     refined = jnp.einsum(
         "ksabc,tqab->kstqc", local_part, refine_sqrt, preferred_element_type=jnp.float32

time: 228 us -> 158 us (0.69)
  local copies, waits for them, and re-layouts: 123 us -> 38.8 us
  matrix products: 21.9 us -> 28.7 us
  other arithmetic: 21.5 us -> 27.7 us
    gather x2 -> x0, local copies, waits for them, and re-layouts: 98.6 us -> none  [shards(): nearby = extended[:, :, halo_index]]
    reshape x1 -> x3, local copies, waits for them, and re-layouts: 3.2 us -> 16.3 us  [the longest x1 12.1 us: gather_nearby(): picked = picked.reshape(blocks, 3, samples, shells, slots, BAND)]
    transpose x0 -> x2, other arithmetic: none -> 7.76 us  [the longest x1 7.57 us: gather_nearby(): picked.transpose(1, 2, 3, 0, 4).reshape(samples, shells, slots, pixels)]
    dot_general x0 -> x1, matrix products: none -> 5.26 us  [gather_nearby(): jnp.einsum('bxw,bwn->bxn', pieces, onehot, preferred_element_type=jnp.flo...]
    unnamed x26 -> x36, local copies, waits for them, and re-layouts: 6.59 us -> 7.54 us
  transfers between devices with their start and end apart: 4 -> 4, of which waited for: 1 -> 1; matrix products, arithmetic and copies ran while one was open for 2% -> 3% of each run, Pallas kernels for 0% -> 0%
where the time goes in v2:
time: 158 us; the launch traced here: 157 us
  blocking collectives  45.9 us (29%)
  local copies, waits for them, and re-layouts  38.8 us (25%)
  matrix products  28.7 us (18%)
  other arithmetic  27.7 us (18%)
  starting transfers between devices  10.9 us (7%)
  waiting for transfers between devices  3.31 us (2%)
    all_to_all x1, blocking collectives, block_carries(): mine = lax.all_to_all(packed, axis, 0, 0, tiled=True)  28.1 us
    all_to_all x1, blocking collectives, block_carries(): lax.all_to_all(jnp.concatenate([carry_in, carry_out], axis=1), axis, 0, 0...  17.8 us
    dot_general x3, matrix products, shards(): jnp.einsum('ksmc,tqm->kstqc', nearby[:, offset:offset + coarse_shells], r...  17.2 us
    reshape x1, local copies, waits for them, and re-layouts, gather_nearby(): picked = picked.reshape(blocks, 3, samples, shells, slots, BAND)  12.1 us
    ppermute x2, starting transfers between devices, with_halo(): lax.ppermute(lax.slice_in_dim(block, block.shape[dim] - width, None, axis...  7.7 us
    transpose x1, other arithmetic, gather_nearby(): picked.transpose(1, 2, 3, 0, 4).reshape(samples, shells, slots, pixels)  7.57 us
    unnamed x36, local copies, waits for them, and re-layouts  7.54 us
    another operation x1, other arithmetic, block_carries(): behind = jnp.flip(jnp.cumsum(jnp.flip(block_misfit, 0), axis=0), 0)  6.33 us
  transfers between devices with their start and end apart: 4, of which 1 were waited for; matrix products, arithmetic and copies ran while one was open for 3% of the time, Pallas kernels for 0%

profile of v2, /device:TPU:1, one launch (start us, length us, event | category | flops | bytes accessed | tf_op | source)
XLA Modules:
  0.0 156.7 jit_solution(9838753612991546989)
XLA Ops:
  0.6 1.0 copy.101
  1.7 4.5 %collective-permute-start = (f32[8,1,8,128]{3,2,1,0:T(8,128)S(1)}, f32[8,1,8,128]{3,2,1,0:T(8,128)S(1)}, u32[]{:S(2)}, u32[]{:S(2)}) collective-permute-start(f32[8,1,8,128]{3,2,1,0:T(8,128)S(1)} %get-tuple-element.26), channel_id=1, source_target_pairs={{0,4},{4,8},{8,12},{12,16},{16,20},{20,24},{24,28},{28,32},{32,36}... | collective-permute-start | bytes 98312 | tf_op jit(solution)/shard_map/ppermute | solution.py:17
  6.2 1.9 %collective-permute-start.1 = (f32[8,1,8,128]{3,2,1,0:T(8,128)S(1)}, f32[8,1,8,128]{3,2,1,0:T(8,128)S(1)}, u32[]{:S(2)}, u32[]{:S(2)}) collective-permute-start(f32[8,1,8,128]{3,2,1,0:T(8,128)S(1)} %get-tuple-element.25), channel_id=1, source_target_pairs={{4,0},{8,4},{12,8},{16,12},{20,16},{24,20},{28,24},{32,28},{36,32}... | collective-permute-start | bytes 98312 | tf_op jit(solution)/shard_map/ppermute | solution.py:20
  8.1 0.9 copy.87
  9.0 1.9 %reshape.491 = bf16[8,8,2,4,1024,1]{4,3,2,1,0,5:T(4,128)(2,1)S(1)} reshape(bf16[8,16,4096]{2,1,0:T(8,128)(2,1)} %param.8) | data formatting | bytes 2097152 | tf_op jit(solution)/shard_map/reshape | solution.py:87
  10.8 0.0 copy-start.5
  10.9 0.0 copy-start.4
  10.9 0.1 fusion.20
  10.9 2.4 %fusion.25 = f32[2,4,8,8,1024,1]{4,1,5,3,2,0:T(4,128)} fusion(bf16[8,8,2,4,1024,1]{4,3,2,1,0,5:T(4,128)(2,1)S(1)} %reshape.491, bf16[2,4,2,4,1,1]{3,2,1,0,5,4:T(2,128)(2,1)S(1)} %bitcast.107), kind=kOutput, calls=%fused_computation.58 | convolution fusion | flops 8388608 | bytes 3145856 | tf_op jit(solution)/shard_map/ksabc,tqab->kstqc/dot_general | solution.py:88
  13.5 0.1 constant_dynamic-update-slice_fusion.1
  13.5 0.1 fusion.32
  13.6 3.2 %collective-permute-start.2 = (f32[8,10,1,128]{3,2,1,0:T(1,128)S(1)}, f32[8,10,1,128]{3,2,1,0:T(1,128)S(1)}, u32[]{:S(2)}, u32[]{:S(2)}) collective-permute-start(f32[8,10,1,128]{3,2,1,0:T(1,128)S(1)} %get-tuple-element.23), channel_id=1, source_target_pairs={{0,1},{1,2},{2,3},{4,5},{5,6},{6,7},{8,9},{9,10},{10,11},{12,13},{... | collective-permute-start | bytes 122888 | tf_op jit(solution)/shard_map/ppermute | solution.py:17
  16.8 1.3 collective-permute-start.3
  18.1 0.1 concatenate.54
  18.2 3.3 %collective-permute-done.3 = f32[8,10,1,128]{3,2,1,0:T(1,128)S(1)} collective-permute-done((f32[8,10,1,128]{3,2,1,0:T(1,128)S(1)}, f32[8,10,1,128]{3,2,1,0:T(1,128)S(1)}, u32[]{:S(2)}, u32[]{:S(2)}) %collective-permute-start.3) | collective-permute-done | bytes 40992 | tf_op jit(solution)/shard_map/ppermute | solution.py:20
  21.5 0.1 pad_maximum_fusion
  21.7 0.2 copy.100
  21.9 0.1 fusion.31
  22.7 0.2 reduce-precision_convert_fusion.1
  22.9 0.2 maximum_bitcast_fusion
  23.1 0.1 copy.54
  23.3 5.3 %fusion = f32[8,240,1152]{2,1,0:T(8,128)} fusion(bf16[8,240,384]{2,1,0:T(8,128)(2,1)S(1)} %bitcast.99, s32[8,1152]{1,0:T(8,128)S(1)} %fusion.20), kind=kOutput, calls=%fused_computation.1 | convolution fusion | flops 1702232064 | bytes 10358784 | tf_op jit(solution)/shard_map/bxw,bwn->bxn/dot_general | solution.py:68
  28.6 12.1 %reshape.486 = f32[8,3,8,10,9,128]{5,4,3,2,1,0:T(8,128)} reshape(f32[8,240,1152]{2,1,0:T(8,128)} %fusion) | data formatting | bytes 17694720 | tf_op jit(solution)/shard_map/reshape | solution.py:69
  40.6 7.6 %fusion.2 = f32[8,10,9,8,128]{4,2,1,0,3:T(8,128)S(1)} fusion(f32[8,3,8,10,9,128]{5,4,3,2,1,0:T(8,128)} %reshape.486), kind=kLoop, calls=%fused_computation.4 | loop fusion | flops 1474560 | bytes 11796480 | tf_op jit(solution)/shard_map/transpose | solution.py:71
  48.2 1.7 %copy.83 = f32[8,10,9,8,128]{4,3,2,1,0:T(8,128)S(1)} copy(f32[8,10,9,8,128]{4,2,1,0,3:T(8,128)S(1)} %fusion.2) | data formatting | bytes 5898240 | tf_op jit(solution)/shard_map/reshape | solution.py:71
  49.9 0.0 copy-start.9
  49.9 2.6 %reshape.504 = f32[8,10,9,1024]{3,2,1,0:T(8,128)} reshape(f32[8,10,9,8,128]{4,3,2,1,0:T(8,128)S(1)} %copy.83) | data formatting | bytes 5898240 | tf_op jit(solution)/shard_map/reshape | solution.py:71
  52.4 7.1 %fusion.3 = f32[8,8,1024,2,4]{2,4,1,0,3:T(4,128)S(1)} fusion(f32[8,10,9,1024]{3,2,1,0:T(8,128)} %reshape.504, f32[2,4,3,9]{3,1,2,0:T(4,128)S(1)} %copy-done.9), kind=kOutput, calls=%fused_computation.7 | convolution fusion | flops 56623104 | bytes 6295552 | tf_op jit(solution)/shard_map/ksmc,tqm->kstqc/dot_general | solution.py:92
  59.6 0.0 copy-start.2
  59.6 4.4 %fusion.4 = f32[8,8,1024,2,4]{2,4,1,0,3:T(4,128)S(1)} fusion(f32[8,10,9,1024]{3,2,1,0:T(8,128)S(1)} %copy-done, f32[2,4,3,9]{3,1,2,0:T(4,128)S(1)} %copy-done.9), kind=kOutput, calls=%fused_computation.9 | convolution fusion | flops 56623104 | bytes 6295552 | tf_op jit(solution)/shard_map/ksmc,tqm->kstqc/dot_general | solution.py:92
  64.0 5.7 %fusion.8 = f32[8,8,2,4,1024]{4,3,1,0,2:T(4,128)S(1)} fusion(f32[2,4,8,8,1024,1]{4,1,5,3,2,0:T(4,128)S(1)} %copy-done.2, f32[8,8,1024,2,4]{2,4,1,0,3:T(4,128)S(1)} %fusion.3, f32[8,8,1024,2,4]{2,4,1,0,3:T(4,128)S(1)} %fusion.4, f32[8,10,9,1024]{3,2,1,0:T(8,128)S(1)} %copy-done, f32[2,4,3,9]{3,1,2,0:T(4,128)S(1)} %copy-done.9), kind=kOutput, calls=%fused_computation.15 | convolution fusion | flops 58195968 | bytes 12587008 | tf_op jit(solution)/shard_map/ksmc,tqm->kstqc/dot_general | solution.py:92
  69.7 1.5 copy.78
  71.2 2.7 %reshape.503 = f32[8,16,4096]{2,0,1:T(8,128)S(1)} reshape(f32[8,8,2,4,1024]{4,3,0,2,1:T(4,128)} %copy.78) | data formatting | bytes 4194304 | tf_op jit(solution)/shard_map/exp | solution.py:102
  74.0 0.4 multiply_reduce_fusion
  74.4 1.3 copy-done.1
  75.7 0.1 concatenate.52
  75.9 0.2 copy.61
  76.0 0.1 concatenate.53
  76.1 0.2 copy.62
  76.3 0.1 maximum_bitcast_fusion.1
  76.4 1.1 reshape.505
  77.4 28.1 %all_to_all.10 = f32[64,1,1088]{2,1,0:T(1,128)S(1)} all-to-all(f32[64,1,1088]{2,1,0:T(1,128)} %reshape.505), channel_id=1, replica_groups=mesh['dist'=64,'sky'=4] {'dist'}, dimensions={0} | all-to-all | bytes 557056 | tf_op jit(solution)/shard_map/all_to_all | solution.py:31
  105.6 0.6 broadcast.58
  106.2 2.1 %reduce = f32[64,1088]{1,0:T(8,128)} reduce(f32[64,1,1088]{2,1,0:T(1,128)S(1)} %all_to_all.10, f32[]{:T(128)} %broadcast.58), dimensions={1}, to_apply=%all_to_all.6.reduce_sub_computation | reduce | bytes 557060 | tf_op jit(solution)/shard_map/all_to_all | solution.py:31
  108.3 1.1 reshape.506
  109.4 0.1 fusion.18
  109.5 0.8 fusion.34
  110.3 6.3 %fusion.35 = f32[64,8,64]{2,1,0:T(8,128)S(1)} fusion(f32[64,8,64]{2,1,0:T(8,128)S(1)} %rev.12), kind=kOutput, calls=%fused_computation.71 | output fusion | flops 2064384 | bytes 262144 | tf_op jit(solution)/shard_map/jit(cumsum)/reduce_window_sum | solution.py:39
  116.8 0.3 reshape.507
  117.1 17.8 %all_to_all.11 = f32[64,1,1024]{2,1,0:T(1,128)S(1)} all-to-all(f32[64,1,1024]{2,1,0:T(1,128)S(1)} %reshape.507), channel_id=1, replica_groups=mesh['dist'=64,'sky'=4] {'dist'}, dimensions={0} | all-to-all | bytes 524288 | tf_op jit(solution)/shard_map/all_to_all | solution.py:41
  134.9 1.3 reduce.1
  136.2 0.1 reshape.508
  136.3 0.7 fusion.30
  137.1 0.1 copy.63
  137.1 0.1 add.78
  137.3 3.3 %subtract_multiply_fusion = (f32[8,16,4096]{2,0,1:T(8,128)}, bf16[8,16,4096]{2,0,1:T(8,128)(2,1)S(1)}) fusion(f32[8,16,4096]{2,0,1:T(8,128)} %copy-done.1, f32[8,4096]{1,0:T(8,128)S(1)} %add.78, f32[16,4096]{1,0:T(8,128)} %param.12, f32[16,4096]{1,0:T(8,128)S(1)} %convert_element_type.17), kind=kLoop, calls=%fused_computation.19 | loop fusion | flops 2097152 | bytes 5898240 | tf_op jit(solution)/shard_map/mul | solution.py:110
  140.6 3.1 %rev.13 = f32[8,16,4096]{2,0,1:T(8,128)} reverse(f32[8,16,4096]{2,0,1:T(8,128)} %get-tuple-element.8), dimensions={1} | reverse | bytes 4194304 | tf_op jit(solution)/shard_map/jit(_flip)/rev | solution.py:111
  143.7 3.1 %fusion.36 = f32[8,16,4096]{2,0,1:T(8,128)} fusion(f32[8,16,4096]{2,0,1:T(8,128)} %rev.13), kind=kOutput, calls=%fused_computation.72 | output fusion | flops 7864320 | bytes 4194304 | tf_op jit(solution)/shard_map/jit(cumsum)/reduce_window_sum | solution.py:111
  146.8 0.1 copy.64
  146.9 0.1 add.81
  147.0 1.9 %add_multiply_fusion = f32[8,16,4096]{2,0,1:T(8,128)S(1)} fusion(f32[8,16,4096]{2,0,1:T(8,128)} %fusion.36, f32[8,16,4096]{2,0,1:T(8,128)S(1)} %reshape.503, f32[8,4096]{1,0:T(8,128)S(1)} %add.81, f32[16]{0:T(128)S(1)} %exponential_multiply_fusion), kind=kLoop, calls=%fused_computation.18 | loop fusion | flops 1572864 | bytes 6422592 | tf_op jit(solution)/shard_map/mul | solution.py:113
  148.9 3.8 %fusion.13 = f32[8,8,2,4,1024]{4,3,2,1,0:T(4,128)S(1)} fusion(f32[8,8,2,4,1024,1]{4,0,3,2,1,5:T(8,128)S(1)} %bitcast.98, bf16[2,4,2,4,1,1]{3,2,1,0,5,4:T(2,128)(2,1)S(1)} %bitcast.108), kind=kOutput, calls=%fused_computation.24 | convolution fusion | flops 50331648 | bytes 4194432 | tf_op jit(solution)/shard_map/kstqc,tqab->ksabc/dot_general | solution.py:114
  152.7 2.4 %reshape.489 = f32[8,16,4096]{2,1,0:T(8,128)} reshape(f32[8,8,2,4,1024]{4,3,2,1,0:T(4,128)S(1)} %fusion.13) | data formatting | bytes 4194304 | tf_op jit(solution)/shard_map/reshape | solution.py:117
  155.2 1.6 copy.67
  (56 shorter events, 0.8 us)
Async XLA Ops:
  0.6 10.3 %copy-start.8 = (bf16[2,4,2,4]{3,2,1,0:T(2,128)(2,1)S(1)}, bf16[2,4,2,4]{3,2,1,0:T(2,128)(2,1)}, u32[]{:S(2)}) copy-start(bf16[2,4,2,4]{3,2,1,0:T(2,128)(2,1)} %param.10) | copy-start | bytes 388
  1.7 11.8 %collective-permute-start = (f32[8,1,8,128]{3,2,1,0:T(8,128)S(1)}, f32[8,1,8,128]{3,2,1,0:T(8,128)S(1)}, u32[]{:S(2)}, u32[]{:S(2)}) collective-permute-start(f32[8,1,8,128]{3,2,1,0:T(8,128)S(1)} %get-tuple-element.26), channel_id=1, source_target_pairs={{0,4},{4,8},{8,12},{12,16},{16,20},{20,24},{24,28},{28,32},{32,36}... | collective-permute-start | bytes 98312 | tf_op jit(solution)/shard_map/ppermute | solution.py:17
  6.2 7.3 %collective-permute-start.1 = (f32[8,1,8,128]{3,2,1,0:T(8,128)S(1)}, f32[8,1,8,128]{3,2,1,0:T(8,128)S(1)}, u32[]{:S(2)}, u32[]{:S(2)}) collective-permute-start(f32[8,1,8,128]{3,2,1,0:T(8,128)S(1)} %get-tuple-element.25), channel_id=1, source_target_pairs={{4,0},{8,4},{12,8},{16,12},{20,16},{24,20},{28,24},{32,28},{36,32}... | collective-permute-start | bytes 98312 | tf_op jit(solution)/shard_map/ppermute | solution.py:20
  10.8 2.5 %copy-start.5 = (s32[16,4096]{1,0:T(8,128)S(1)}, s32[16,4096]{1,0:T(8,128)}, u32[]{:S(2)}) copy-start(s32[16,4096]{1,0:T(8,128)} %param.13) | copy-start | bytes 786436
  10.9 2.6 %copy-start.4 = (f32[8,8,1024]{2,1,0:T(8,128)S(1)}, f32[8,8,1024]{2,1,0:T(8,128)}, u32[]{:S(2)}) copy-start(f32[8,8,1024]{2,1,0:T(8,128)} %param.7) | copy-start | bytes 786436
  13.6 4.6 %collective-permute-start.2 = (f32[8,10,1,128]{3,2,1,0:T(1,128)S(1)}, f32[8,10,1,128]{3,2,1,0:T(1,128)S(1)}, u32[]{:S(2)}, u32[]{:S(2)}) collective-permute-start(f32[8,10,1,128]{3,2,1,0:T(1,128)S(1)} %get-tuple-element.23), channel_id=1, source_target_pairs={{0,1},{1,2},{2,3},{4,5},{5,6},{6,7},{8,9},{9,10},{10,11},{12,13},{... | collective-permute-start | bytes 122888 | tf_op jit(solution)/shard_map/ppermute | solution.py:17
  16.8 4.7 %collective-permute-start.3 = (f32[8,10,1,128]{3,2,1,0:T(1,128)S(1)}, f32[8,10,1,128]{3,2,1,0:T(1,128)S(1)}, u32[]{:S(2)}, u32[]{:S(2)}) collective-permute-start(f32[8,10,1,128]{3,2,1,0:T(1,128)S(1)} %get-tuple-element.24), channel_id=1, source_target_pairs={{1,0},{2,1},{3,2},{5,4},{6,5},{7,6},{9,8},{10,9},{11,10},{13,12},{... | collective-permute-start | bytes 122888 | tf_op jit(solution)/shard_map/ppermute | solution.py:20
  49.9 2.6 %copy-start.9 = (f32[2,4,3,9]{3,1,2,0:T(4,128)S(1)}, f32[2,4,3,9]{3,1,2,0:T(4,128)}, u32[]{:S(2)}) copy-start(f32[2,4,3,9]{3,1,2,0:T(4,128)} %param.9) | copy-start | bytes 2596
  52.4 7.1 %copy-start = (f32[8,10,9,1024]{3,2,1,0:T(8,128)S(1)}, f32[8,10,9,1024]{3,2,1,0:T(8,128)}, u32[]{:S(2)}) copy-start(f32[8,10,9,1024]{3,2,1,0:T(8,128)} %reshape.504) | copy-start | bytes 8847364
  59.6 4.4 %copy-start.2 = (f32[2,4,8,8,1024,1]{4,1,5,3,2,0:T(4,128)S(1)}, f32[2,4,8,8,1024,1]{4,1,5,3,2,0:T(4,128)}, u32[]{:S(2)}) copy-start(f32[2,4,8,8,1024,1]{4,1,5,3,2,0:T(4,128)} %fusion.25) | copy-start | bytes 6291460
  71.2 2.7 %copy-start.3 = (f32[16,4096]{1,0:T(8,128)S(1)}, f32[16,4096]{1,0:T(8,128)}, u32[]{:S(2)}) copy-start(f32[16,4096]{1,0:T(8,128)} %param.12) | copy-start | bytes 786436
  74.4 1.3 copy-start.1
  110.3 6.4 %copy-start.7 = (f32[64,8,64]{2,1,0:T(8,128)S(1)}, f32[64,8,64]{2,1,0:T(8,128)}, u32[]{:S(2)}) copy-start(f32[64,8,64]{2,1,0:T(8,128)} %get-tuple-element.27) | copy-start | bytes 393220
  143.7 3.1 %copy-start.6 = (f32[8,64,64]{2,0,1:T(8,128)S(1)}, f32[8,64,64]{2,0,1:T(8,128)}, u32[]{:S(2)}) copy-start(f32[8,64,64]{2,0,1:T(8,128)} %get-tuple-element.13) | copy-start | bytes 393220

commit v3 on v2

--- a/solution.py
+++ b/solution.py
@@ -1,6 +1,8 @@
 import jax
 import jax.numpy as jnp
 from jax import lax
+from jax.experimental import pallas as pl
+from jax.experimental.pallas import tpu as pltpu
 from jax.sharding import PartitionSpec as P
 
 BAND = 128
@@ -71,6 +73,217 @@
     return picked.transpose(1, 2, 3, 0, 4).reshape(samples, shells, slots, pixels)
 
 
+INTERPRET = False
+LANES = 128
+
+
+def shifted(values, amount, toward_end):
+    rows = values.shape[0]
+    row = lax.broadcasted_iota(jnp.int32, values.shape, 0)
+    forward = pltpu.roll(values, amount, 0)
+    backward = pltpu.roll(values, rows - amount, 0)
+    probe = pltpu.roll(row, amount, 0)
+    plain = probe == jnp.where(row >= amount, row - amount, row + rows - amount)
+    if toward_end:
+        moved = jnp.where(plain, forward, backward)
+        return jnp.where(row >= amount, moved, 0.0)
+    moved = jnp.where(plain, backward, forward)
+    return jnp.where(row < rows - amount, moved, 0.0)
+
+
+def running(values, toward_end):
+    for amount in (1, 2, 4):
+        values = values + shifted(values, amount, toward_end)
+    return values
+
+
+def forward_kernel(
+    weights_ref, sqrt_ref, pieces_ref, onehot_ref, excite_ref, counts_ref, stars_ref, widths_ref,
+    density_ref, local_ref, sums_ref, picked_ref,
+):
+    blocks = onehot_ref.shape[0]
+    slots = onehot_ref.shape[2] // LANES
+    tile = blocks * LANES
+
+    def one_block(b, carry):
+        picked = jnp.dot(pieces_ref[0, b], onehot_ref[b], preferred_element_type=jnp.float32)
+        picked_ref[...] = (picked[0:16] + picked[16:32]) + picked[32:48]
+        acc = {}
+        for t in range(2):
+            for q in range(4):
+                total = None
+                for u in range(2):
+                    for r in range(4):
+                        lanes = pl.ds(pl.multiple_of(r * tile + b * LANES, LANES), LANES)
+                        term = sqrt_ref[((t * 4 + q) * 2 + u) * 4 + r] * excite_ref[0, u, :, lanes].astype(jnp.float32)
+                        total = term if total is None else total + term
+                acc[t, q] = total
+        for j in range(3):
+            for m in range(slots):
+                near = picked_ref[pl.ds(j, 8), pl.ds(m * LANES, LANES)]
+                for t in range(2):
+                    for q in range(4):
+                        acc[t, q] = acc[t, q] + weights_ref[((t * 4 + q) * 3 + j) * 9 + m] * near
+        for q in range(4):
+            lanes = pl.ds(pl.multiple_of(q * tile + b * LANES, LANES), LANES)
+            even = jnp.exp(acc[0, q]) * widths_ref[0]
+            odd = jnp.exp(acc[1, q]) * widths_ref[1]
+            density_ref[0, 0, :, lanes] = even
+            density_ref[0, 1, :, lanes] = odd
+            through = running(even + odd, True)
+            before = shifted(through, 1, True) + even
+            local_ref[0, 0, :, lanes] = before
+            local_ref[0, 1, :, lanes] = through
+            misfit = counts_ref[0, :, lanes] * (before - stars_ref[0, :, lanes]) + counts_ref[1, :, lanes] * (
+                through - stars_ref[1, :, lanes]
+            )
+            sums_ref[0, 0:1, lanes] = through[7:8]
+            sums_ref[0, 1:2, lanes] = jnp.sum(misfit, axis=0, keepdims=True)
+        return carry
+
+    lax.fori_loop(0, blocks, one_block, 0)
+
+
+def backward_kernel(
+    sqrt_ref, density_ref, local_ref, carries_ref, counts_ref, stars_ref, extinct_ref, grad_ref
+):
+    tile = density_ref.shape[3] // 4
+    blocks = tile // LANES
+
+    def one_block(b, carry):
+        flow = {}
+        for q in range(4):
+            lanes = pl.ds(pl.multiple_of(q * tile + b * LANES, LANES), LANES)
+            into = carries_ref[0, 0:1, lanes]
+            past = carries_ref[0, 1:2, lanes]
+            even = local_ref[0, 0, :, lanes] + into
+            odd = local_ref[0, 1, :, lanes] + into
+            extinct_ref[0, 0, :, lanes] = even.astype(extinct_ref.dtype)
+            extinct_ref[0, 1, :, lanes] = odd.astype(extinct_ref.dtype)
+            miss_even = counts_ref[0, :, lanes] * (even - stars_ref[0, :, lanes])
+            miss_odd = counts_ref[1, :, lanes] * (odd - stars_ref[1, :, lanes])
+            behind = running(miss_even + miss_odd, False)
+            back_even = behind + past
+            back_odd = (shifted(behind, 1, False) + miss_odd) + past
+            flow[0, q] = density_ref[0, 0, :, lanes] * back_even
+            flow[1, q] = density_ref[0, 1, :, lanes] * back_odd
+        for u in range(2):
+            for r in range(4):
+                total = None
+                for t in range(2):
+                    for q in range(4):
+                        term = sqrt_ref[((t * 4 + q) * 2 + u) * 4 + r] * flow[t, q]
+                        total = term if total is None else total + term
+                lanes = pl.ds(pl.multiple_of(r * tile + b * LANES, LANES), LANES)
+                grad_ref[0, u, :, lanes] = total
+        return carry
+
+    lax.fori_loop(0, blocks, one_block, 0)
+
+
+def by_parity(values):
+    lead = values.shape[:-2]
+    shells, width = values.shape[-2:]
+    values = values.reshape(lead + (shells // 2, 2, width))
+    return jnp.swapaxes(values, -2, -3)
+
+
+def from_parity(values):
+    lead = values.shape[:-3]
+    _, shells, width = values.shape[-3:]
+    return jnp.swapaxes(values, -2, -3).reshape(lead + (2 * shells, width))
+
+
+def local_forward(extended, halo_index, excitations, refine_weights, refine_sqrt, counts, stars, widths):
+    samples, shells, _ = extended.shape
+    slots, pixels = halo_index.shape
+    blocks = pixels // BAND
+    window = 3 * BAND
+    fine_shells = excitations.shape[1]
+    fine_pixels = excitations.shape[2]
+    windows = jnp.stack(
+        [extended[:, :, b * BAND : b * BAND + window] for b in range(blocks)], axis=1
+    )
+    pieces = split_three(windows)
+    pieces = jnp.pad(pieces, ((0, 0), (0, 0), (0, 0), (0, 16 - shells), (0, 0)))
+    pieces = pieces.transpose(1, 2, 0, 3, 4).reshape(samples, blocks, 3 * 16, window)
+    starts = (jnp.arange(blocks, dtype=jnp.int32) * BAND)[None, :, None]
+    local = halo_index.reshape(slots, blocks, BAND) - starts
+    spots = jnp.arange(window, dtype=jnp.int32)[None, :, None, None]
+    onehot = (local.transpose(1, 0, 2)[:, None] == spots).astype(jnp.bfloat16)
+    onehot = onehot.reshape(blocks, window, slots * BAND)
+    excite = by_parity(excitations)
+    half = fine_shells // 2
+    wide = jnp.broadcast_to(widths.reshape(half, 2).T[:, :, None], (2, half, LANES))
+    smem = pl.BlockSpec(memory_space=pltpu.SMEM)
+    whole = lambda shape: pl.BlockSpec(shape, lambda k: (0,) * len(shape))
+    per_sample = lambda shape: pl.BlockSpec(shape, lambda k: (k,) + (0,) * (len(shape) - 1))
+    return pl.pallas_call(
+        forward_kernel,
+        grid=(samples,),
+        in_specs=[
+            smem,
+            smem,
+            per_sample((1, blocks, 48, window)),
+            whole((blocks, window, slots * BAND)),
+            per_sample((1, 2, half, fine_pixels)),
+            whole((2, half, fine_pixels)),
+            whole((2, half, fine_pixels)),
+            whole((2, half, LANES)),
+        ],
+        out_specs=[
+            per_sample((1, 2, half, fine_pixels)),
+            per_sample((1, 2, half, fine_pixels)),
+            per_sample((1, 2, fine_pixels)),
+        ],
+        out_shape=[
+            jax.ShapeDtypeStruct((samples, 2, half, fine_pixels), jnp.float32),
+            jax.ShapeDtypeStruct((samples, 2, half, fine_pixels), jnp.float32),
+            jax.ShapeDtypeStruct((samples, 2, fine_pixels), jnp.float32),
+        ],
+        scratch_shapes=[pltpu.VMEM((16, slots * BAND), jnp.float32)],
+        interpret=INTERPRET,
+    )(
+        refine_weights.reshape(-1),
+        refine_sqrt.astype(jnp.float32).reshape(-1),
+        pieces,
+        onehot,
+        excite,
+        by_parity(counts),
+        by_parity(stars),
+        wide,
+    )
+
+
+def local_backward(refine_sqrt, density, local_cum, carries, counts, stars):
+    samples, _, half, fine_pixels = density.shape
+    smem = pl.BlockSpec(memory_space=pltpu.SMEM)
+    whole = lambda shape: pl.BlockSpec(shape, lambda k: (0,) * len(shape))
+    per_sample = lambda shape: pl.BlockSpec(shape, lambda k: (k,) + (0,) * (len(shape) - 1))
+    extinct, grad = pl.pallas_call(
+        backward_kernel,
+        grid=(samples,),
+        in_specs=[
+            smem,
+            per_sample((1, 2, half, fine_pixels)),
+            per_sample((1, 2, half, fine_pixels)),
+            per_sample((1, 2, fine_pixels)),
+            whole((2, half, fine_pixels)),
+            whole((2, half, fine_pixels)),
+        ],
+        out_specs=[
+            per_sample((1, 2, half, fine_pixels)),
+            per_sample((1, 2, half, fine_pixels)),
+        ],
+        out_shape=[
+            jax.ShapeDtypeStruct((samples, 2, half, fine_pixels), jnp.bfloat16),
+            jax.ShapeDtypeStruct((samples, 2, half, fine_pixels), jnp.float32),
+        ],
+        interpret=INTERPRET,
+    )(refine_sqrt.astype(jnp.float32).reshape(-1), density, local_cum, carries, by_parity(counts), by_parity(stars))
+    return from_parity(extinct), from_parity(grad)
+
+
 def shards(
     coarse_field, excitations, refine_weights, refine_sqrt, halo_index, star_extinction, star_counts
 ):
@@ -83,38 +296,17 @@
     blocked = coarse_field.reshape(samples, coarse_shells, coarse_pixels // BAND, BAND)
     extended = with_halo(blocked, (("dist", 1), ("sky", 2)), 1)
     extended = extended.reshape(samples, coarse_shells + 2, coarse_pixels + 2 * BAND)
-    nearby = gather_nearby(extended, halo_index)
-    local_part = excitations.reshape(samples, coarse_shells, 2, 4, coarse_pixels)
-    refined = jnp.einsum(
-        "ksabc,tqab->kstqc", local_part, refine_sqrt, preferred_element_type=jnp.float32
-    )
-    for offset in range(3):
-        refined = refined + jnp.einsum(
-            "ksmc,tqm->kstqc",
-            nearby[:, offset : offset + coarse_shells],
-            refine_weights[:, :, offset, :],
-            precision=exact_mode,
-        )
-    refined = refined.reshape(samples, fine_shells, fine_pixels)
     shells = dist_rank * fine_shells + jnp.arange(fine_shells, dtype=jnp.int32)
     middle = (shells.astype(jnp.float32) + 0.5) / all_shells
     widths = 3.0 * jnp.exp(3.0 * middle - 3.0) / all_shells
-    density = jnp.exp(refined) * widths[None, :, None]
-    local_cum = jnp.cumsum(density, axis=1)
-    totals = local_cum[:, -1, :]
     counts = star_counts.astype(jnp.float32)
-    partial = jnp.sum(counts[None] * (local_cum - star_extinction[None]), axis=1)
+    density, local_cum, sums = local_forward(
+        extended, halo_index, excitations, refine_weights, refine_sqrt, counts, star_extinction, widths
+    )
     weight = jnp.sum(counts, axis=0, keepdims=True)
-    carry_in, carry_out = block_carries(totals, partial, weight, "dist")
-    cumulative = local_cum + carry_in[:, None, :]
-    misfit = counts[None] * (cumulative - star_extinction[None])
-    local_back = jnp.flip(jnp.cumsum(jnp.flip(misfit, 1), axis=1), 1)
-    back = local_back + carry_out[:, None, :]
-    flowing = (density * back).reshape(samples, coarse_shells, 2, 4, coarse_pixels)
-    gradient = jnp.einsum(
-        "kstqc,tqab->ksabc", flowing, refine_sqrt.astype(jnp.float32), precision=exact_mode
-    )
-    return (cumulative.astype(jnp.bfloat16), gradient.reshape(samples, fine_shells, fine_pixels))
+    carry_in, carry_out = block_carries(sums[:, 0], sums[:, 1], weight, "dist")
+    carries = jnp.stack([carry_in, carry_out], axis=1)
+    return local_backward(refine_sqrt, density, local_cum, carries, counts, star_extinction)
 
 
 def solution(mesh):

time: 158 us -> 139 us (0.88)
  Pallas kernels: 0 us -> 40.5 us
  matrix products: 28.7 us -> 0 us
  local copies, waits for them, and re-layouts: 38.8 us -> 22.4 us
  other arithmetic: 27.7 us -> 17.7 us
  waiting for transfers between devices: 3.31 us -> 0.01 us
    pallas_call x0 -> x2, Pallas kernels: none -> 40.5 us  [the longest x1 32.3 us: local_forward(): pl.pallas_call(forward_kernel, grid=(samples,), in_specs=[smem, smem, per...]
    dot_general x6 -> x0, matrix products: 28.7 us -> none  [the longest x3 17.2 us: shards(): jnp.einsum('ksmc,tqm->kstqc', nearby[:, offset:offset + coarse_shells], r...]
    reshape x5, local copies, waits for them, and re-layouts: 20.6 us -> 4.09 us  [the longest x3 2.81 us: by_parity(): values = values.reshape(lead + (shells // 2, 2, width))]
    transpose x2 -> x1, other arithmetic: 7.76 us -> 0.36 us  [local_forward(): pieces.transpose(1, 2, 0, 3, 4).reshape(samples, blocks, 3 * 16, window)]
    transpose x1 -> x4, local copies, waits for them, and re-layouts: 0.15 us -> 6.27 us  [the longest x2 3.39 us: from_parity(): return jnp.swapaxes(values, -2, -3).reshape(lead + (2 * shells, width))]
    convert_element_type x0 -> x1, other arithmetic: none -> 5.74 us  [local_forward(): onehot = (local.transpose(1, 0, 2)[:, None] == spots).astype(jnp.bfloat16)]
    mul x3 -> x1, other arithmetic: 5.24 us -> 0.01 us  [local_forward(): starts = (jnp.arange(blocks, dtype=jnp.int32) * BAND)[None, :, None]]
    exp x2 -> x0, local copies, waits for them, and re-layouts: 4.27 us -> none  [shards(): density = jnp.exp(refined) * widths[None, :, None]]
  transfers between devices with their start and end apart: 4 -> 4, of which waited for: 1 -> 0; matrix products, arithmetic and copies ran while one was open for 3% -> 10% of each run, Pallas kernels for 0% -> 0%
where the time goes in v3:
time: 139 us; the launch traced here: 138 us
  blocking collectives  45.6 us (33%)
  Pallas kernels  40.5 us (29%)
  local copies, waits for them, and re-layouts  22.4 us (16%)
  other arithmetic  17.7 us (13%)
  starting transfers between devices  10.9 us (8%)
    pallas_call x1, Pallas kernels, local_forward(): pl.pallas_call(forward_kernel, grid=(samples,), in_specs=[smem, smem, per...  32.3 us
    all_to_all x1, blocking collectives, block_carries(): mine = lax.all_to_all(packed, axis, 0, 0, tiled=True)  27.8 us
    all_to_all x1, blocking collectives, block_carries(): lax.all_to_all(jnp.concatenate([carry_in, carry_out], axis=1), axis, 0, 0...  17.8 us
    pallas_call x1, Pallas kernels, local_backward(): pl.pallas_call(backward_kernel, grid=(samples,), in_specs=[smem, per_samp...  8.17 us
    ppermute x2, starting transfers between devices, with_halo(): lax.ppermute(lax.slice_in_dim(block, block.shape[dim] - width, None, axis...  7.7 us
    unnamed x31, local copies, waits for them, and re-layouts  7.65 us
    another operation x1, other arithmetic, block_carries(): behind = jnp.flip(jnp.cumsum(jnp.flip(block_misfit, 0), axis=0), 0)  6.33 us
    convert_element_type x1, other arithmetic, local_forward(): onehot = (local.transpose(1, 0, 2)[:, None] == spots).astype(jnp.bfloat16)  5.74 us
  transfers between devices with their start and end apart: 4, of which 0 were waited for; matrix products, arithmetic and copies ran while one was open for 10% of the time, Pallas kernels for 0%

profile of v3, /device:TPU:1, one launch (start us, length us, event | category | flops | bytes accessed | tf_op | source)
XLA Modules:
  0.0 138.3 jit_solution(13338964004727298235)
XLA Ops:
  0.6 1.0 copy.61
  1.6 4.5 %collective-permute-start = (f32[8,1,8,128]{3,2,1,0:T(8,128)S(1)}, f32[8,1,8,128]{3,2,1,0:T(8,128)S(1)}, u32[]{:S(2)}, u32[]{:S(2)}) collective-permute-start(f32[8,1,8,128]{3,2,1,0:T(8,128)S(1)} %get-tuple-element.26), channel_id=1, source_target_pairs={{0,4},{4,8},{8,12},{12,16},{16,20},{20,24},{24,28},{28,32},{32,36}... | collective-permute-start | bytes 98312 | tf_op jit(solution)/shard_map/ppermute | solution.py:19
  6.2 1.9 %collective-permute-start.1 = (f32[8,1,8,128]{3,2,1,0:T(8,128)S(1)}, f32[8,1,8,128]{3,2,1,0:T(8,128)S(1)}, u32[]{:S(2)}, u32[]{:S(2)}) collective-permute-start(f32[8,1,8,128]{3,2,1,0:T(8,128)S(1)} %get-tuple-element.25), channel_id=1, source_target_pairs={{4,0},{8,4},{12,8},{16,12},{20,16},{24,20},{28,24},{32,28},{36,32}... | collective-permute-start | bytes 98312 | tf_op jit(solution)/shard_map/ppermute | solution.py:22
  8.1 1.0 convert_element_type.18
  9.1 0.2 reshape.469
  9.2 1.1 reshape.470
  10.4 0.9 copy.51
  11.2 0.1 fusion.18
  11.3 5.7 %fusion.onehot_ref = bf16[8,384,1152]{2,1,0:T(8,128)(2,1)} fusion(s32[8,1152]{1,0:T(8,128)S(1)} %fusion.18), kind=kLoop, calls=%fused_computation.1 | loop fusion | flops 7077888 | bytes 7114752 | tf_op jit(solution)/shard_map/convert_element_type | solution.py:213
  17.0 1.1 copy_bitcast_fusion.3
  18.1 0.0 copy-done.2
  18.2 0.0 collective-permute-done
  18.2 0.0 copy-done.3
  18.2 0.0 copy-start.4
  18.2 0.1 constant_dynamic-update-slice_fusion.1
  18.3 0.0 collective-permute-done.1
  18.3 0.1 fusion.20
  18.4 3.2 %collective-permute-start.2 = (f32[8,10,1,128]{3,2,1,0:T(1,128)S(1)}, f32[8,10,1,128]{3,2,1,0:T(1,128)S(1)}, u32[]{:S(2)}, u32[]{:S(2)}) collective-permute-start(f32[8,10,1,128]{3,2,1,0:T(1,128)S(1)} %get-tuple-element.23), channel_id=1, source_target_pairs={{0,1},{1,2},{2,3},{4,5},{5,6},{6,7},{8,9},{9,10},{10,11},{12,13},{... | collective-permute-start | bytes 122888 | tf_op jit(solution)/shard_map/ppermute | solution.py:19
  21.6 1.3 collective-permute-start.3
  22.9 0.0 copy-done.5
  22.9 0.6 reshape.474.sqrt_ref
  23.5 0.6 copy.38
  24.1 1.6 %copy.59 = bf16[8,8,2,4096]{3,1,2,0:T(8,128)(2,1)} copy(bf16[8,8,2,4096]{3,0,2,1:T(8,128)(2,1)S(1)} %bitcast.82) | data formatting | bytes 2097152 | tf_op jit(solution)/shard_map/reshape | solution.py:187
  25.6 0.0 copy-done.4
  25.7 0.7 reshape.463.weights_ref
  26.3 0.1 concatenate.53
  26.4 0.0 collective-permute-done.2
  26.4 0.0 collective-permute-done.3
  26.4 0.1 pad_maximum_fusion
  26.6 0.2 copy.60
  27.0 0.2 reduce-precision_convert_fusion.1
  27.2 0.4 fusion.6
  27.6 1.8 %copy.37 = bf16[8,8,3,16,384]{4,3,2,1,0:T(8,128)(2,1)} copy(bf16[8,8,3,16,384]{4,0,3,1,2:T(8,128)(2,1)S(1)} %fusion.6) | data formatting | bytes 4718592 | tf_op jit(solution)/shard_map/transpose | solution.py:209
  29.4 0.7 broadcast_in_dim.2.widths_ref
  30.0 32.3 %shard_map.86 = (f32[8,2,8,4096]{3,2,1,0:T(8,128)}, f32[8,2,8,4096]{3,2,1,0:T(8,128)}, f32[8,2,4096]{2,1,0:T(2,128)}) custom-call(f32[216]{0:T(256)} %reshape.463.weights_ref, f32[64]{0:T(128)} %reshape.474.sqrt_ref, bf16[8,8,48,384]{3,2,1,0:T(8,128)(2,1)} %bitcast.70, bf16[8,384,1152]{2,1,0:T(8,128)(2,1)} %fusion.onehot_ref, ...), custom_call_target="tpu_custom_call" | custom-call | tf_op jit(solution)/shard_map/pallas_call | solution.py:221
  62.4 1.7 %slice_reduce_fusion.1 = (f32[8,4096]{1,0:T(8,128)S(1)}, f32[8,4096]{1,0:T(8,128)S(1)}) fusion(f32[8,2,4096]{2,1,0:T(2,128)} %get-tuple-element.9), kind=kLoop, calls=%fused_computation.28 | loop fusion | bytes 524288 | tf_op jit(solution)/shard_map/slice | solution.py:307
  64.1 0.1 concatenate.51
  64.2 0.2 copy.42
  64.4 0.1 concatenate.52
  64.5 0.2 copy.43
  64.7 0.1 maximum_bitcast_fusion
  64.7 0.4 reshape.477
  65.1 27.8 %all_to_all.10 = f32[64,1,1088]{2,1,0:T(1,128)S(1)} all-to-all(f32[64,1,1088]{2,1,0:T(1,128)S(1)} %reshape.477), channel_id=1, replica_groups=mesh['dist'=64,'sky'=4] {'dist'}, dimensions={0} | all-to-all | bytes 557056 | tf_op jit(solution)/shard_map/all_to_all | solution.py:33
  92.9 0.5 broadcast.61
  93.4 1.3 reduce.4
  94.8 0.1 reshape.478
  94.9 0.1 fusion.8
  95.0 0.1 fusion.22
  95.1 6.3 %fusion.23 = f32[64,8,64]{2,1,0:T(8,128)S(1)} fusion(f32[64,8,64]{2,1,0:T(8,128)S(1)} %rev.5), kind=kOutput, calls=%fused_computation.57 | output fusion | flops 2064384 | bytes 262144 | tf_op jit(solution)/shard_map/jit(cumsum)/reduce_window_sum | solution.py:41
  101.5 0.3 reshape.479
  101.9 17.8 %all_to_all.11 = f32[64,1,1024]{2,1,0:T(1,128)S(1)} all-to-all(f32[64,1,1024]{2,1,0:T(1,128)S(1)} %reshape.479), channel_id=1, replica_groups=mesh['dist'=64,'sky'=4] {'dist'}, dimensions={0} | all-to-all | bytes 524288 | tf_op jit(solution)/shard_map/all_to_all | solution.py:43
  119.7 1.3 reduce.5
  121.0 0.1 reshape.480
  121.1 0.1 copy.44
  121.2 0.2 stack.53
  121.4 0.1 copy.45
  121.4 0.2 stack.54
  121.6 1.0 pad_maximum_fusion.1.carries_ref
  122.6 8.2 %shard_map.87 = (bf16[8,2,8,4096]{3,2,1,0:T(8,128)(2,1)}, f32[8,2,8,4096]{3,2,1,0:T(8,128)}) custom-call(f32[64]{0:T(128)} %reshape.474.sqrt_ref, f32[8,2,8,4096]{3,2,1,0:T(8,128)} %get-tuple-element.7.density_ref, f32[8,2,8,4096]{3,2,1,0:T(8,128)} %get-tuple-element.8.local_ref, f32[8,2,4096]{2,1,0:T(2,128)} %pad_maximum_fusion.1.carries_ref, ...), custom_call_target="tpu_custom_call" | custom-call | tf_op jit(solution)/shard_map/pallas_call | solution.py:263
  130.8 2.8 %copy.47 = f32[8,8,2,4096]{3,0,2,1:T(8,128)S(1)} copy(f32[8,8,2,4096]{3,1,2,0:T(8,128)} %bitcast.83) | data formatting | bytes 4194304 | tf_op jit(solution)/shard_map/transpose | solution.py:194
  133.6 0.0 copy-start.1
  133.6 2.5 %copy.49 = f32[8,16,4096]{2,1,0:T(8,128)} copy(f32[8,16,4096]{2,0,1:T(8,128)S(1)} %bitcast.71) | data formatting | bytes 4194304
  136.1 0.6 copy.46
  136.7 1.6 %copy.48 = bf16[8,16,4096]{2,1,0:T(8,128)(2,1)} copy(bf16[8,16,4096]{2,0,1:T(8,128)(2,1)S(1)} %bitcast.81) | data formatting | bytes 2097152
  (28 shorter events, 0.4 us)
Async XLA Ops:
  1.6 16.5 %collective-permute-start = (f32[8,1,8,128]{3,2,1,0:T(8,128)S(1)}, f32[8,1,8,128]{3,2,1,0:T(8,128)S(1)}, u32[]{:S(2)}, u32[]{:S(2)}) collective-permute-start(f32[8,1,8,128]{3,2,1,0:T(8,128)S(1)} %get-tuple-element.26), channel_id=1, source_target_pairs={{0,4},{4,8},{8,12},{12,16},{16,20},{20,24},{24,28},{28,32},{32,36}... | collective-permute-start | bytes 98312 | tf_op jit(solution)/shard_map/ppermute | solution.py:19
  6.2 12.1 %collective-permute-start.1 = (f32[8,1,8,128]{3,2,1,0:T(8,128)S(1)}, f32[8,1,8,128]{3,2,1,0:T(8,128)S(1)}, u32[]{:S(2)}, u32[]{:S(2)}) collective-permute-start(f32[8,1,8,128]{3,2,1,0:T(8,128)S(1)} %get-tuple-element.25), channel_id=1, source_target_pairs={{4,0},{8,4},{12,8},{16,12},{20,16},{24,20},{28,24},{32,28},{36,32}... | collective-permute-start | bytes 98312 | tf_op jit(solution)/shard_map/ppermute | solution.py:22
  11.3 6.9 %copy-start.2 = (s32[16,4096]{1,0:T(8,128)S(1)}, s32[16,4096]{1,0:T(8,128)}, u32[]{:S(2)}) copy-start(s32[16,4096]{1,0:T(8,128)} %param.13) | copy-start | bytes 786436
  11.3 6.9 %copy-start.3 = (f32[8,8,1024]{2,1,0:T(8,128)S(1)}, f32[8,8,1024]{2,1,0:T(8,128)}, u32[]{:S(2)}) copy-start(f32[8,8,1024]{2,1,0:T(8,128)} %param.7) | copy-start | bytes 786436
  11.3 11.6 %copy-start.5 = (bf16[2,4,2,4]{3,2,1,0:T(2,128)(2,1)S(1)}, bf16[2,4,2,4]{3,2,1,0:T(2,128)(2,1)}, u32[]{:S(2)}) copy-start(bf16[2,4,2,4]{3,2,1,0:T(2,128)(2,1)} %param.10) | copy-start | bytes 388
  17.0 6.5 %copy-start = (bf16[8,16,4096]{2,1,0:T(8,128)(2,1)S(1)}, bf16[8,16,4096]{2,1,0:T(8,128)(2,1)}, u32[]{:S(2)}) copy-start(bf16[8,16,4096]{2,1,0:T(8,128)(2,1)} %param.8) | copy-start | bytes 3145732
  18.2 7.4 %copy-start.4 = (f32[2,4,3,9]{3,1,2,0:T(4,128)S(1)}, f32[2,4,3,9]{3,1,2,0:T(4,128)}, u32[]{:S(2)}) copy-start(f32[2,4,3,9]{3,1,2,0:T(4,128)} %param.9) | copy-start | bytes 2596
  18.4 8.1 %collective-permute-start.2 = (f32[8,10,1,128]{3,2,1,0:T(1,128)S(1)}, f32[8,10,1,128]{3,2,1,0:T(1,128)S(1)}, u32[]{:S(2)}, u32[]{:S(2)}) collective-permute-start(f32[8,10,1,128]{3,2,1,0:T(1,128)S(1)} %get-tuple-element.23), channel_id=1, source_target_pairs={{0,1},{1,2},{2,3},{4,5},{5,6},{6,7},{8,9},{9,10},{10,11},{12,13},{... | collective-permute-start | bytes 122888 | tf_op jit(solution)/shard_map/ppermute | solution.py:19
  21.6 4.9 %collective-permute-start.3 = (f32[8,10,1,128]{3,2,1,0:T(1,128)S(1)}, f32[8,10,1,128]{3,2,1,0:T(1,128)S(1)}, u32[]{:S(2)}, u32[]{:S(2)}) collective-permute-start(f32[8,10,1,128]{3,2,1,0:T(1,128)S(1)} %get-tuple-element.24), channel_id=1, source_target_pairs={{1,0},{2,1},{3,2},{5,4},{6,5},{7,6},{9,8},{10,9},{11,10},{13,12},{... | collective-permute-start | bytes 122888 | tf_op jit(solution)/shard_map/ppermute | solution.py:22
  133.6 2.6 %copy-start.1 = (bf16[8,2,8,4096]{3,2,1,0:T(8,128)(2,1)S(1)}, bf16[8,2,8,4096]{3,2,1,0:T(8,128)(2,1)}, u32[]{:S(2)}) copy-start(bf16[8,2,8,4096]{3,2,1,0:T(8,128)(2,1)} %get-tuple-element.10) | copy-start | bytes 3145732

commit v4 on v3

--- a/solution.py
+++ b/solution.py
@@ -6,6 +6,7 @@
 from jax.sharding import PartitionSpec as P
 
 BAND = 128
+DIST = ("dist_outer", "dist_inner")
 
 
 exact_mode = lax.Precision.HIGHEST
@@ -24,24 +25,50 @@
     return block
 
 
-def block_carries(totals, partial, weight, axis):
+def exclusive(values, reverse):
+    zero = jnp.zeros_like(values[:1])
+    if reverse:
+        behind = jnp.flip(jnp.cumsum(jnp.flip(values, 0), axis=0), 0)
+        return jnp.concatenate([behind[1:], zero], axis=0)
+    ahead = jnp.cumsum(values, axis=0)
+    return jnp.concatenate([zero, ahead[:-1]], axis=0)
+
+
+def spread(packed, axis):
     count = lax.axis_size(axis)
-    rows, pixels = totals.shape
-    width = pixels // count
-    packed = jnp.concatenate([totals, partial, weight], axis=0)
-    packed = packed.reshape(packed.shape[0], count, width).transpose(1, 0, 2)
-    mine = lax.all_to_all(packed, axis, 0, 0, tiled=True)
+    height, width = packed.shape
+    packed = packed.reshape(height, count, width // count).transpose(1, 0, 2)
+    return lax.all_to_all(packed, axis, 0, 0, tiled=True)
+
+
+def gather_back(parts, axis):
+    parts = lax.all_to_all(parts, axis, 0, 0, tiled=True)
+    count, height, width = parts.shape
+    return parts.transpose(1, 0, 2).reshape(height, count * width)
+
+
+def block_carries(totals, partial, weight, outer, inner):
+    rows = totals.shape[0]
+    mine = spread(jnp.concatenate([totals, partial, weight], axis=0), inner)
     block_totals = mine[:, :rows]
-    block_partial = mine[:, rows : 2 * rows]
     block_weight = mine[:, 2 * rows :]
-    zero = jnp.zeros_like(block_totals[:1])
-    ahead = jnp.cumsum(block_totals, axis=0)
-    carry_in = jnp.concatenate([zero, ahead[:-1]], axis=0)
-    block_misfit = block_partial + block_weight * carry_in
-    behind = jnp.flip(jnp.cumsum(jnp.flip(block_misfit, 0), axis=0), 0)
-    carry_out = jnp.concatenate([behind[1:], zero], axis=0)
-    back = lax.all_to_all(jnp.concatenate([carry_in, carry_out], axis=1), axis, 0, 0, tiled=True)
-    back = back.transpose(1, 0, 2).reshape(2 * rows, pixels)
+    within_in = exclusive(block_totals, False)
+    block_misfit = mine[:, rows : 2 * rows] + block_weight * within_in
+    within_out = exclusive(block_misfit, True)
+    weight_out = exclusive(block_weight, True)
+    group = jnp.concatenate(
+        [jnp.sum(block_totals, axis=0), jnp.sum(block_misfit, axis=0), jnp.sum(block_weight, axis=0)], axis=0
+    )
+    groups = spread(group, outer)
+    group_in = exclusive(groups[:, :rows], False)
+    group_misfit = groups[:, rows : 2 * rows] + groups[:, 2 * rows :] * group_in
+    group_out = exclusive(group_misfit, True)
+    shared = gather_back(jnp.concatenate([group_in, group_out], axis=1), outer)
+    before = shared[:rows][None]
+    after = shared[rows:][None]
+    carry_in = within_in + before
+    carry_out = (within_out + before * weight_out) + after
+    back = gather_back(jnp.concatenate([carry_in, carry_out], axis=1), inner)
     return back[:rows], back[rows:]
 
 
@@ -290,11 +317,11 @@
     samples, coarse_shells, coarse_pixels = coarse_field.shape
     fine_shells = 2 * coarse_shells
     fine_pixels = 4 * coarse_pixels
-    dist_count = lax.axis_size("dist")
-    dist_rank = lax.axis_index("dist")
+    dist_count = lax.axis_size(DIST)
+    dist_rank = lax.axis_index(DIST)
     all_shells = fine_shells * dist_count
     blocked = coarse_field.reshape(samples, coarse_shells, coarse_pixels // BAND, BAND)
-    extended = with_halo(blocked, (("dist", 1), ("sky", 2)), 1)
+    extended = with_halo(blocked, ((DIST, 1), ("sky", 2)), 1)
     extended = extended.reshape(samples, coarse_shells + 2, coarse_pixels + 2 * BAND)
     shells = dist_rank * fine_shells + jnp.arange(fine_shells, dtype=jnp.int32)
     middle = (shells.astype(jnp.float32) + 0.5) / all_shells
@@ -304,25 +331,29 @@
         extended, halo_index, excitations, refine_weights, refine_sqrt, counts, star_extinction, widths
     )
     weight = jnp.sum(counts, axis=0, keepdims=True)
-    carry_in, carry_out = block_carries(sums[:, 0], sums[:, 1], weight, "dist")
+    carry_in, carry_out = block_carries(sums[:, 0], sums[:, 1], weight, *DIST)
     carries = jnp.stack([carry_in, carry_out], axis=1)
     return local_backward(refine_sqrt, density, local_cum, carries, counts, star_extinction)
 
 
 def solution(mesh):
+    dist_count = mesh.shape["dist"]
+    inner = 8 if dist_count % 8 == 0 else dist_count
+    devices = mesh.devices.reshape(dist_count // inner, inner, mesh.shape["sky"])
+    split = jax.sharding.Mesh(devices, DIST + ("sky",))
     placed = (
-        P(None, "dist", "sky"),
-        P(None, "dist", "sky"),
+        P(None, DIST, "sky"),
+        P(None, DIST, "sky"),
         P(),
         P(),
         P(None, "sky"),
-        P("dist", "sky"),
-        P("dist", "sky"),
+        P(DIST, "sky"),
+        P(DIST, "sky"),
     )
     return jax.shard_map(
         shards,
-        mesh=mesh,
+        mesh=split,
         in_specs=placed,
-        out_specs=(P(None, "dist", "sky"), P(None, "dist", "sky")),
+        out_specs=(P(None, DIST, "sky"), P(None, DIST, "sky")),
         check_vma=False,
     )

time: 139 us -> 140 us (level)
  blocking collectives: 45.6 us -> 26.6 us
  starting transfers between devices: 10.9 us -> 24.1 us
  waiting for transfers between devices: 0.01 us -> 12.6 us
  other arithmetic: 17.7 us -> 11.6 us
    all_to_all x2, blocking collectives: 45.6 us -> 26.6 us  [the longest x1 14.2 us: spread(): return lax.all_to_all(packed, axis, 0, 0, tiled=True)]
    all_to_all x0 -> x2, starting transfers between devices: none -> 13.1 us  [the longest x1 9.79 us: spread(): return lax.all_to_all(packed, axis, 0, 0, tiled=True)]
    all_to_all x0 -> x2, waiting for transfers between devices: none -> 12.5 us  [the longest x1 6.78 us: gather_back(): parts = lax.all_to_all(parts, axis, 0, 0, tiled=True)]
    another operation x3 -> x6, other arithmetic: 6.63 us -> 1.62 us  [the longest x3 1.27 us: exclusive(): behind = jnp.flip(jnp.cumsum(jnp.flip(values, 0), axis=0), 0)]
    unnamed x31 -> x34, local copies, waits for them, and re-layouts: 7.65 us -> 8.28 us
  transfers between devices with their start and end apart: 4 -> 6, of which waited for: 0 -> 2; matrix products, arithmetic and copies ran while one was open for 10% -> 11% of each run, Pallas kernels for 0% -> 0%
where the time goes in v4:
time: 140 us; the launch traced here: 139 us
  Pallas kernels  40.5 us (29%)
  blocking collectives  26.6 us (19%)
  starting transfers between devices  24.1 us (17%)
  local copies, waits for them, and re-layouts  22.9 us (16%)
  waiting for transfers between devices  12.6 us (9%)
  other arithmetic  11.6 us (8%)
    pallas_call x1, Pallas kernels, local_forward(): pl.pallas_call(forward_kernel, grid=(samples,), in_specs=[smem, smem, per...  32.3 us
    all_to_all x1, blocking collectives, spread(): return lax.all_to_all(packed, axis, 0, 0, tiled=True)  14.2 us
    all_to_all x1, blocking collectives, gather_back(): parts = lax.all_to_all(parts, axis, 0, 0, tiled=True)  12.3 us
    all_to_all x1, starting transfers between devices, spread(): return lax.all_to_all(packed, axis, 0, 0, tiled=True)  9.79 us
    unnamed x34, local copies, waits for them, and re-layouts  8.28 us
    pallas_call x1, Pallas kernels, local_backward(): pl.pallas_call(backward_kernel, grid=(samples,), in_specs=[smem, per_samp...  8.17 us
    ppermute x2, starting transfers between devices, with_halo(): lax.ppermute(lax.slice_in_dim(block, block.shape[dim] - width, None, axis...  7.7 us
    all_to_all x1, waiting for transfers between devices, gather_back(): parts = lax.all_to_all(parts, axis, 0, 0, tiled=True)  6.78 us
  transfers between devices with their start and end apart: 6, of which 2 were waited for; matrix products, arithmetic and copies ran while one was open for 11% of the time, Pallas kernels for 0%

profile of v4, /device:TPU:1, one launch (start us, length us, event | category | flops | bytes accessed | tf_op | source)
XLA Modules:
  0.0 139.4 jit_solution(9485665715105872445)
XLA Ops:
  0.6 1.0 copy.86
  1.6 4.5 %collective-permute-start = (f32[8,1,8,128]{3,2,1,0:T(8,128)S(1)}, f32[8,1,8,128]{3,2,1,0:T(8,128)S(1)}, u32[]{:S(2)}, u32[]{:S(2)}) collective-permute-start(f32[8,1,8,128]{3,2,1,0:T(8,128)S(1)} %get-tuple-element.35), channel_id=1, source_target_pairs={{0,4},{4,8},{8,12},{12,16},{16,20},{20,24},{24,28},{28,32},{32,36}... | collective-permute-start | bytes 98312 | tf_op jit(solution)/shard_map/ppermute | solution.py:20
  6.2 1.9 %collective-permute-start.1 = (f32[8,1,8,128]{3,2,1,0:T(8,128)S(1)}, f32[8,1,8,128]{3,2,1,0:T(8,128)S(1)}, u32[]{:S(2)}, u32[]{:S(2)}) collective-permute-start(f32[8,1,8,128]{3,2,1,0:T(8,128)S(1)} %get-tuple-element.34), channel_id=1, source_target_pairs={{4,0},{8,4},{12,8},{16,12},{20,16},{24,20},{28,24},{32,28},{36,32}... | collective-permute-start | bytes 98312 | tf_op jit(solution)/shard_map/ppermute | solution.py:23
  8.1 1.0 convert_element_type.18
  9.1 0.2 reshape.482
  9.2 1.1 reshape.483
  10.4 0.9 copy.75
  11.2 0.1 fusion.19
  11.3 5.7 %fusion.onehot_ref = bf16[8,384,1152]{2,1,0:T(8,128)(2,1)} fusion(s32[8,1152]{1,0:T(8,128)S(1)} %fusion.19), kind=kLoop, calls=%fused_computation.1 | loop fusion | flops 7077888 | bytes 7114752 | tf_op jit(solution)/shard_map/convert_element_type | solution.py:240
  17.0 1.1 copy_bitcast_fusion.3
  18.2 0.0 collective-permute-done
  18.2 0.0 copy-start.4
  18.2 0.1 constant_dynamic-update-slice_fusion.1
  18.3 0.0 collective-permute-done.1
  18.3 0.1 fusion.24
  18.4 3.2 %collective-permute-start.2 = (f32[8,10,1,128]{3,2,1,0:T(1,128)S(1)}, f32[8,10,1,128]{3,2,1,0:T(1,128)S(1)}, u32[]{:S(2)}, u32[]{:S(2)}) collective-permute-start(f32[8,10,1,128]{3,2,1,0:T(1,128)S(1)} %get-tuple-element.30), channel_id=1, source_target_pairs={{0,1},{1,2},{2,3},{4,5},{5,6},{6,7},{8,9},{9,10},{10,11},{12,13},{... | collective-permute-start | bytes 122888 | tf_op jit(solution)/shard_map/ppermute | solution.py:20
  21.6 1.3 collective-permute-start.3
  22.9 0.6 reshape.487.sqrt_ref
  23.5 0.6 copy.56
  24.1 1.6 %copy.84 = bf16[8,8,2,4096]{3,1,2,0:T(8,128)(2,1)} copy(bf16[8,8,2,4096]{3,0,2,1:T(8,128)(2,1)S(1)} %bitcast.95) | data formatting | bytes 2097152 | tf_op jit(solution)/shard_map/reshape | solution.py:214
  25.7 0.0 copy-done.4
  25.7 0.7 reshape.476.weights_ref
  26.3 0.0 collective-permute-done.2
  26.3 0.0 collective-permute-done.3
  26.3 0.1 pad_maximum_fusion
  26.5 0.2 copy.85
  26.9 0.2 reduce-precision_convert_fusion.1
  27.1 0.4 fusion.6
  27.5 1.8 %copy.55 = bf16[8,8,3,16,384]{4,3,2,1,0:T(8,128)(2,1)} copy(bf16[8,8,3,16,384]{4,0,3,1,2:T(8,128)(2,1)S(1)} %fusion.6) | data formatting | bytes 4718592 | tf_op jit(solution)/shard_map/transpose | solution.py:236
  29.3 0.7 broadcast_in_dim.2.widths_ref
  29.9 32.3 %shard_map.86 = (f32[8,2,8,4096]{3,2,1,0:T(8,128)}, f32[8,2,8,4096]{3,2,1,0:T(8,128)}, f32[8,2,4096]{2,1,0:T(2,128)}) custom-call(f32[216]{0:T(256)} %reshape.476.weights_ref, f32[64]{0:T(128)} %reshape.487.sqrt_ref, bf16[8,8,48,384]{3,2,1,0:T(8,128)(2,1)} %bitcast.83, bf16[8,384,1152]{2,1,0:T(8,128)(2,1)} %fusion.onehot_ref, ...), custom_call_target="tpu_custom_call" | custom-call | tf_op jit(solution)/shard_map/pallas_call | solution.py:248
  62.3 1.7 %slice_reduce_fusion.1 = (f32[8,4096]{1,0:T(8,128)S(1)}, f32[8,4096]{1,0:T(8,128)S(1)}) fusion(f32[8,2,4096]{2,1,0:T(2,128)} %get-tuple-element.9), kind=kLoop, calls=%fused_computation.28 | loop fusion | bytes 524288 | tf_op jit(solution)/shard_map/slice | solution.py:334
  64.1 14.2 %all_to_all.20 = f32[8,17,512]{2,1,0:T(8,128)S(1)} all-to-all(f32[8,17,512]{2,1,0:T(8,128)S(1)} %maximum_bitcast_fusion), channel_id=1, replica_groups=mesh['dist_outer'=8,'dist_inner'=8,'sky'=4] {'dist_inner'}, dimensions={0} | all-to-all | bytes 557056 | tf_op jit(solution)/shard_map/all_to_all | solution.py:41
  78.3 0.1 fusion.9
  78.5 0.1 concatenate.78
  78.6 0.1 concatenate.79
  78.7 0.1 concatenate.80
  78.8 0.7 reshape.490
  79.5 9.8 %all-to-all-start.1 = ((f32[8,1,1088]{2,1,0:T(1,128)}), f32[8,1,1088]{2,1,0:T(1,128)S(1)}, u32[]{:S(2)}, u32[]{:S(2)}) async-start(f32[8,1,1088]{2,1,0:T(1,128)} %reshape.490), calls=%async_computation.1 | async-start | bytes 73728 | tf_op jit(solution)/shard_map/all_to_all | solution.py:41
  89.3 1.0 fusion.30
  90.4 5.8 %all-to-all-done.1 = f32[8,1,1088]{2,1,0:T(1,128)S(1)} async-done(((f32[8,1,1088]{2,1,0:T(1,128)}), f32[8,1,1088]{2,1,0:T(1,128)S(1)}, u32[]{:S(2)}, u32[]{:S(2)}) %all-to-all-start.1) | async-done | bytes 34848 | tf_op jit(solution)/shard_map/all_to_all | solution.py:41
  96.2 0.6 broadcast.69
  96.8 0.8 reduce.5
  97.6 0.1 reshape.491
  97.7 0.2 fusion.29
  98.0 0.7 reshape.492
  98.7 3.3 %all-to-all-start.2 = ((f32[8,1,1024]{2,1,0:T(1,128)}), f32[8,1,1024]{2,1,0:T(1,128)S(1)}, u32[]{:S(2)}, u32[]{:S(2)}) async-start(f32[8,1,1024]{2,1,0:T(1,128)} %reshape.492), calls=%async_computation.2 | async-start | bytes 65536 | tf_op jit(solution)/shard_map/all_to_all | solution.py:45
  102.0 6.8 %all-to-all-done.2 = f32[8,1,1024]{2,1,0:T(1,128)S(1)} async-done(((f32[8,1,1024]{2,1,0:T(1,128)}), f32[8,1,1024]{2,1,0:T(1,128)S(1)}, u32[]{:S(2)}, u32[]{:S(2)}) %all-to-all-start.2) | async-done | bytes 32800 | tf_op jit(solution)/shard_map/all_to_all | solution.py:45
  108.8 0.7 reduce.6
  109.6 0.1 reshape.493
  109.7 0.1 add.68
  109.8 0.1 add.72
  109.9 12.3 %all_to_all.21 = f32[8,16,512]{2,1,0:T(8,128)S(1)} all-to-all(f32[8,16,512]{2,1,0:T(8,128)S(1)} %pad_maximum_fusion.1), channel_id=1, replica_groups=mesh['dist_outer'=8,'dist_inner'=8,'sky'=4] {'dist_inner'}, dimensions={0} | all-to-all | bytes 524288 | tf_op jit(solution)/shard_map/all_to_all | solution.py:45
  122.3 0.1 copy.65
  122.3 0.1 stack.53
  122.5 0.1 copy.66
  122.6 0.1 stack.54
  122.7 1.0 pad_maximum_fusion.2.carries_ref
  123.7 8.2 %shard_map.87 = (bf16[8,2,8,4096]{3,2,1,0:T(8,128)(2,1)}, f32[8,2,8,4096]{3,2,1,0:T(8,128)}) custom-call(f32[64]{0:T(128)} %reshape.487.sqrt_ref, f32[8,2,8,4096]{3,2,1,0:T(8,128)} %get-tuple-element.7.density_ref, f32[8,2,8,4096]{3,2,1,0:T(8,128)} %get-tuple-element.8.local_ref, f32[8,2,4096]{2,1,0:T(2,128)} %pad_maximum_fusion.2.carries_ref, ...), custom_call_target="tpu_custom_call" | custom-call | tf_op jit(solution)/shard_map/pallas_call | solution.py:290
  131.9 2.8 %copy.68 = f32[8,8,2,4096]{3,0,2,1:T(8,128)S(1)} copy(f32[8,8,2,4096]{3,1,2,0:T(8,128)} %bitcast.96) | data formatting | bytes 4194304 | tf_op jit(solution)/shard_map/transpose | solution.py:221
  134.7 0.0 copy-start.1
  134.7 2.5 %copy.70 = f32[8,16,4096]{2,1,0:T(8,128)} copy(f32[8,16,4096]{2,0,1:T(8,128)S(1)} %bitcast.84) | data formatting | bytes 4194304
  137.2 0.6 copy.67
  137.8 1.6 %copy.69 = bf16[8,16,4096]{2,1,0:T(8,128)(2,1)} copy(bf16[8,16,4096]{2,0,1:T(8,128)(2,1)S(1)} %bitcast.94) | data formatting | bytes 2097152
  (54 shorter events, 0.5 us)
Async XLA Ops:
  1.6 16.5 %collective-permute-start = (f32[8,1,8,128]{3,2,1,0:T(8,128)S(1)}, f32[8,1,8,128]{3,2,1,0:T(8,128)S(1)}, u32[]{:S(2)}, u32[]{:S(2)}) collective-permute-start(f32[8,1,8,128]{3,2,1,0:T(8,128)S(1)} %get-tuple-element.35), channel_id=1, source_target_pairs={{0,4},{4,8},{8,12},{12,16},{16,20},{20,24},{24,28},{28,32},{32,36}... | collective-permute-start | bytes 98312 | tf_op jit(solution)/shard_map/ppermute | solution.py:20
  6.2 12.1 %collective-permute-start.1 = (f32[8,1,8,128]{3,2,1,0:T(8,128)S(1)}, f32[8,1,8,128]{3,2,1,0:T(8,128)S(1)}, u32[]{:S(2)}, u32[]{:S(2)}) collective-permute-start(f32[8,1,8,128]{3,2,1,0:T(8,128)S(1)} %get-tuple-element.34), channel_id=1, source_target_pairs={{4,0},{8,4},{12,8},{16,12},{20,16},{24,20},{28,24},{32,28},{36,32}... | collective-permute-start | bytes 98312 | tf_op jit(solution)/shard_map/ppermute | solution.py:23
  11.3 6.9 %copy-start.2 = (s32[16,4096]{1,0:T(8,128)S(1)}, s32[16,4096]{1,0:T(8,128)}, u32[]{:S(2)}) copy-start(s32[16,4096]{1,0:T(8,128)} %param.13) | copy-start | bytes 786436
  11.3 6.9 %copy-start.3 = (f32[8,8,1024]{2,1,0:T(8,128)S(1)}, f32[8,8,1024]{2,1,0:T(8,128)}, u32[]{:S(2)}) copy-start(f32[8,8,1024]{2,1,0:T(8,128)} %param.7) | copy-start | bytes 786436
  11.3 11.6 %copy-start.5 = (bf16[2,4,2,4]{3,2,1,0:T(2,128)(2,1)S(1)}, bf16[2,4,2,4]{3,2,1,0:T(2,128)(2,1)}, u32[]{:S(2)}) copy-start(bf16[2,4,2,4]{3,2,1,0:T(2,128)(2,1)} %param.10) | copy-start | bytes 388
  17.0 6.5 %copy-start = (bf16[8,16,4096]{2,1,0:T(8,128)(2,1)S(1)}, bf16[8,16,4096]{2,1,0:T(8,128)(2,1)}, u32[]{:S(2)}) copy-start(bf16[8,16,4096]{2,1,0:T(8,128)(2,1)} %param.8) | copy-start | bytes 3145732
  18.2 7.4 %copy-start.4 = (f32[2,4,3,9]{3,1,2,0:T(4,128)S(1)}, f32[2,4,3,9]{3,1,2,0:T(4,128)}, u32[]{:S(2)}) copy-start(f32[2,4,3,9]{3,1,2,0:T(4,128)} %param.9) | copy-start | bytes 2596
  18.4 8.0 %collective-permute-start.2 = (f32[8,10,1,128]{3,2,1,0:T(1,128)S(1)}, f32[8,10,1,128]{3,2,1,0:T(1,128)S(1)}, u32[]{:S(2)}, u32[]{:S(2)}) collective-permute-start(f32[8,10,1,128]{3,2,1,0:T(1,128)S(1)} %get-tuple-element.30), channel_id=1, source_target_pairs={{0,1},{1,2},{2,3},{4,5},{5,6},{6,7},{8,9},{9,10},{10,11},{12,13},{... | collective-permute-start | bytes 122888 | tf_op jit(solution)/shard_map/ppermute | solution.py:20
  21.6 4.8 %collective-permute-start.3 = (f32[8,10,1,128]{3,2,1,0:T(1,128)S(1)}, f32[8,10,1,128]{3,2,1,0:T(1,128)S(1)}, u32[]{:S(2)}, u32[]{:S(2)}) collective-permute-start(f32[8,10,1,128]{3,2,1,0:T(1,128)S(1)} %get-tuple-element.31), channel_id=1, source_target_pairs={{1,0},{2,1},{3,2},{5,4},{6,5},{7,6},{9,8},{10,9},{11,10},{13,12},{... | collective-permute-start | bytes 122888 | tf_op jit(solution)/shard_map/ppermute | solution.py:23
  79.5 16.7 %all-to-all-start.1 = ((f32[8,1,1088]{2,1,0:T(1,128)}), f32[8,1,1088]{2,1,0:T(1,128)S(1)}, u32[]{:S(2)}, u32[]{:S(2)}) async-start(f32[8,1,1088]{2,1,0:T(1,128)} %reshape.490), calls=%async_computation.1 | async-start | bytes 73728 | tf_op jit(solution)/shard_map/all_to_all | solution.py:41
  98.7 10.1 %all-to-all-start.2 = ((f32[8,1,1024]{2,1,0:T(1,128)}), f32[8,1,1024]{2,1,0:T(1,128)S(1)}, u32[]{:S(2)}, u32[]{:S(2)}) async-start(f32[8,1,1024]{2,1,0:T(1,128)} %reshape.492), calls=%async_computation.2 | async-start | bytes 65536 | tf_op jit(solution)/shard_map/all_to_all | solution.py:45
  134.7 2.6 %copy-start.1 = (bf16[8,2,8,4096]{3,2,1,0:T(8,128)(2,1)S(1)}, bf16[8,2,8,4096]{3,2,1,0:T(8,128)(2,1)}, u32[]{:S(2)}) copy-start(bf16[8,2,8,4096]{3,2,1,0:T(8,128)(2,1)} %get-tuple-element.10) | copy-start | bytes 3145732

commit v5 on v3

--- a/solution.py
+++ b/solution.py
@@ -34,12 +34,13 @@
     block_totals = mine[:, :rows]
     block_partial = mine[:, rows : 2 * rows]
     block_weight = mine[:, 2 * rows :]
-    zero = jnp.zeros_like(block_totals[:1])
-    ahead = jnp.cumsum(block_totals, axis=0)
-    carry_in = jnp.concatenate([zero, ahead[:-1]], axis=0)
+    blocks, height, width = block_totals.shape
+    order = jnp.arange(blocks, dtype=jnp.int32)
+    earlier = (order[None, :] < order[:, None]).astype(jnp.float32)
+    flat = lambda values: values.reshape(blocks, -1)
+    carry_in = jnp.dot(earlier, flat(block_totals), precision=exact_mode).reshape(blocks, height, width)
     block_misfit = block_partial + block_weight * carry_in
-    behind = jnp.flip(jnp.cumsum(jnp.flip(block_misfit, 0), axis=0), 0)
-    carry_out = jnp.concatenate([behind[1:], zero], axis=0)
+    carry_out = jnp.dot(earlier.T, flat(block_misfit), precision=exact_mode).reshape(blocks, height, width)
     back = lax.all_to_all(jnp.concatenate([carry_in, carry_out], axis=1), axis, 0, 0, tiled=True)
     back = back.transpose(1, 0, 2).reshape(2 * rows, pixels)
     return back[:rows], back[rows:]
@@ -194,6 +195,11 @@
     return jnp.swapaxes(values, -2, -3).reshape(lead + (2 * shells, width))
 
 
+def tiles(values):
+    flat = values.reshape(-1)
+    return jnp.broadcast_to(flat[:, None, None], (flat.shape[0], 8, LANES))
+
+
 def local_forward(extended, halo_index, excitations, refine_weights, refine_sqrt, counts, stars, widths):
     samples, shells, _ = extended.shape
     slots, pixels = halo_index.shape
@@ -222,8 +228,8 @@
         forward_kernel,
         grid=(samples,),
         in_specs=[
-            smem,
-            smem,
+            whole((2 * 4 * 3 * slots, 8, LANES)),
+            whole((2 * 4 * 2 * 4, 8, LANES)),
             per_sample((1, blocks, 48, window)),
             whole((blocks, window, slots * BAND)),
             per_sample((1, 2, half, fine_pixels)),
@@ -244,8 +250,8 @@
         scratch_shapes=[pltpu.VMEM((16, slots * BAND), jnp.float32)],
         interpret=INTERPRET,
     )(
-        refine_weights.reshape(-1),
-        refine_sqrt.astype(jnp.float32).reshape(-1),
+        tiles(refine_weights),
+        tiles(refine_sqrt.astype(jnp.float32)),
         pieces,
         onehot,
         excite,

time: 139 us -> 131 us (0.942)
  other arithmetic: 17.7 us -> 11.2 us
  Pallas kernels: 40.5 us -> 35.3 us
  local copies, waits for them, and re-layouts: 22.4 us -> 24.3 us
    another operation x3 -> x1, other arithmetic: 6.63 us -> 0.24 us  [the longest x1 6.33 us: block_carries(): behind = jnp.flip(jnp.cumsum(jnp.flip(block_misfit, 0), axis=0), 0)]
    pallas_call x1, Pallas kernels: 32.3 us -> 27.1 us  [local_forward(): pl.pallas_call(forward_kernel, grid=(samples,), in_specs=[whole((2 * 4 *...]
    broadcast_in_dim x0 -> x3, local copies, waits for them, and re-layouts: none -> 2.15 us  [tiles(): return jnp.broadcast_to(flat[:, None, None], (flat.shape[0], 8, LANES))]
    unnamed x31 -> x33, local copies, waits for them, and re-layouts: 7.65 us -> 7.65 us
  transfers between devices with their start and end apart: 4 -> 4, of which waited for: 0 -> 1; matrix products, arithmetic and copies ran while one was open for 10% -> 10% of each run, Pallas kernels for 0% -> 0%
where the time goes in v5:
time: 131 us
  blocking collectives  45.7 us (35%)
  Pallas kernels  35.3 us (27%)
  local copies, waits for them, and re-layouts  24.3 us (19%)
  other arithmetic  11.2 us (9%)
  starting transfers between devices  10.9 us (8%)
    all_to_all x1, blocking collectives, block_carries(): mine = lax.all_to_all(packed, axis, 0, 0, tiled=True)  27.9 us
    pallas_call x1, Pallas kernels, local_forward(): pl.pallas_call(forward_kernel, grid=(samples,), in_specs=[whole((2 * 4 *...  27.1 us
    all_to_all x1, blocking collectives, block_carries(): lax.all_to_all(jnp.concatenate([carry_in, carry_out], axis=1), axis, 0, 0...  17.8 us
    pallas_call x1, Pallas kernels, local_backward(): pl.pallas_call(backward_kernel, grid=(samples,), in_specs=[smem, per_samp...  8.17 us
    ppermute x2, starting transfers between devices, with_halo(): lax.ppermute(lax.slice_in_dim(block, block.shape[dim] - width, None, axis...  7.7 us
    unnamed x33, local copies, waits for them, and re-layouts  7.65 us
    convert_element_type x1, other arithmetic, local_forward(): onehot = (local.transpose(1, 0, 2)[:, None] == spots).astype(jnp.bfloat16)  5.74 us
    transpose x2, local copies, waits for them, and re-layouts, from_parity(): return jnp.swapaxes(values, -2, -3).reshape(lead + (2 * shells, width))  3.39 us
  transfers between devices with their start and end apart: 4, of which 1 were waited for; matrix products, arithmetic and copies ran while one was open for 10% of the time, Pallas kernels for 0%

profile of v5, /device:TPU:1, one launch (start us, length us, event | category | flops | bytes accessed | tf_op | source)
XLA Modules:
  0.0 130.6 jit_solution(16311187919317318733)
XLA Ops:
  0.6 1.0 copy.86
  1.6 4.5 %collective-permute-start = (f32[8,1,8,128]{3,2,1,0:T(8,128)S(1)}, f32[8,1,8,128]{3,2,1,0:T(8,128)S(1)}, u32[]{:S(2)}, u32[]{:S(2)}) collective-permute-start(f32[8,1,8,128]{3,2,1,0:T(8,128)S(1)} %get-tuple-element.30), channel_id=1, source_target_pairs={{0,4},{4,8},{8,12},{12,16},{16,20},{20,24},{24,28},{28,32},{32,36}... | collective-permute-start | bytes 98312 | tf_op jit(solution)/shard_map/ppermute | solution.py:19
  6.2 1.9 %collective-permute-start.1 = (f32[8,1,8,128]{3,2,1,0:T(8,128)S(1)}, f32[8,1,8,128]{3,2,1,0:T(8,128)S(1)}, u32[]{:S(2)}, u32[]{:S(2)}) collective-permute-start(f32[8,1,8,128]{3,2,1,0:T(8,128)S(1)} %get-tuple-element.29), channel_id=1, source_target_pairs={{4,0},{8,4},{12,8},{16,12},{20,16},{24,20},{28,24},{32,28},{36,32}... | collective-permute-start | bytes 98312 | tf_op jit(solution)/shard_map/ppermute | solution.py:22
  8.1 1.0 convert_element_type.19
  9.1 0.2 reshape.476
  9.2 1.1 reshape.477
  10.4 0.9 copy.75
  11.2 0.1 fusion.16
  11.3 5.7 %fusion.onehot_ref = bf16[8,384,1152]{2,1,0:T(8,128)(2,1)} fusion(s32[8,1152]{1,0:T(8,128)S(1)} %fusion.16), kind=kLoop, calls=%fused_computation.1 | loop fusion | flops 7077888 | bytes 7114752 | tf_op jit(solution)/shard_map/convert_element_type | solution.py:219
  17.0 1.1 copy_bitcast_fusion.3
  18.2 0.0 copy-start.4
  18.3 0.1 constant_dynamic-update-slice_fusion.1
  18.3 0.1 fusion.25
  18.4 3.2 %collective-permute-start.2 = (f32[8,10,1,128]{3,2,1,0:T(1,128)S(1)}, f32[8,10,1,128]{3,2,1,0:T(1,128)S(1)}, u32[]{:S(2)}, u32[]{:S(2)}) collective-permute-start(f32[8,10,1,128]{3,2,1,0:T(1,128)S(1)} %get-tuple-element.27), channel_id=1, source_target_pairs={{0,1},{1,2},{2,3},{4,5},{5,6},{6,7},{8,9},{9,10},{10,11},{12,13},{... | collective-permute-start | bytes 122888 | tf_op jit(solution)/shard_map/ppermute | solution.py:19
  21.6 1.3 collective-permute-start.3
  22.9 0.1 reshape.483.sqrt_ref
  23.0 0.6 copy.52
  23.6 1.6 %copy.84 = bf16[8,8,2,4096]{3,1,2,0:T(8,128)(2,1)} copy(bf16[8,8,2,4096]{3,0,2,1:T(8,128)(2,1)S(1)} %bitcast.95) | data formatting | bytes 2097152 | tf_op jit(solution)/shard_map/reshape | solution.py:188
  25.2 0.1 broadcast_in_dim.8
  25.3 0.1 concatenate.47
  25.4 0.9 collective-permute-done.3
  26.4 0.1 pad_maximum_fusion
  26.5 0.2 copy.85
  26.9 0.2 reduce-precision_convert_fusion.1
  27.1 0.4 fusion.6
  27.5 1.8 %copy.51 = bf16[8,8,3,16,384]{4,3,2,1,0:T(8,128)(2,1)} copy(bf16[8,8,3,16,384]{4,0,3,1,2:T(8,128)(2,1)S(1)} %fusion.6) | data formatting | bytes 4718592 | tf_op jit(solution)/shard_map/transpose | solution.py:215
  29.3 0.8 broadcast_in_dim.10.sqrt_ref
  30.1 1.2 broadcast_in_dim.9.weights_ref
  31.3 0.7 broadcast_in_dim.11.widths_ref
  32.0 27.1 %shard_map.86 = (f32[8,2,8,4096]{3,2,1,0:T(8,128)}, f32[8,2,8,4096]{3,2,1,0:T(8,128)}, f32[8,2,4096]{2,1,0:T(2,128)}) custom-call(f32[216,8,128]{2,1,0:T(8,128)} %broadcast_in_dim.9.weights_ref, f32[64,8,128]{2,1,0:T(8,128)} %broadcast_in_dim.10.sqrt_ref, bf16[8,8,48,384]{3,2,1,0:T(8,128)(2,1)} %bitcast.84, bf16[8,384,1152]{2,1,0:T(8,128)(2,1)} %fusion.onehot_ref, ...), custom_call_target="tpu_custom_call" | custom-call | tf_op jit(solution)/shard_map/pallas_call | solution.py:227
  59.1 1.7 %slice_reduce_fusion.1 = (f32[8,4096]{1,0:T(8,128)S(1)}, f32[8,4096]{1,0:T(8,128)S(1)}) fusion(f32[8,2,4096]{2,1,0:T(2,128)} %get-tuple-element.9), kind=kLoop, calls=%fused_computation.25 | loop fusion | bytes 524288 | tf_op jit(solution)/shard_map/slice | solution.py:313
  60.8 0.1 concatenate.45
  60.9 0.2 copy.56
  61.1 0.1 concatenate.46
  61.2 0.2 copy.57
  61.4 0.1 maximum_bitcast_fusion
  61.4 0.4 reshape.488
  61.8 27.9 %all_to_all.10 = f32[64,1,1088]{2,1,0:T(1,128)S(1)} all-to-all(f32[64,1,1088]{2,1,0:T(1,128)S(1)} %reshape.488), channel_id=1, replica_groups=mesh['dist'=64,'sky'=4] {'dist'}, dimensions={0} | all-to-all | bytes 557056 | tf_op jit(solution)/shard_map/all_to_all | solution.py:33
  89.7 0.5 broadcast.53
  90.3 1.3 %reduce.4 = f32[64,1088]{1,0:T(8,128)S(1)} reduce(f32[64,1,1088]{2,1,0:T(1,128)S(1)} %all_to_all.10, f32[]{:T(128)} %broadcast.53), dimensions={1}, to_apply=%all_to_all.6.reduce_sub_computation | reduce | bytes 557060 | tf_op jit(solution)/shard_map/all_to_all | solution.py:33
  91.6 0.1 reshape.489
  91.8 0.1 reshape.478
  91.9 0.1 copy.58
  92.1 0.5 copy_add_fusion
  92.6 0.2 copy.61
  92.8 0.1 reshape.479
  92.9 0.1 copy.72
  93.0 0.5 fusion.18
  93.5 0.1 pad_maximum_fusion.1
  93.6 0.3 copy.63
  93.9 0.3 reshape.490
  94.2 17.8 %all_to_all.11 = f32[64,1,1024]{2,1,0:T(1,128)S(1)} all-to-all(f32[64,1,1024]{2,1,0:T(1,128)S(1)} %reshape.490), channel_id=1, replica_groups=mesh['dist'=64,'sky'=4] {'dist'}, dimensions={0} | all-to-all | bytes 524288 | tf_op jit(solution)/shard_map/all_to_all | solution.py:44
  112.0 1.3 reduce.5
  113.3 0.1 reshape.491
  113.5 0.1 copy.64
  113.5 0.2 stack.53
  113.7 0.1 copy.65
  113.8 0.2 stack.54
  114.0 0.9 pad_maximum_fusion.2.carries_ref
  114.9 8.2 %shard_map.87 = (bf16[8,2,8,4096]{3,2,1,0:T(8,128)(2,1)}, f32[8,2,8,4096]{3,2,1,0:T(8,128)}) custom-call(f32[64]{0:T(128)} %copy-done.5, f32[8,2,8,4096]{3,2,1,0:T(8,128)} %get-tuple-element.7.density_ref, f32[8,2,8,4096]{3,2,1,0:T(8,128)} %get-tuple-element.8.local_ref, f32[8,2,4096]{2,1,0:T(2,128)} %pad_maximum_fusion.2.carries_ref, ...), custom_call_target="tpu_custom_call" | custom-call | tf_op jit(solution)/shard_map/pallas_call | solution.py:269
  123.1 2.8 %copy.67 = f32[8,8,2,4096]{3,0,2,1:T(8,128)S(1)} copy(f32[8,8,2,4096]{3,1,2,0:T(8,128)} %bitcast.97) | data formatting | bytes 4194304 | tf_op jit(solution)/shard_map/transpose | solution.py:195
  125.9 2.5 %copy.69 = f32[8,16,4096]{2,1,0:T(8,128)} copy(f32[8,16,4096]{2,0,1:T(8,128)S(1)} %bitcast.85) | data formatting | bytes 4194304
  128.5 0.6 copy.66
  129.0 1.6 %copy.68 = bf16[8,16,4096]{2,1,0:T(8,128)(2,1)} copy(bf16[8,16,4096]{2,0,1:T(8,128)(2,1)S(1)} %bitcast.94) | data formatting | bytes 2097152
  (34 shorter events, 0.3 us)
Async XLA Ops:
  1.6 16.6 %collective-permute-start = (f32[8,1,8,128]{3,2,1,0:T(8,128)S(1)}, f32[8,1,8,128]{3,2,1,0:T(8,128)S(1)}, u32[]{:S(2)}, u32[]{:S(2)}) collective-permute-start(f32[8,1,8,128]{3,2,1,0:T(8,128)S(1)} %get-tuple-element.30), channel_id=1, source_target_pairs={{0,4},{4,8},{8,12},{12,16},{16,20},{20,24},{24,28},{28,32},{32,36}... | collective-permute-start | bytes 98312 | tf_op jit(solution)/shard_map/ppermute | solution.py:19
  6.2 12.2 %collective-permute-start.1 = (f32[8,1,8,128]{3,2,1,0:T(8,128)S(1)}, f32[8,1,8,128]{3,2,1,0:T(8,128)S(1)}, u32[]{:S(2)}, u32[]{:S(2)}) collective-permute-start(f32[8,1,8,128]{3,2,1,0:T(8,128)S(1)} %get-tuple-element.29), channel_id=1, source_target_pairs={{4,0},{8,4},{12,8},{16,12},{20,16},{24,20},{28,24},{32,28},{36,32}... | collective-permute-start | bytes 98312 | tf_op jit(solution)/shard_map/ppermute | solution.py:22
  11.3 6.9 %copy-start.2 = (s32[16,4096]{1,0:T(8,128)S(1)}, s32[16,4096]{1,0:T(8,128)}, u32[]{:S(2)}) copy-start(s32[16,4096]{1,0:T(8,128)} %param.13) | copy-start | bytes 786436
  11.3 7.0 %copy-start.3 = (f32[8,8,1024]{2,1,0:T(8,128)S(1)}, f32[8,8,1024]{2,1,0:T(8,128)}, u32[]{:S(2)}) copy-start(f32[8,8,1024]{2,1,0:T(8,128)} %param.7) | copy-start | bytes 786436
  11.3 11.6 %copy-start.6 = (bf16[2,4,2,4]{3,2,1,0:T(2,128)(2,1)S(1)}, bf16[2,4,2,4]{3,2,1,0:T(2,128)(2,1)}, u32[]{:S(2)}) copy-start(bf16[2,4,2,4]{3,2,1,0:T(2,128)(2,1)} %param.10) | copy-start | bytes 388
  17.0 6.0 %copy-start = (bf16[8,16,4096]{2,1,0:T(8,128)(2,1)S(1)}, bf16[8,16,4096]{2,1,0:T(8,128)(2,1)}, u32[]{:S(2)}) copy-start(bf16[8,16,4096]{2,1,0:T(8,128)(2,1)} %param.8) | copy-start | bytes 3145732
  18.2 6.9 %copy-start.4 = (f32[2,4,3,9]{3,1,2,0:T(4,128)S(1)}, f32[2,4,3,9]{3,1,2,0:T(4,128)}, u32[]{:S(2)}) copy-start(f32[2,4,3,9]{3,1,2,0:T(4,128)} %param.9) | copy-start | bytes 2596
  18.4 7.0 %collective-permute-start.2 = (f32[8,10,1,128]{3,2,1,0:T(1,128)S(1)}, f32[8,10,1,128]{3,2,1,0:T(1,128)S(1)}, u32[]{:S(2)}, u32[]{:S(2)}) collective-permute-start(f32[8,10,1,128]{3,2,1,0:T(1,128)S(1)} %get-tuple-element.27), channel_id=1, source_target_pairs={{0,1},{1,2},{2,3},{4,5},{5,6},{6,7},{8,9},{9,10},{10,11},{12,13},{... | collective-permute-start | bytes 122888 | tf_op jit(solution)/shard_map/ppermute | solution.py:19
  21.6 4.7 %collective-permute-start.3 = (f32[8,10,1,128]{3,2,1,0:T(1,128)S(1)}, f32[8,10,1,128]{3,2,1,0:T(1,128)S(1)}, u32[]{:S(2)}, u32[]{:S(2)}) collective-permute-start(f32[8,10,1,128]{3,2,1,0:T(1,128)S(1)} %get-tuple-element.28), channel_id=1, source_target_pairs={{1,0},{2,1},{3,2},{5,4},{6,5},{7,6},{9,8},{10,9},{11,10},{13,12},{... | collective-permute-start | bytes 122888 | tf_op jit(solution)/shard_map/ppermute | solution.py:22
  23.0 6.3 %copy-start.5 = (f32[64]{0:T(128)}, f32[64]{0:T(128)S(1)}, u32[]{:S(2)}) copy-start(f32[64]{0:T(128)S(1)} %reshape.483.sqrt_ref) | copy-start | bytes 772
  125.9 2.6 %copy-start.1 = (bf16[8,2,8,4096]{3,2,1,0:T(8,128)(2,1)S(1)}, bf16[8,2,8,4096]{3,2,1,0:T(8,128)(2,1)}, u32[]{:S(2)}) copy-start(bf16[8,2,8,4096]{3,2,1,0:T(8,128)(2,1)} %get-tuple-element.10) | copy-start | bytes 3145732

commit v6 on v5

--- a/solution.py
+++ b/solution.py
@@ -11,17 +11,32 @@
 exact_mode = lax.Precision.HIGHEST
 
 
-def with_halo(block, sides, width):
-    for axis, dim in sides:
-        count = lax.axis_size(axis)
-        forward = [(i, i + 1) for i in range(count - 1)]
-        backward = [(target, source) for source, target in forward]
-        low = lax.ppermute(
-            lax.slice_in_dim(block, block.shape[dim] - width, None, axis=dim), axis, forward
-        )
-        high = lax.ppermute(lax.slice_in_dim(block, 0, width, axis=dim), axis, backward)
-        block = jnp.concatenate([low, block, high], axis=dim)
-    return block
+def with_halo(block, band):
+    dist = lax.axis_size("dist")
+    sky = lax.axis_size("sky")
+
+    def moved(piece, step_dist, step_sky):
+        pairs = []
+        for d in range(dist):
+            for s in range(sky):
+                if 0 <= d + step_dist < dist and 0 <= s + step_sky < sky:
+                    pairs.append((d * sky + s, (d + step_dist) * sky + s + step_sky))
+        return lax.ppermute(piece, ("dist", "sky"), pairs)
+
+    last_row = block[:, -1:]
+    first_row = block[:, :1]
+    rows_low = moved(last_row, 1, 0)
+    rows_high = moved(first_row, -1, 0)
+    left = moved(block[:, :, -band:], 0, 1)
+    right = moved(block[:, :, :band], 0, -1)
+    corner_ll = moved(last_row[:, :, -band:], 1, 1)
+    corner_lh = moved(last_row[:, :, :band], 1, -1)
+    corner_hl = moved(first_row[:, :, -band:], -1, 1)
+    corner_hh = moved(first_row[:, :, :band], -1, -1)
+    low = jnp.concatenate([corner_ll, rows_low, corner_lh], axis=2)
+    middle = jnp.concatenate([left, block, right], axis=2)
+    high = jnp.concatenate([corner_hl, rows_high, corner_hh], axis=2)
+    return jnp.concatenate([low, middle, high], axis=1)
 
 
 def block_carries(totals, partial, weight, axis):
@@ -299,9 +314,7 @@
     dist_count = lax.axis_size("dist")
     dist_rank = lax.axis_index("dist")
     all_shells = fine_shells * dist_count
-    blocked = coarse_field.reshape(samples, coarse_shells, coarse_pixels // BAND, BAND)
-    extended = with_halo(blocked, (("dist", 1), ("sky", 2)), 1)
-    extended = extended.reshape(samples, coarse_shells + 2, coarse_pixels + 2 * BAND)
+    extended = with_halo(coarse_field, BAND)
     shells = dist_rank * fine_shells + jnp.arange(fine_shells, dtype=jnp.int32)
     middle = (shells.astype(jnp.float32) + 0.5) / all_shells
     widths = 3.0 * jnp.exp(3.0 * middle - 3.0) / all_shells

time: 131 us -> 148 us (1.13)
  starting transfers between devices: 10.9 us -> 21.3 us
  blocking collectives: 45.7 us -> 48.4 us
  waiting for transfers between devices: 0.95 us -> 3.21 us
    ppermute x4 -> x8, starting transfers between devices: 10.9 us -> 21.3 us  [moved(): return lax.ppermute(piece, ('dist', 'sky'), pairs)]
    slice x2 -> x3, local copies, waits for them, and re-layouts: 0.06 us -> 2.74 us  [the longest x1 1.08 us: with_halo(): last_row = block[:, -1:]]
    all_to_all x1, blocking collectives: 27.9 us -> 30.5 us  [block_carries(): mine = lax.all_to_all(packed, axis, 0, 0, tiled=True)]
    ppermute x4 -> x8, waiting for transfers between devices: 0.95 us -> 3.21 us  [moved(): return lax.ppermute(piece, ('dist', 'sky'), pairs)]
    unnamed x33 -> x34, local copies, waits for them, and re-layouts: 7.65 us -> 5.81 us
  transfers between devices with their start and end apart: 4 -> 8, of which waited for: 1 -> 1; matrix products, arithmetic and copies ran while one was open for 10% -> 9% of each run, Pallas kernels for 0% -> 0%
where the time goes in v6:
time: 148 us; the launch traced here: 147 us
  blocking collectives  48.4 us (33%)
  Pallas kernels  35.3 us (24%)
  local copies, waits for them, and re-layouts  24 us (16%)
  starting transfers between devices  21.3 us (14%)
  other arithmetic  12.6 us (9%)
  waiting for transfers between devices  3.21 us (2%)
    all_to_all x1, blocking collectives, block_carries(): mine = lax.all_to_all(packed, axis, 0, 0, tiled=True)  30.5 us
    pallas_call x1, Pallas kernels, local_forward(): pl.pallas_call(forward_kernel, grid=(samples,), in_specs=[whole((2 * 4 *...  27.1 us
    ppermute x8, starting transfers between devices, moved(): return lax.ppermute(piece, ('dist', 'sky'), pairs)  21.3 us
    all_to_all x1, blocking collectives, block_carries(): lax.all_to_all(jnp.concatenate([carry_in, carry_out], axis=1), axis, 0, 0...  17.8 us
    pallas_call x1, Pallas kernels, local_backward(): pl.pallas_call(backward_kernel, grid=(samples,), in_specs=[smem, per_samp...  8.21 us
    unnamed x34, local copies, waits for them, and re-layouts  5.81 us
    convert_element_type x1, other arithmetic, local_forward(): onehot = (local.transpose(1, 0, 2)[:, None] == spots).astype(jnp.bfloat16)  5.73 us
    transpose x2, local copies, waits for them, and re-layouts, from_parity(): return jnp.swapaxes(values, -2, -3).reshape(lead + (2 * shells, width))  3.39 us
  transfers between devices with their start and end apart: 8, of which 1 were waited for; matrix products, arithmetic and copies ran while one was open for 9% of the time, Pallas kernels for 0%

profile of v6, /device:TPU:1, one launch (start us, length us, event | category | flops | bytes accessed | tf_op | source)
XLA Modules:
  0.0 147.0 jit_solution(11832480371927899403)
XLA Ops:
  0.6 0.9 fusion.25
  1.5 5.5 %collective-permute-start = (f32[8,1,128]{2,0,1:T(8,128)S(1)}, f32[8,1,128]{2,0,1:T(8,128)S(1)}, u32[]{:S(2)}, u32[]{:S(2)}) collective-permute-start(f32[8,1,128]{2,0,1:T(8,128)S(1)} %bitcast.95), channel_id=1, source_target_pairs={{0,5},{1,6},{2,7},{4,9},{5,10},{6,11},{8,13},{9,14},{10,15},{12,17... | collective-permute-start | bytes 12296 | tf_op jit(solution)/shard_map/ppermute | solution.py:24
  7.0 1.3 collective-permute-start.2
  8.3 1.1 fusion.26
  9.4 1.9 %collective-permute-start.1 = (f32[8,1,1024]{2,0,1:T(8,128)S(1)}, f32[8,1,1024]{2,0,1:T(8,128)S(1)}, u32[]{:S(2)}, u32[]{:S(2)}) collective-permute-start(f32[8,1,1024]{2,0,1:T(8,128)S(1)} %copy.58), channel_id=1, source_target_pairs={{0,4},{1,5},{2,6},{3,7},{4,8},{5,9},{6,10},{7,11},{8,12},{9,13},{1... | collective-permute-start | bytes 98312 | tf_op jit(solution)/shard_map/ppermute | solution.py:24
  11.4 4.2 %collective-permute-start.5 = (f32[8,1,128]{2,0,1:T(8,128)S(1)}, f32[8,1,128]{2,0,1:T(8,128)S(1)}, u32[]{:S(2)}, u32[]{:S(2)}) collective-permute-start(f32[8,1,128]{2,0,1:T(8,128)S(1)} %bitcast.93), channel_id=1, source_target_pairs={{4,1},{5,2},{6,3},{8,5},{9,6},{10,7},{12,9},{13,10},{14,11},{16,13... | collective-permute-start | bytes 12296 | tf_op jit(solution)/shard_map/ppermute | solution.py:24
  15.6 1.3 collective-permute-start.7
  16.9 0.8 fusion.27
  17.7 1.0 convert_element_type.19
  18.7 1.0 convert_reduce_fusion
  19.7 0.2 reshape.468
  19.8 0.2 reshape.469
  20.0 0.1 fusion.16
  20.1 5.7 %fusion.onehot_ref = bf16[8,384,1152]{2,1,0:T(8,128)(2,1)} fusion(s32[8,1152]{1,0:T(8,128)S(1)} %fusion.16), kind=kLoop, calls=%fused_computation.1 | loop fusion | flops 7077888 | bytes 7114752 | tf_op jit(solution)/shard_map/convert_element_type | solution.py:234
  25.8 1.1 copy_bitcast_fusion.1
  27.0 0.1 reshape.475.sqrt_ref
  27.1 0.6 copy.36
  27.7 1.6 %copy.69 = bf16[8,8,2,4096]{3,1,2,0:T(8,128)(2,1)} copy(bf16[8,8,2,4096]{3,0,2,1:T(8,128)(2,1)S(1)} %bitcast.80) | data formatting | bytes 2097152 | tf_op jit(solution)/shard_map/reshape | solution.py:203
  29.3 0.1 broadcast_in_dim.8
  29.4 0.1 concatenate.55
  29.5 1.9 %collective-permute-start.6 = (f32[8,1,1024]{2,0,1:T(8,128)S(1)}, f32[8,1,1024]{2,0,1:T(8,128)S(1)}, u32[]{:S(2)}, u32[]{:S(2)}) collective-permute-start(f32[8,1,1024]{2,0,1:T(8,128)S(1)} %copy.61), channel_id=1, source_target_pairs={{4,0},{5,1},{6,2},{7,3},{8,4},{9,5},{10,6},{11,7},{12,8},{13,9},{1... | collective-permute-start | bytes 98312 | tf_op jit(solution)/shard_map/ppermute | solution.py:24
  31.4 3.8 %collective-permute-start.3 = (f32[8,8,128]{2,1,0:T(8,128)S(1)}, f32[8,8,128]{2,1,0:T(8,128)S(1)}, u32[]{:S(2)}, u32[]{:S(2)}) collective-permute-start(f32[8,8,128]{2,1,0:T(8,128)S(1)} %get-tuple-element.31), channel_id=1, source_target_pairs={{0,1},{1,2},{2,3},{4,5},{5,6},{6,7},{8,9},{9,10},{10,11},{12,13},{... | collective-permute-start | bytes 98312 | tf_op jit(solution)/shard_map/ppermute | solution.py:24
  35.2 1.3 collective-permute-start.4
  36.7 3.2 %collective-permute-done.4 = f32[8,8,128]{2,1,0:T(8,128)S(1)} collective-permute-done((f32[8,8,128]{2,1,0:T(8,128)S(1)}, f32[8,8,128]{2,1,0:T(8,128)S(1)}, u32[]{:S(2)}, u32[]{:S(2)}) %collective-permute-start.4) | collective-permute-done | bytes 32800 | tf_op jit(solution)/shard_map/ppermute | solution.py:24
  39.9 0.1 pad_maximum_fusion
  40.2 0.5 reduce-precision_convert_fusion.1
  40.7 0.6 fusion.6
  41.3 1.7 %copy.35 = bf16[8,8,3,16,384]{4,3,2,1,0:T(8,128)(2,1)} copy(bf16[8,8,3,16,384]{4,3,0,1,2:T(8,128)(2,1)S(1)} %fusion.6) | data formatting | bytes 4718592 | tf_op jit(solution)/shard_map/transpose | solution.py:230
  43.0 0.9 broadcast_in_dim.10.sqrt_ref
  43.9 1.2 broadcast_in_dim.9.weights_ref
  45.1 0.7 broadcast_in_dim.11.widths_ref
  45.8 27.1 %shard_map.86 = (f32[8,2,8,4096]{3,2,1,0:T(8,128)}, f32[8,2,8,4096]{3,2,1,0:T(8,128)}, f32[8,2,4096]{2,1,0:T(2,128)}) custom-call(f32[216,8,128]{2,1,0:T(8,128)} %broadcast_in_dim.9.weights_ref, f32[64,8,128]{2,1,0:T(8,128)} %broadcast_in_dim.10.sqrt_ref, bf16[8,8,48,384]{3,2,1,0:T(8,128)(2,1)} %bitcast.77, bf16[8,384,1152]{2,1,0:T(8,128)(2,1)} %fusion.onehot_ref, ...), custom_call_target="tpu_custom_call" | custom-call | tf_op jit(solution)/shard_map/pallas_call | solution.py:242
  72.9 1.7 %slice_reduce_fusion.1 = (f32[8,4096]{1,0:T(8,128)S(1)}, f32[8,4096]{1,0:T(8,128)S(1)}) fusion(f32[8,2,4096]{2,1,0:T(2,128)} %get-tuple-element.9), kind=kLoop, calls=%fused_computation.39 | loop fusion | bytes 524288 | tf_op jit(solution)/shard_map/slice | solution.py:326
  74.6 0.1 concatenate.53
  74.7 0.2 copy.40
  74.9 0.1 concatenate.54
  75.0 0.2 copy.41
  75.2 0.1 maximum_bitcast_fusion
  75.2 0.4 reshape.480
  75.6 30.5 %all_to_all.10 = f32[64,1,1088]{2,1,0:T(1,128)S(1)} all-to-all(f32[64,1,1088]{2,1,0:T(1,128)S(1)} %reshape.480), channel_id=1, replica_groups=mesh['dist'=64,'sky'=4] {'dist'}, dimensions={0} | all-to-all | bytes 557056 | tf_op jit(solution)/shard_map/all_to_all | solution.py:48
  106.1 0.5 broadcast.53
  106.7 1.3 reduce.4
  108.0 0.1 reshape.481
  108.2 0.1 reshape.470
  108.3 0.1 copy.42
  108.5 0.5 copy_add_fusion
  109.0 0.2 copy.45
  109.2 0.1 reshape.471
  109.3 0.1 copy.56
  109.4 0.5 fusion.18
  109.9 0.1 pad_maximum_fusion.1
  110.0 0.3 copy.47
  110.3 0.3 reshape.482
  110.6 17.8 %all_to_all.11 = f32[64,1,1024]{2,1,0:T(1,128)S(1)} all-to-all(f32[64,1,1024]{2,1,0:T(1,128)S(1)} %reshape.482), channel_id=1, replica_groups=mesh['dist'=64,'sky'=4] {'dist'}, dimensions={0} | all-to-all | bytes 524288 | tf_op jit(solution)/shard_map/all_to_all | solution.py:59
  128.4 1.3 reduce.5
  129.7 0.1 reshape.483
  129.9 0.2 stack.53
  130.2 0.2 stack.54
  130.4 0.9 pad_maximum_fusion.2.carries_ref
  131.3 8.2 %shard_map.87 = (bf16[8,2,8,4096]{3,2,1,0:T(8,128)(2,1)}, f32[8,2,8,4096]{3,2,1,0:T(8,128)}) custom-call(f32[64]{0:T(128)} %copy-done.6, f32[8,2,8,4096]{3,2,1,0:T(8,128)} %get-tuple-element.7.density_ref, f32[8,2,8,4096]{3,2,1,0:T(8,128)} %get-tuple-element.8.local_ref, f32[8,2,4096]{2,1,0:T(2,128)} %pad_maximum_fusion.2.carries_ref, ...), custom_call_target="tpu_custom_call" | custom-call | tf_op jit(solution)/shard_map/pallas_call | solution.py:284
  139.5 2.8 %copy.51 = f32[8,8,2,4096]{3,0,2,1:T(8,128)S(1)} copy(f32[8,8,2,4096]{3,1,2,0:T(8,128)} %bitcast.82) | data formatting | bytes 4194304 | tf_op jit(solution)/shard_map/transpose | solution.py:210
  142.3 2.5 %copy.53 = f32[8,16,4096]{2,1,0:T(8,128)} copy(f32[8,16,4096]{2,0,1:T(8,128)S(1)} %bitcast.78) | data formatting | bytes 4194304
  144.9 0.6 copy.50
  145.5 1.6 %copy.52 = bf16[8,16,4096]{2,1,0:T(8,128)(2,1)} copy(bf16[8,16,4096]{2,0,1:T(8,128)(2,1)S(1)} %bitcast.79) | data formatting | bytes 2097152
  (46 shorter events, 0.5 us)
Async XLA Ops:
  0.6 19.2 %copy-start.3 = (f32[16,4096]{1,0:T(8,128)S(1)}, f32[16,4096]{1,0:T(8,128)}, u32[]{:S(2)}) copy-start(f32[16,4096]{1,0:T(8,128)} %param.12) | copy-start | bytes 786436
  0.6 19.3 %copy-start.4 = (s32[9,1024]{1,0:T(8,128)S(1)}, s32[9,1024]{1,0:T(8,128)}, u32[]{:S(2)}) copy-start(s32[9,1024]{1,0:T(8,128)} %param.11) | copy-start | bytes 110596
  1.5 28.0 %collective-permute-start = (f32[8,1,128]{2,0,1:T(8,128)S(1)}, f32[8,1,128]{2,0,1:T(8,128)S(1)}, u32[]{:S(2)}, u32[]{:S(2)}) collective-permute-start(f32[8,1,128]{2,0,1:T(8,128)S(1)} %bitcast.95), channel_id=1, source_target_pairs={{0,5},{1,6},{2,7},{4,9},{5,10},{6,11},{8,13},{9,14},{10,15},{12,17... | collective-permute-start | bytes 12296 | tf_op jit(solution)/shard_map/ppermute | solution.py:24
  7.0 24.4 %collective-permute-start.2 = (f32[8,1,128]{2,0,1:T(8,128)S(1)}, f32[8,1,128]{2,0,1:T(8,128)S(1)}, u32[]{:S(2)}, u32[]{:S(2)}) collective-permute-start(f32[8,1,128]{2,0,1:T(8,128)S(1)} %bitcast.94), channel_id=1, source_target_pairs={{1,4},{2,5},{3,6},{5,8},{6,9},{7,10},{9,12},{10,13},{11,14},{13,16... | collective-permute-start | bytes 12296 | tf_op jit(solution)/shard_map/ppermute | solution.py:24
  9.4 25.8 %collective-permute-start.1 = (f32[8,1,1024]{2,0,1:T(8,128)S(1)}, f32[8,1,1024]{2,0,1:T(8,128)S(1)}, u32[]{:S(2)}, u32[]{:S(2)}) collective-permute-start(f32[8,1,1024]{2,0,1:T(8,128)S(1)} %copy.58), channel_id=1, source_target_pairs={{0,4},{1,5},{2,6},{3,7},{4,8},{5,9},{6,10},{7,11},{8,12},{9,13},{1... | collective-permute-start | bytes 98312 | tf_op jit(solution)/shard_map/ppermute | solution.py:24
  11.4 25.2 %collective-permute-start.5 = (f32[8,1,128]{2,0,1:T(8,128)S(1)}, f32[8,1,128]{2,0,1:T(8,128)S(1)}, u32[]{:S(2)}, u32[]{:S(2)}) collective-permute-start(f32[8,1,128]{2,0,1:T(8,128)S(1)} %bitcast.93), channel_id=1, source_target_pairs={{4,1},{5,2},{6,3},{8,5},{9,6},{10,7},{12,9},{13,10},{14,11},{16,13... | collective-permute-start | bytes 12296 | tf_op jit(solution)/shard_map/ppermute | solution.py:24
  15.6 21.0 %collective-permute-start.7 = (f32[8,1,128]{2,0,1:T(8,128)S(1)}, f32[8,1,128]{2,0,1:T(8,128)S(1)}, u32[]{:S(2)}, u32[]{:S(2)}) collective-permute-start(f32[8,1,128]{2,0,1:T(8,128)S(1)} %bitcast.92), channel_id=1, source_target_pairs={{5,0},{6,1},{7,2},{9,4},{10,5},{11,6},{13,8},{14,9},{15,10},{17,12... | collective-permute-start | bytes 12296 | tf_op jit(solution)/shard_map/ppermute | solution.py:24
  20.1 6.9 %copy-start.7 = (bf16[2,4,2,4]{3,2,1,0:T(2,128)(2,1)S(1)}, bf16[2,4,2,4]{3,2,1,0:T(2,128)(2,1)}, u32[]{:S(2)}) copy-start(bf16[2,4,2,4]{3,2,1,0:T(2,128)(2,1)} %param.10) | copy-start | bytes 388
  25.8 1.3 copy-start
  27.1 16.0 %copy-start.6 = (f32[64]{0:T(128)}, f32[64]{0:T(128)S(1)}, u32[]{:S(2)}) copy-start(f32[64]{0:T(128)S(1)} %reshape.475.sqrt_ref) | copy-start | bytes 772
  27.7 1.6 %copy-start.5 = (f32[2,4,3,9]{3,1,2,0:T(4,128)S(1)}, f32[2,4,3,9]{3,1,2,0:T(4,128)}, u32[]{:S(2)}) copy-start(f32[2,4,3,9]{3,1,2,0:T(4,128)} %param.9) | copy-start | bytes 2596
  27.7 12.2 %copy-start.2 = (f32[8,8,1024]{2,1,0:T(8,128)S(1)}, f32[8,8,1024]{2,1,0:T(8,128)}, u32[]{:S(2)}) copy-start(f32[8,8,1024]{2,1,0:T(8,128)} %param.7) | copy-start | bytes 786436
  29.5 7.1 %collective-permute-start.6 = (f32[8,1,1024]{2,0,1:T(8,128)S(1)}, f32[8,1,1024]{2,0,1:T(8,128)S(1)}, u32[]{:S(2)}, u32[]{:S(2)}) collective-permute-start(f32[8,1,1024]{2,0,1:T(8,128)S(1)} %copy.61), channel_id=1, source_target_pairs={{4,0},{5,1},{6,2},{7,3},{8,4},{9,5},{10,6},{11,7},{12,8},{13,9},{1... | collective-permute-start | bytes 98312 | tf_op jit(solution)/shard_map/ppermute | solution.py:24
  31.4 5.3 %collective-permute-start.3 = (f32[8,8,128]{2,1,0:T(8,128)S(1)}, f32[8,8,128]{2,1,0:T(8,128)S(1)}, u32[]{:S(2)}, u32[]{:S(2)}) collective-permute-start(f32[8,8,128]{2,1,0:T(8,128)S(1)} %get-tuple-element.31), channel_id=1, source_target_pairs={{0,1},{1,2},{2,3},{4,5},{5,6},{6,7},{8,9},{9,10},{10,11},{12,13},{... | collective-permute-start | bytes 98312 | tf_op jit(solution)/shard_map/ppermute | solution.py:24
  35.2 4.7 %collective-permute-start.4 = (f32[8,8,128]{2,1,0:T(8,128)S(1)}, f32[8,8,128]{2,1,0:T(8,128)S(1)}, u32[]{:S(2)}, u32[]{:S(2)}) collective-permute-start(f32[8,8,128]{2,1,0:T(8,128)S(1)} %get-tuple-element.32), channel_id=1, source_target_pairs={{1,0},{2,1},{3,2},{5,4},{6,5},{7,6},{9,8},{10,9},{11,10},{13,12},{... | collective-permute-start | bytes 98312 | tf_op jit(solution)/shard_map/ppermute | solution.py:24
  142.3 2.6 %copy-start.1 = (bf16[8,2,8,4096]{3,2,1,0:T(8,128)(2,1)S(1)}, bf16[8,2,8,4096]{3,2,1,0:T(8,128)(2,1)}, u32[]{:S(2)}) copy-start(bf16[8,2,8,4096]{3,2,1,0:T(8,128)(2,1)} %get-tuple-element.10) | copy-start | bytes 3145732

commit v7 on v5

--- a/solution.py
+++ b/solution.py
@@ -142,7 +142,7 @@
             sums_ref[0, 1:2, lanes] = jnp.sum(misfit, axis=0, keepdims=True)
         return carry
 
-    lax.fori_loop(0, blocks, one_block, 0)
+    lax.fori_loop(0, blocks, one_block, 0, unroll=8)
 
 
 def backward_kernel(
@@ -179,7 +179,7 @@
                 grad_ref[0, u, :, lanes] = total
         return carry
 
-    lax.fori_loop(0, blocks, one_block, 0)
+    lax.fori_loop(0, blocks, one_block, 0, unroll=8)
 
 
 def by_parity(values):

time: 131 us -> 120 us (0.916)
  Pallas kernels: 35.3 us -> 23.9 us
    pallas_call x1, Pallas kernels: 27.1 us -> 16.3 us  [local_forward(): pl.pallas_call(forward_kernel, grid=(samples,), in_specs=[whole((2 * 4 *...]
  transfers between devices with their start and end apart: 4 -> 4, of which waited for: 1 -> 1; matrix products, arithmetic and copies ran while one was open for 10% -> 11% of each run, Pallas kernels for 0% -> 0%
where the time goes in v7:
time: 120 us; the launch traced here: 119 us
  blocking collectives  45.7 us (38%)
  local copies, waits for them, and re-layouts  24.3 us (20%)
  Pallas kernels  23.9 us (20%)
  other arithmetic  11.2 us (9%)
  starting transfers between devices  10.9 us (9%)
    all_to_all x1, blocking collectives, block_carries(): mine = lax.all_to_all(packed, axis, 0, 0, tiled=True)  27.9 us
    all_to_all x1, blocking collectives, block_carries(): lax.all_to_all(jnp.concatenate([carry_in, carry_out], axis=1), axis, 0, 0...  17.8 us
    pallas_call x1, Pallas kernels, local_forward(): pl.pallas_call(forward_kernel, grid=(samples,), in_specs=[whole((2 * 4 *...  16.3 us
    ppermute x2, starting transfers between devices, with_halo(): lax.ppermute(lax.slice_in_dim(block, block.shape[dim] - width, None, axis...  7.7 us
    unnamed x33, local copies, waits for them, and re-layouts  7.65 us
    pallas_call x1, Pallas kernels, local_backward(): pl.pallas_call(backward_kernel, grid=(samples,), in_specs=[smem, per_samp...  7.57 us
    convert_element_type x1, other arithmetic, local_forward(): onehot = (local.transpose(1, 0, 2)[:, None] == spots).astype(jnp.bfloat16)  5.74 us
    transpose x2, local copies, waits for them, and re-layouts, from_parity(): return jnp.swapaxes(values, -2, -3).reshape(lead + (2 * shells, width))  3.39 us
  transfers between devices with their start and end apart: 4, of which 1 were waited for; matrix products, arithmetic and copies ran while one was open for 11% of the time, Pallas kernels for 0%

profile of v7, /device:TPU:1, one launch (start us, length us, event | category | flops | bytes accessed | tf_op | source)
XLA Modules:
  0.0 119.2 jit_solution(13896029859468824979)
XLA Ops:
  0.6 1.0 copy.86
  1.6 4.5 %collective-permute-start = (f32[8,1,8,128]{3,2,1,0:T(8,128)S(1)}, f32[8,1,8,128]{3,2,1,0:T(8,128)S(1)}, u32[]{:S(2)}, u32[]{:S(2)}) collective-permute-start(f32[8,1,8,128]{3,2,1,0:T(8,128)S(1)} %get-tuple-element.30), channel_id=1, source_target_pairs={{0,4},{4,8},{8,12},{12,16},{16,20},{20,24},{24,28},{28,32},{32,36}... | collective-permute-start | bytes 98312 | tf_op jit(solution)/shard_map/ppermute | solution.py:19
  6.2 1.9 %collective-permute-start.1 = (f32[8,1,8,128]{3,2,1,0:T(8,128)S(1)}, f32[8,1,8,128]{3,2,1,0:T(8,128)S(1)}, u32[]{:S(2)}, u32[]{:S(2)}) collective-permute-start(f32[8,1,8,128]{3,2,1,0:T(8,128)S(1)} %get-tuple-element.29), channel_id=1, source_target_pairs={{4,0},{8,4},{12,8},{16,12},{20,16},{24,20},{28,24},{32,28},{36,32}... | collective-permute-start | bytes 98312 | tf_op jit(solution)/shard_map/ppermute | solution.py:22
  8.1 1.0 convert_element_type.19
  9.1 0.2 reshape.476
  9.2 1.1 reshape.477
  10.4 0.9 copy.75
  11.2 0.1 fusion.16
  11.3 5.7 %fusion.onehot_ref = bf16[8,384,1152]{2,1,0:T(8,128)(2,1)} fusion(s32[8,1152]{1,0:T(8,128)S(1)} %fusion.16), kind=kLoop, calls=%fused_computation.1 | loop fusion | flops 7077888 | bytes 7114752 | tf_op jit(solution)/shard_map/convert_element_type | solution.py:219
  17.0 1.1 copy_bitcast_fusion.3
  18.3 0.1 constant_dynamic-update-slice_fusion.1
  18.3 0.1 fusion.25
  18.4 3.2 %collective-permute-start.2 = (f32[8,10,1,128]{3,2,1,0:T(1,128)S(1)}, f32[8,10,1,128]{3,2,1,0:T(1,128)S(1)}, u32[]{:S(2)}, u32[]{:S(2)}) collective-permute-start(f32[8,10,1,128]{3,2,1,0:T(1,128)S(1)} %get-tuple-element.27), channel_id=1, source_target_pairs={{0,1},{1,2},{2,3},{4,5},{5,6},{6,7},{8,9},{9,10},{10,11},{12,13},{... | collective-permute-start | bytes 122888 | tf_op jit(solution)/shard_map/ppermute | solution.py:19
  21.6 1.3 %collective-permute-start.3 = (f32[8,10,1,128]{3,2,1,0:T(1,128)S(1)}, f32[8,10,1,128]{3,2,1,0:T(1,128)S(1)}, u32[]{:S(2)}, u32[]{:S(2)}) collective-permute-start(f32[8,10,1,128]{3,2,1,0:T(1,128)S(1)} %get-tuple-element.28), channel_id=1, source_target_pairs={{1,0},{2,1},{3,2},{5,4},{6,5},{7,6},{9,8},{10,9},{11,10},{13,12},{... | collective-permute-start | bytes 122888 | tf_op jit(solution)/shard_map/ppermute | solution.py:22
  22.9 0.1 reshape.483.sqrt_ref
  23.0 0.6 copy.52
  23.6 1.6 %copy.84 = bf16[8,8,2,4096]{3,1,2,0:T(8,128)(2,1)} copy(bf16[8,8,2,4096]{3,0,2,1:T(8,128)(2,1)S(1)} %bitcast.95) | data formatting | bytes 2097152 | tf_op jit(solution)/shard_map/reshape | solution.py:188
  25.2 0.1 broadcast_in_dim.8
  25.3 0.1 concatenate.47
  25.4 0.9 collective-permute-done.3
  26.4 0.1 pad_maximum_fusion
  26.5 0.2 copy.85
  26.9 0.2 reduce-precision_convert_fusion.1
  27.1 0.4 fusion.6
  27.5 1.8 %copy.51 = bf16[8,8,3,16,384]{4,3,2,1,0:T(8,128)(2,1)} copy(bf16[8,8,3,16,384]{4,0,3,1,2:T(8,128)(2,1)S(1)} %fusion.6) | data formatting | bytes 4718592 | tf_op jit(solution)/shard_map/transpose | solution.py:215
  29.3 0.8 broadcast_in_dim.10.sqrt_ref
  30.1 1.2 %broadcast_in_dim.9.weights_ref = f32[216,8,128]{2,1,0:T(8,128)} broadcast(f32[216]{0:T(256)S(1)} %broadcast_in_dim.8), dimensions={0} | broadcast | bytes 885600 | tf_op jit(solution)/shard_map/broadcast_in_dim | solution.py:200
  31.3 0.7 broadcast_in_dim.11.widths_ref
  32.0 16.3 %shard_map.86 = (f32[8,2,8,4096]{3,2,1,0:T(8,128)}, f32[8,2,8,4096]{3,2,1,0:T(8,128)}, f32[8,2,4096]{2,1,0:T(2,128)}) custom-call(f32[216,8,128]{2,1,0:T(8,128)} %broadcast_in_dim.9.weights_ref, f32[64,8,128]{2,1,0:T(8,128)} %broadcast_in_dim.10.sqrt_ref, bf16[8,8,48,384]{3,2,1,0:T(8,128)(2,1)} %bitcast.84, bf16[8,384,1152]{2,1,0:T(8,128)(2,1)} %fusion.onehot_ref, ...), custom_call_target="tpu_custom_call" | custom-call | tf_op jit(solution)/shard_map/pallas_call | solution.py:227
  48.3 1.7 %slice_reduce_fusion.1 = (f32[8,4096]{1,0:T(8,128)S(1)}, f32[8,4096]{1,0:T(8,128)S(1)}) fusion(f32[8,2,4096]{2,1,0:T(2,128)} %get-tuple-element.9), kind=kLoop, calls=%fused_computation.25 | loop fusion | bytes 524288 | tf_op jit(solution)/shard_map/slice | solution.py:313
  50.0 0.1 concatenate.45
  50.1 0.2 copy.56
  50.3 0.1 concatenate.46
  50.4 0.2 copy.57
  50.6 0.1 maximum_bitcast_fusion
  50.6 0.4 reshape.488
  51.0 27.9 %all_to_all.10 = f32[64,1,1088]{2,1,0:T(1,128)S(1)} all-to-all(f32[64,1,1088]{2,1,0:T(1,128)S(1)} %reshape.488), channel_id=1, replica_groups=mesh['dist'=64,'sky'=4] {'dist'}, dimensions={0} | all-to-all | bytes 557056 | tf_op jit(solution)/shard_map/all_to_all | solution.py:33
  78.9 0.5 broadcast.53
  79.4 1.3 %reduce.4 = f32[64,1088]{1,0:T(8,128)S(1)} reduce(f32[64,1,1088]{2,1,0:T(1,128)S(1)} %all_to_all.10, f32[]{:T(128)} %broadcast.53), dimensions={1}, to_apply=%all_to_all.6.reduce_sub_computation | reduce | bytes 557060 | tf_op jit(solution)/shard_map/all_to_all | solution.py:33
  80.8 0.1 reshape.489
  81.0 0.1 reshape.478
  81.1 0.1 copy.58
  81.2 0.5 copy_add_fusion
  81.8 0.2 copy.61
  81.9 0.1 reshape.479
  82.1 0.1 copy.72
  82.2 0.5 fusion.18
  82.7 0.1 pad_maximum_fusion.1
  82.8 0.3 copy.63
  83.1 0.3 reshape.490
  83.4 17.8 %all_to_all.11 = f32[64,1,1024]{2,1,0:T(1,128)S(1)} all-to-all(f32[64,1,1024]{2,1,0:T(1,128)S(1)} %reshape.490), channel_id=1, replica_groups=mesh['dist'=64,'sky'=4] {'dist'}, dimensions={0} | all-to-all | bytes 524288 | tf_op jit(solution)/shard_map/all_to_all | solution.py:44
  101.2 1.3 %reduce.5 = f32[64,1024]{1,0:T(8,128)S(1)} reduce(f32[64,1,1024]{2,1,0:T(1,128)S(1)} %all_to_all.11, f32[]{:T(128)} %broadcast.53), dimensions={1}, to_apply=%all_to_all.7.reduce_sub_computation | reduce | bytes 524292 | tf_op jit(solution)/shard_map/all_to_all | solution.py:44
  102.5 0.1 reshape.491
  102.7 0.1 copy.64
  102.7 0.2 stack.53
  102.9 0.1 copy.65
  103.0 0.2 stack.54
  103.2 0.9 pad_maximum_fusion.2.carries_ref
  104.1 7.6 %shard_map.87 = (bf16[8,2,8,4096]{3,2,1,0:T(8,128)(2,1)}, f32[8,2,8,4096]{3,2,1,0:T(8,128)}) custom-call(f32[64]{0:T(128)} %copy-done.5, f32[8,2,8,4096]{3,2,1,0:T(8,128)} %get-tuple-element.7.density_ref, f32[8,2,8,4096]{3,2,1,0:T(8,128)} %get-tuple-element.8.local_ref, f32[8,2,4096]{2,1,0:T(2,128)} %pad_maximum_fusion.2.carries_ref, ...), custom_call_target="tpu_custom_call" | custom-call | tf_op jit(solution)/shard_map/pallas_call | solution.py:269
  111.7 2.8 %copy.67 = f32[8,8,2,4096]{3,0,2,1:T(8,128)S(1)} copy(f32[8,8,2,4096]{3,1,2,0:T(8,128)} %bitcast.97) | data formatting | bytes 4194304 | tf_op jit(solution)/shard_map/transpose | solution.py:195
  114.5 0.0 copy-start.1
  114.5 2.5 %copy.69 = f32[8,16,4096]{2,1,0:T(8,128)} copy(f32[8,16,4096]{2,0,1:T(8,128)S(1)} %bitcast.85) | data formatting | bytes 4194304
  117.0 0.6 copy.66
  117.6 1.6 %copy.68 = bf16[8,16,4096]{2,1,0:T(8,128)(2,1)} copy(bf16[8,16,4096]{2,0,1:T(8,128)(2,1)S(1)} %bitcast.94) | data formatting | bytes 2097152
  (34 shorter events, 0.3 us)
Async XLA Ops:
  1.6 16.6 %collective-permute-start = (f32[8,1,8,128]{3,2,1,0:T(8,128)S(1)}, f32[8,1,8,128]{3,2,1,0:T(8,128)S(1)}, u32[]{:S(2)}, u32[]{:S(2)}) collective-permute-start(f32[8,1,8,128]{3,2,1,0:T(8,128)S(1)} %get-tuple-element.30), channel_id=1, source_target_pairs={{0,4},{4,8},{8,12},{12,16},{16,20},{20,24},{24,28},{28,32},{32,36}... | collective-permute-start | bytes 98312 | tf_op jit(solution)/shard_map/ppermute | solution.py:19
  6.2 12.2 %collective-permute-start.1 = (f32[8,1,8,128]{3,2,1,0:T(8,128)S(1)}, f32[8,1,8,128]{3,2,1,0:T(8,128)S(1)}, u32[]{:S(2)}, u32[]{:S(2)}) collective-permute-start(f32[8,1,8,128]{3,2,1,0:T(8,128)S(1)} %get-tuple-element.29), channel_id=1, source_target_pairs={{4,0},{8,4},{12,8},{16,12},{20,16},{24,20},{28,24},{32,28},{36,32}... | collective-permute-start | bytes 98312 | tf_op jit(solution)/shard_map/ppermute | solution.py:22
  11.3 6.9 %copy-start.2 = (s32[16,4096]{1,0:T(8,128)S(1)}, s32[16,4096]{1,0:T(8,128)}, u32[]{:S(2)}) copy-start(s32[16,4096]{1,0:T(8,128)} %param.13) | copy-start | bytes 786436
  11.3 7.0 %copy-start.3 = (f32[8,8,1024]{2,1,0:T(8,128)S(1)}, f32[8,8,1024]{2,1,0:T(8,128)}, u32[]{:S(2)}) copy-start(f32[8,8,1024]{2,1,0:T(8,128)} %param.7) | copy-start | bytes 786436
  11.3 11.6 %copy-start.6 = (bf16[2,4,2,4]{3,2,1,0:T(2,128)(2,1)S(1)}, bf16[2,4,2,4]{3,2,1,0:T(2,128)(2,1)}, u32[]{:S(2)}) copy-start(bf16[2,4,2,4]{3,2,1,0:T(2,128)(2,1)} %param.10) | copy-start | bytes 388
  17.0 6.0 %copy-start = (bf16[8,16,4096]{2,1,0:T(8,128)(2,1)S(1)}, bf16[8,16,4096]{2,1,0:T(8,128)(2,1)}, u32[]{:S(2)}) copy-start(bf16[8,16,4096]{2,1,0:T(8,128)(2,1)} %param.8) | copy-start | bytes 3145732
  18.2 6.9 %copy-start.4 = (f32[2,4,3,9]{3,1,2,0:T(4,128)S(1)}, f32[2,4,3,9]{3,1,2,0:T(4,128)}, u32[]{:S(2)}) copy-start(f32[2,4,3,9]{3,1,2,0:T(4,128)} %param.9) | copy-start | bytes 2596
  18.4 7.0 %collective-permute-start.2 = (f32[8,10,1,128]{3,2,1,0:T(1,128)S(1)}, f32[8,10,1,128]{3,2,1,0:T(1,128)S(1)}, u32[]{:S(2)}, u32[]{:S(2)}) collective-permute-start(f32[8,10,1,128]{3,2,1,0:T(1,128)S(1)} %get-tuple-element.27), channel_id=1, source_target_pairs={{0,1},{1,2},{2,3},{4,5},{5,6},{6,7},{8,9},{9,10},{10,11},{12,13},{... | collective-permute-start | bytes 122888 | tf_op jit(solution)/shard_map/ppermute | solution.py:19
  21.6 4.7 %collective-permute-start.3 = (f32[8,10,1,128]{3,2,1,0:T(1,128)S(1)}, f32[8,10,1,128]{3,2,1,0:T(1,128)S(1)}, u32[]{:S(2)}, u32[]{:S(2)}) collective-permute-start(f32[8,10,1,128]{3,2,1,0:T(1,128)S(1)} %get-tuple-element.28), channel_id=1, source_target_pairs={{1,0},{2,1},{3,2},{5,4},{6,5},{7,6},{9,8},{10,9},{11,10},{13,12},{... | collective-permute-start | bytes 122888 | tf_op jit(solution)/shard_map/ppermute | solution.py:22
  23.0 6.3 %copy-start.5 = (f32[64]{0:T(128)}, f32[64]{0:T(128)S(1)}, u32[]{:S(2)}) copy-start(f32[64]{0:T(128)S(1)} %reshape.483.sqrt_ref) | copy-start | bytes 772
  114.5 2.6 %copy-start.1 = (bf16[8,2,8,4096]{3,2,1,0:T(8,128)(2,1)S(1)}, bf16[8,2,8,4096]{3,2,1,0:T(8,128)(2,1)}, u32[]{:S(2)}) copy-start(bf16[8,2,8,4096]{3,2,1,0:T(8,128)(2,1)} %get-tuple-element.10) | copy-start | bytes 3145732

commit v8 on v7

--- a/solution.py
+++ b/solution.py
@@ -100,11 +100,24 @@
 
 def forward_kernel(
     weights_ref, sqrt_ref, pieces_ref, onehot_ref, excite_ref, counts_ref, stars_ref, widths_ref,
-    density_ref, local_ref, sums_ref, picked_ref,
+    density_ref, local_ref, sums_ref, picked_ref, weight_tiles, sqrt_tiles, width_tiles,
 ):
     blocks = onehot_ref.shape[0]
     slots = onehot_ref.shape[2] // LANES
     tile = blocks * LANES
+
+    @pl.when(pl.program_id(0) == 0)
+    def _():
+        for index in range(weight_tiles.shape[0]):
+            weight_tiles[index] = jnp.full((8, LANES), weights_ref[index], jnp.float32)
+        for index in range(sqrt_tiles.shape[0]):
+            sqrt_tiles[index] = jnp.full((8, LANES), sqrt_ref[index], jnp.float32)
+        row = lax.broadcasted_iota(jnp.int32, (8, LANES), 0)
+        for t in range(2):
+            column = jnp.zeros((8, LANES), jnp.float32)
+            for s in range(8):
+                column = jnp.where(row == s, widths_ref[2 * s + t], column)
+            width_tiles[t] = column
 
     def one_block(b, carry):
         picked = jnp.dot(pieces_ref[0, b], onehot_ref[b], preferred_element_type=jnp.float32)
@@ -116,7 +129,7 @@
                 for u in range(2):
                     for r in range(4):
                         lanes = pl.ds(pl.multiple_of(r * tile + b * LANES, LANES), LANES)
-                        term = sqrt_ref[((t * 4 + q) * 2 + u) * 4 + r] * excite_ref[0, u, :, lanes].astype(jnp.float32)
+                        term = sqrt_tiles[((t * 4 + q) * 2 + u) * 4 + r] * excite_ref[0, u, :, lanes].astype(jnp.float32)
                         total = term if total is None else total + term
                 acc[t, q] = total
         for j in range(3):
@@ -124,11 +137,11 @@
                 near = picked_ref[pl.ds(j, 8), pl.ds(m * LANES, LANES)]
                 for t in range(2):
                     for q in range(4):
-                        acc[t, q] = acc[t, q] + weights_ref[((t * 4 + q) * 3 + j) * 9 + m] * near
+                        acc[t, q] = acc[t, q] + weight_tiles[((t * 4 + q) * 3 + j) * 9 + m] * near
         for q in range(4):
             lanes = pl.ds(pl.multiple_of(q * tile + b * LANES, LANES), LANES)
-            even = jnp.exp(acc[0, q]) * widths_ref[0]
-            odd = jnp.exp(acc[1, q]) * widths_ref[1]
+            even = jnp.exp(acc[0, q]) * width_tiles[0]
+            odd = jnp.exp(acc[1, q]) * width_tiles[1]
             density_ref[0, 0, :, lanes] = even
             density_ref[0, 1, :, lanes] = odd
             through = running(even + odd, True)
@@ -220,7 +233,6 @@
     onehot = onehot.reshape(blocks, window, slots * BAND)
     excite = by_parity(excitations)
     half = fine_shells // 2
-    wide = jnp.broadcast_to(widths.reshape(half, 2).T[:, :, None], (2, half, LANES))
     smem = pl.BlockSpec(memory_space=pltpu.SMEM)
     whole = lambda shape: pl.BlockSpec(shape, lambda k: (0,) * len(shape))
     per_sample = lambda shape: pl.BlockSpec(shape, lambda k: (k,) + (0,) * (len(shape) - 1))
@@ -228,14 +240,14 @@
         forward_kernel,
         grid=(samples,),
         in_specs=[
-            whole((2 * 4 * 3 * slots, 8, LANES)),
-            whole((2 * 4 * 2 * 4, 8, LANES)),
+            smem,
+            smem,
             per_sample((1, blocks, 48, window)),
             whole((blocks, window, slots * BAND)),
             per_sample((1, 2, half, fine_pixels)),
             whole((2, half, fine_pixels)),
             whole((2, half, fine_pixels)),
-            whole((2, half, LANES)),
+            smem,
         ],
         out_specs=[
             per_sample((1, 2, half, fine_pixels)),
@@ -247,17 +259,22 @@
             jax.ShapeDtypeStruct((samples, 2, half, fine_pixels), jnp.float32),
             jax.ShapeDtypeStruct((samples, 2, fine_pixels), jnp.float32),
         ],
-        scratch_shapes=[pltpu.VMEM((16, slots * BAND), jnp.float32)],
+        scratch_shapes=[
+            pltpu.VMEM((16, slots * BAND), jnp.float32),
+            pltpu.VMEM((2 * 4 * 3 * slots, 8, LANES), jnp.float32),
+            pltpu.VMEM((2 * 4 * 2 * 4, 8, LANES), jnp.float32),
+            pltpu.VMEM((2, 8, LANES), jnp.float32),
+        ],
         interpret=INTERPRET,
     )(
-        tiles(refine_weights),
-        tiles(refine_sqrt.astype(jnp.float32)),
+        refine_weights.reshape(-1),
+        refine_sqrt.astype(jnp.float32).reshape(-1),
         pieces,
         onehot,
         excite,
         by_parity(counts),
         by_parity(stars),
-        wide,
+        widths,
     )
 
 

time: 120 us -> 117 us (0.975)
  local copies, waits for them, and re-layouts: 24.3 us -> 22.6 us
    broadcast_in_dim x4 -> x0, local copies, waits for them, and re-layouts: 2.81 us -> none  [the longest x3 2.15 us: tiles(): return jnp.broadcast_to(flat[:, None, None], (flat.shape[0], 8, LANES))]
    unnamed x33 -> x31, local copies, waits for them, and re-layouts: 7.65 us -> 7.65 us
  transfers between devices with their start and end apart: 4 -> 4, of which waited for: 1 -> 0; matrix products, arithmetic and copies ran while one was open for 11% -> 12% of each run, Pallas kernels for 0% -> 0%
where the time goes in v8:
time: 117 us; the launch traced here: 116 us
  blocking collectives  45.2 us (39%)
  Pallas kernels  23.6 us (20%)
  local copies, waits for them, and re-layouts  22.6 us (19%)
  other arithmetic  11.8 us (10%)
  starting transfers between devices  10.9 us (9%)
    all_to_all x1, blocking collectives, block_carries(): mine = lax.all_to_all(packed, axis, 0, 0, tiled=True)  27.3 us
    all_to_all x1, blocking collectives, block_carries(): lax.all_to_all(jnp.concatenate([carry_in, carry_out], axis=1), axis, 0, 0...  17.8 us
    pallas_call x1, Pallas kernels, local_forward(): pl.pallas_call(forward_kernel, grid=(samples,), in_specs=[smem, smem, per...  16.1 us
    ppermute x2, starting transfers between devices, with_halo(): lax.ppermute(lax.slice_in_dim(block, block.shape[dim] - width, None, axis...  7.7 us
    unnamed x31, local copies, waits for them, and re-layouts  7.65 us
    pallas_call x1, Pallas kernels, local_backward(): pl.pallas_call(backward_kernel, grid=(samples,), in_specs=[smem, per_samp...  7.56 us
    convert_element_type x1, other arithmetic, local_forward(): onehot = (local.transpose(1, 0, 2)[:, None] == spots).astype(jnp.bfloat16)  5.75 us
    transpose x2, local copies, waits for them, and re-layouts, from_parity(): return jnp.swapaxes(values, -2, -3).reshape(lead + (2 * shells, width))  3.39 us
  transfers between devices with their start and end apart: 4, of which 0 were waited for; matrix products, arithmetic and copies ran while one was open for 12% of the time, Pallas kernels for 0%

profile of v8, /device:TPU:1, one launch (start us, length us, event | category | flops | bytes accessed | tf_op | source)
XLA Modules:
  0.0 116.2 jit_solution(12238000879604409179)
XLA Ops:
  0.6 1.0 copy.86
  1.6 4.5 %collective-permute-start = (f32[8,1,8,128]{3,2,1,0:T(8,128)S(1)}, f32[8,1,8,128]{3,2,1,0:T(8,128)S(1)}, u32[]{:S(2)}, u32[]{:S(2)}) collective-permute-start(f32[8,1,8,128]{3,2,1,0:T(8,128)S(1)} %get-tuple-element.30), channel_id=1, source_target_pairs={{0,4},{4,8},{8,12},{12,16},{16,20},{20,24},{24,28},{28,32},{32,36}... | collective-permute-start | bytes 98312 | tf_op jit(solution)/shard_map/ppermute | solution.py:19
  6.2 1.9 %collective-permute-start.1 = (f32[8,1,8,128]{3,2,1,0:T(8,128)S(1)}, f32[8,1,8,128]{3,2,1,0:T(8,128)S(1)}, u32[]{:S(2)}, u32[]{:S(2)}) collective-permute-start(f32[8,1,8,128]{3,2,1,0:T(8,128)S(1)} %get-tuple-element.29), channel_id=1, source_target_pairs={{4,0},{8,4},{12,8},{16,12},{20,16},{24,20},{28,24},{32,28},{36,32}... | collective-permute-start | bytes 98312 | tf_op jit(solution)/shard_map/ppermute | solution.py:22
  8.1 1.0 convert_element_type.17
  9.1 0.2 reshape.476
  9.2 1.1 reshape.477
  10.4 0.9 copy.75
  11.2 0.1 fusion.16
  11.3 5.7 %fusion.onehot_ref = bf16[8,384,1152]{2,1,0:T(8,128)(2,1)} fusion(s32[8,1152]{1,0:T(8,128)S(1)} %fusion.16), kind=kLoop, calls=%fused_computation.1 | loop fusion | flops 7077888 | bytes 7114752 | tf_op jit(solution)/shard_map/convert_element_type | solution.py:232
  17.0 1.1 copy_bitcast_fusion.3
  18.2 0.0 collective-permute-done
  18.2 0.0 copy-start.4
  18.2 0.1 constant_dynamic-update-slice_fusion.1
  18.3 0.1 fusion.25
  18.4 3.2 %collective-permute-start.2 = (f32[8,10,1,128]{3,2,1,0:T(1,128)S(1)}, f32[8,10,1,128]{3,2,1,0:T(1,128)S(1)}, u32[]{:S(2)}, u32[]{:S(2)}) collective-permute-start(f32[8,10,1,128]{3,2,1,0:T(1,128)S(1)} %get-tuple-element.27), channel_id=1, source_target_pairs={{0,1},{1,2},{2,3},{4,5},{5,6},{6,7},{8,9},{9,10},{10,11},{12,13},{... | collective-permute-start | bytes 122888 | tf_op jit(solution)/shard_map/ppermute | solution.py:19
  21.6 1.3 %collective-permute-start.3 = (f32[8,10,1,128]{3,2,1,0:T(1,128)S(1)}, f32[8,10,1,128]{3,2,1,0:T(1,128)S(1)}, u32[]{:S(2)}, u32[]{:S(2)}) collective-permute-start(f32[8,10,1,128]{3,2,1,0:T(1,128)S(1)} %get-tuple-element.28), channel_id=1, source_target_pairs={{1,0},{2,1},{3,2},{5,4},{6,5},{7,6},{9,8},{10,9},{11,10},{13,12},{... | collective-permute-start | bytes 122888 | tf_op jit(solution)/shard_map/ppermute | solution.py:22
  22.9 0.5 exponential_multiply_fusion.widths_ref
  23.4 0.6 reshape.483.sqrt_ref
  24.0 0.6 copy.52
  24.6 1.6 %copy.84 = bf16[8,8,2,4096]{3,1,2,0:T(8,128)(2,1)} copy(bf16[8,8,2,4096]{3,0,2,1:T(8,128)(2,1)S(1)} %bitcast.96) | data formatting | bytes 2097152 | tf_op jit(solution)/shard_map/reshape | solution.py:201
  26.2 0.6 reshape.470.weights_ref
  26.8 0.1 concatenate.47
  26.9 0.0 collective-permute-done.2
  26.9 0.1 pad_maximum_fusion
  27.0 0.2 copy.85
  27.4 0.2 reduce-precision_convert_fusion.1
  27.7 0.4 fusion.6
  28.0 1.8 %copy.51 = bf16[8,8,3,16,384]{4,3,2,1,0:T(8,128)(2,1)} copy(bf16[8,8,3,16,384]{4,0,3,1,2:T(8,128)(2,1)S(1)} %fusion.6) | data formatting | bytes 4718592 | tf_op jit(solution)/shard_map/transpose | solution.py:228
  29.8 16.1 %shard_map.86 = (f32[8,2,8,4096]{3,2,1,0:T(8,128)}, f32[8,2,8,4096]{3,2,1,0:T(8,128)}, f32[8,2,4096]{2,1,0:T(2,128)}) custom-call(f32[216]{0:T(256)} %reshape.470.weights_ref, f32[64]{0:T(128)} %reshape.483.sqrt_ref, bf16[8,8,48,384]{3,2,1,0:T(8,128)(2,1)} %bitcast.84, bf16[8,384,1152]{2,1,0:T(8,128)(2,1)} %fusion.onehot_ref, ...), custom_call_target="tpu_custom_call" | custom-call | tf_op jit(solution)/shard_map/pallas_call | solution.py:239
  45.9 1.7 %slice_reduce_fusion.1 = (f32[8,4096]{1,0:T(8,128)S(1)}, f32[8,4096]{1,0:T(8,128)S(1)}) fusion(f32[8,2,4096]{2,1,0:T(2,128)} %get-tuple-element.9), kind=kLoop, calls=%fused_computation.25 | loop fusion | bytes 524288 | tf_op jit(solution)/shard_map/slice | solution.py:330
  47.6 0.1 concatenate.45
  47.7 0.2 copy.56
  47.9 0.1 concatenate.46
  48.0 0.2 copy.57
  48.1 0.1 maximum_bitcast_fusion
  48.2 0.4 reshape.488
  48.6 27.3 %all_to_all.10 = f32[64,1,1088]{2,1,0:T(1,128)S(1)} all-to-all(f32[64,1,1088]{2,1,0:T(1,128)S(1)} %reshape.488), channel_id=1, replica_groups=mesh['dist'=64,'sky'=4] {'dist'}, dimensions={0} | all-to-all | bytes 557056 | tf_op jit(solution)/shard_map/all_to_all | solution.py:33
  75.9 0.5 broadcast.39
  76.4 1.3 %reduce.4 = f32[64,1088]{1,0:T(8,128)S(1)} reduce(f32[64,1,1088]{2,1,0:T(1,128)S(1)} %all_to_all.10, f32[]{:T(128)} %broadcast.39), dimensions={1}, to_apply=%all_to_all.6.reduce_sub_computation | reduce | bytes 557060 | tf_op jit(solution)/shard_map/all_to_all | solution.py:33
  77.8 0.1 reshape.489
  78.0 0.1 reshape.478
  78.1 0.1 copy.58
  78.2 0.5 copy_add_fusion
  78.8 0.2 copy.61
  78.9 0.1 reshape.479
  79.1 0.1 copy.72
  79.2 0.5 fusion.18
  79.7 0.1 pad_maximum_fusion.1
  79.8 0.3 copy.63
  80.1 0.3 reshape.490
  80.4 17.8 %all_to_all.11 = f32[64,1,1024]{2,1,0:T(1,128)S(1)} all-to-all(f32[64,1,1024]{2,1,0:T(1,128)S(1)} %reshape.490), channel_id=1, replica_groups=mesh['dist'=64,'sky'=4] {'dist'}, dimensions={0} | all-to-all | bytes 524288 | tf_op jit(solution)/shard_map/all_to_all | solution.py:44
  98.2 1.3 %reduce.5 = f32[64,1024]{1,0:T(8,128)S(1)} reduce(f32[64,1,1024]{2,1,0:T(1,128)S(1)} %all_to_all.11, f32[]{:T(128)} %broadcast.39), dimensions={1}, to_apply=%all_to_all.7.reduce_sub_computation | reduce | bytes 524292 | tf_op jit(solution)/shard_map/all_to_all | solution.py:44
  99.5 0.1 reshape.491
  99.7 0.1 copy.64
  99.7 0.2 stack.53
  99.9 0.1 copy.65
  100.0 0.2 stack.54
  100.2 0.9 pad_maximum_fusion.2.carries_ref
  101.1 7.6 %shard_map.87 = (bf16[8,2,8,4096]{3,2,1,0:T(8,128)(2,1)}, f32[8,2,8,4096]{3,2,1,0:T(8,128)}) custom-call(f32[64]{0:T(128)} %reshape.483.sqrt_ref, f32[8,2,8,4096]{3,2,1,0:T(8,128)} %get-tuple-element.7.density_ref, f32[8,2,8,4096]{3,2,1,0:T(8,128)} %get-tuple-element.8.local_ref, f32[8,2,4096]{2,1,0:T(2,128)} %pad_maximum_fusion.2.carries_ref, ...), custom_call_target="tpu_custom_call" | custom-call | tf_op jit(solution)/shard_map/pallas_call | solution.py:286
  108.7 2.8 %copy.67 = f32[8,8,2,4096]{3,0,2,1:T(8,128)S(1)} copy(f32[8,8,2,4096]{3,1,2,0:T(8,128)} %bitcast.97) | data formatting | bytes 4194304 | tf_op jit(solution)/shard_map/transpose | solution.py:208
  111.5 0.0 copy-start.1
  111.5 2.5 %copy.69 = f32[8,16,4096]{2,1,0:T(8,128)} copy(f32[8,16,4096]{2,0,1:T(8,128)S(1)} %bitcast.85) | data formatting | bytes 4194304
  114.0 0.6 copy.66
  114.6 1.6 %copy.68 = bf16[8,16,4096]{2,1,0:T(8,128)(2,1)} copy(bf16[8,16,4096]{2,0,1:T(8,128)(2,1)S(1)} %bitcast.95) | data formatting | bytes 2097152
  (29 shorter events, 0.3 us)
Async XLA Ops:
  1.6 16.5 %collective-permute-start = (f32[8,1,8,128]{3,2,1,0:T(8,128)S(1)}, f32[8,1,8,128]{3,2,1,0:T(8,128)S(1)}, u32[]{:S(2)}, u32[]{:S(2)}) collective-permute-start(f32[8,1,8,128]{3,2,1,0:T(8,128)S(1)} %get-tuple-element.30), channel_id=1, source_target_pairs={{0,4},{4,8},{8,12},{12,16},{16,20},{20,24},{24,28},{28,32},{32,36}... | collective-permute-start | bytes 98312 | tf_op jit(solution)/shard_map/ppermute | solution.py:19
  6.2 12.1 %collective-permute-start.1 = (f32[8,1,8,128]{3,2,1,0:T(8,128)S(1)}, f32[8,1,8,128]{3,2,1,0:T(8,128)S(1)}, u32[]{:S(2)}, u32[]{:S(2)}) collective-permute-start(f32[8,1,8,128]{3,2,1,0:T(8,128)S(1)} %get-tuple-element.29), channel_id=1, source_target_pairs={{4,0},{8,4},{12,8},{16,12},{20,16},{24,20},{28,24},{32,28},{36,32}... | collective-permute-start | bytes 98312 | tf_op jit(solution)/shard_map/ppermute | solution.py:22
  11.3 6.8 %copy-start.2 = (s32[16,4096]{1,0:T(8,128)S(1)}, s32[16,4096]{1,0:T(8,128)}, u32[]{:S(2)}) copy-start(s32[16,4096]{1,0:T(8,128)} %param.13) | copy-start | bytes 786436
  11.3 6.9 %copy-start.3 = (f32[8,8,1024]{2,1,0:T(8,128)S(1)}, f32[8,8,1024]{2,1,0:T(8,128)}, u32[]{:S(2)}) copy-start(f32[8,8,1024]{2,1,0:T(8,128)} %param.7) | copy-start | bytes 786436
  11.3 12.1 %copy-start.5 = (bf16[2,4,2,4]{3,2,1,0:T(2,128)(2,1)S(1)}, bf16[2,4,2,4]{3,2,1,0:T(2,128)(2,1)}, u32[]{:S(2)}) copy-start(bf16[2,4,2,4]{3,2,1,0:T(2,128)(2,1)} %param.10) | copy-start | bytes 388
  17.0 7.0 %copy-start = (bf16[8,16,4096]{2,1,0:T(8,128)(2,1)S(1)}, bf16[8,16,4096]{2,1,0:T(8,128)(2,1)}, u32[]{:S(2)}) copy-start(bf16[8,16,4096]{2,1,0:T(8,128)(2,1)} %param.8) | copy-start | bytes 3145732
  18.2 7.9 %copy-start.4 = (f32[2,4,3,9]{3,1,2,0:T(4,128)S(1)}, f32[2,4,3,9]{3,1,2,0:T(4,128)}, u32[]{:S(2)}) copy-start(f32[2,4,3,9]{3,1,2,0:T(4,128)} %param.9) | copy-start | bytes 2596
  18.4 8.5 %collective-permute-start.2 = (f32[8,10,1,128]{3,2,1,0:T(1,128)S(1)}, f32[8,10,1,128]{3,2,1,0:T(1,128)S(1)}, u32[]{:S(2)}, u32[]{:S(2)}) collective-permute-start(f32[8,10,1,128]{3,2,1,0:T(1,128)S(1)} %get-tuple-element.27), channel_id=1, source_target_pairs={{0,1},{1,2},{2,3},{4,5},{5,6},{6,7},{8,9},{9,10},{10,11},{12,13},{... | collective-permute-start | bytes 122888 | tf_op jit(solution)/shard_map/ppermute | solution.py:19
  21.6 5.3 %collective-permute-start.3 = (f32[8,10,1,128]{3,2,1,0:T(1,128)S(1)}, f32[8,10,1,128]{3,2,1,0:T(1,128)S(1)}, u32[]{:S(2)}, u32[]{:S(2)}) collective-permute-start(f32[8,10,1,128]{3,2,1,0:T(1,128)S(1)} %get-tuple-element.28), channel_id=1, source_target_pairs={{1,0},{2,1},{3,2},{5,4},{6,5},{7,6},{9,8},{10,9},{11,10},{13,12},{... | collective-permute-start | bytes 122888 | tf_op jit(solution)/shard_map/ppermute | solution.py:22
  111.5 2.6 %copy-start.1 = (bf16[8,2,8,4096]{3,2,1,0:T(8,128)(2,1)S(1)}, bf16[8,2,8,4096]{3,2,1,0:T(8,128)(2,1)}, u32[]{:S(2)}) copy-start(bf16[8,2,8,4096]{3,2,1,0:T(8,128)(2,1)} %get-tuple-element.10) | copy-start | bytes 3145732

commit v9 on v8

--- a/solution.py
+++ b/solution.py
@@ -98,6 +98,21 @@
     return values
 
 
+def paired(values, odd_from_even):
+    row = lax.broadcasted_iota(jnp.int32, values.shape, 0)
+    if odd_from_even:
+        return jnp.where(row % 2 == 1, shifted(values, 1, True), values)
+    return jnp.where(row % 2 == 0, shifted(values, 1, False), values)
+
+
+def alternating(table, index_of, count, target):
+    row = lax.broadcasted_iota(jnp.int32, (8, LANES), 0)
+    for n in range(count):
+        even = jnp.full((8, LANES), table[index_of(n, 0)], jnp.float32)
+        odd = jnp.full((8, LANES), table[index_of(n, 1)], jnp.float32)
+        target[n] = jnp.where(row % 2 == 0, even, odd)
+
+
 def forward_kernel(
     weights_ref, sqrt_ref, pieces_ref, onehot_ref, excite_ref, counts_ref, stars_ref, widths_ref,
     density_ref, local_ref, sums_ref, picked_ref, weight_tiles, sqrt_tiles, width_tiles,
@@ -105,94 +120,96 @@
     blocks = onehot_ref.shape[0]
     slots = onehot_ref.shape[2] // LANES
     tile = blocks * LANES
+    rows = picked_ref.shape[0]
 
     @pl.when(pl.program_id(0) == 0)
     def _():
-        for index in range(weight_tiles.shape[0]):
-            weight_tiles[index] = jnp.full((8, LANES), weights_ref[index], jnp.float32)
-        for index in range(sqrt_tiles.shape[0]):
-            sqrt_tiles[index] = jnp.full((8, LANES), sqrt_ref[index], jnp.float32)
+        alternating(weights_ref, lambda n, t: t * 4 * 3 * slots + n, 4 * 3 * slots, weight_tiles)
+        alternating(sqrt_ref, lambda n, t: t * 4 * 2 * 4 + n, 4 * 2 * 4, sqrt_tiles)
         row = lax.broadcasted_iota(jnp.int32, (8, LANES), 0)
-        for t in range(2):
+        for h in range(2):
             column = jnp.zeros((8, LANES), jnp.float32)
-            for s in range(8):
-                column = jnp.where(row == s, widths_ref[2 * s + t], column)
-            width_tiles[t] = column
-
-    def one_block(b, carry):
+            for i in range(8):
+                column = jnp.where(row == i, widths_ref[8 * h + i], column)
+            width_tiles[h] = column
+
+    for b in range(blocks):
         picked = jnp.dot(pieces_ref[0, b], onehot_ref[b], preferred_element_type=jnp.float32)
-        picked_ref[...] = (picked[0:16] + picked[16:32]) + picked[32:48]
+        picked_ref[...] = (picked[0:rows] + picked[rows : 2 * rows]) + picked[2 * rows : 3 * rows]
         acc = {}
-        for t in range(2):
+        for h in range(2):
+            spread = {}
+            for r in range(4):
+                lanes = pl.ds(r * tile + b * LANES, LANES)
+                values = excite_ref[0, pl.ds(8 * h, 8), lanes].astype(jnp.float32)
+                spread[0, r] = paired(values, True)
+                spread[1, r] = paired(values, False)
             for q in range(4):
                 total = None
                 for u in range(2):
                     for r in range(4):
-                        lanes = pl.ds(pl.multiple_of(r * tile + b * LANES, LANES), LANES)
-                        term = sqrt_tiles[((t * 4 + q) * 2 + u) * 4 + r] * excite_ref[0, u, :, lanes].astype(jnp.float32)
+                        term = sqrt_tiles[(q * 2 + u) * 4 + r] * spread[u, r]
                         total = term if total is None else total + term
-                acc[t, q] = total
+                acc[h, q] = total
         for j in range(3):
             for m in range(slots):
-                near = picked_ref[pl.ds(j, 8), pl.ds(m * LANES, LANES)]
-                for t in range(2):
+                for h in range(2):
+                    near = picked_ref[pl.ds(8 * h + 2 * j, 8), pl.ds(m * LANES, LANES)]
                     for q in range(4):
-                        acc[t, q] = acc[t, q] + weight_tiles[((t * 4 + q) * 3 + j) * 9 + m] * near
+                        acc[h, q] = acc[h, q] + weight_tiles[(q * 3 + j) * 9 + m] * near
         for q in range(4):
-            lanes = pl.ds(pl.multiple_of(q * tile + b * LANES, LANES), LANES)
-            even = jnp.exp(acc[0, q]) * width_tiles[0]
-            odd = jnp.exp(acc[1, q]) * width_tiles[1]
-            density_ref[0, 0, :, lanes] = even
-            density_ref[0, 1, :, lanes] = odd
-            through = running(even + odd, True)
-            before = shifted(through, 1, True) + even
-            local_ref[0, 0, :, lanes] = before
-            local_ref[0, 1, :, lanes] = through
-            misfit = counts_ref[0, :, lanes] * (before - stars_ref[0, :, lanes]) + counts_ref[1, :, lanes] * (
-                through - stars_ref[1, :, lanes]
-            )
-            sums_ref[0, 0:1, lanes] = through[7:8]
+            lanes = pl.ds(q * tile + b * LANES, LANES)
+            first = jnp.exp(acc[0, q]) * width_tiles[0]
+            second = jnp.exp(acc[1, q]) * width_tiles[1]
+            density_ref[0, pl.ds(0, 8), lanes] = first
+            density_ref[0, pl.ds(8, 8), lanes] = second
+            low = running(first, True)
+            high = running(second, True) + jnp.broadcast_to(low[7:8], low.shape)
+            local_ref[0, pl.ds(0, 8), lanes] = low
+            local_ref[0, pl.ds(8, 8), lanes] = high
+            misfit = counts_ref[pl.ds(0, 8), lanes] * (low - stars_ref[pl.ds(0, 8), lanes]) + counts_ref[
+                pl.ds(8, 8), lanes
+            ] * (high - stars_ref[pl.ds(8, 8), lanes])
+            sums_ref[0, 0:1, lanes] = high[7:8]
             sums_ref[0, 1:2, lanes] = jnp.sum(misfit, axis=0, keepdims=True)
-        return carry
-
-    lax.fori_loop(0, blocks, one_block, 0, unroll=8)
 
 
 def backward_kernel(
-    sqrt_ref, density_ref, local_ref, carries_ref, counts_ref, stars_ref, extinct_ref, grad_ref
+    sqrt_ref, density_ref, local_ref, carries_ref, counts_ref, stars_ref, extinct_ref, grad_ref, sqrt_tiles
 ):
-    tile = density_ref.shape[3] // 4
+    tile = density_ref.shape[2] // 4
     blocks = tile // LANES
 
-    def one_block(b, carry):
+    @pl.when(pl.program_id(0) == 0)
+    def _():
+        alternating(sqrt_ref, lambda n, u: ((n // 4) * 2 + u) * 4 + n % 4, 2 * 4 * 4, sqrt_tiles)
+
+    for b in range(blocks):
         flow = {}
         for q in range(4):
-            lanes = pl.ds(pl.multiple_of(q * tile + b * LANES, LANES), LANES)
+            lanes = pl.ds(q * tile + b * LANES, LANES)
             into = carries_ref[0, 0:1, lanes]
             past = carries_ref[0, 1:2, lanes]
-            even = local_ref[0, 0, :, lanes] + into
-            odd = local_ref[0, 1, :, lanes] + into
-            extinct_ref[0, 0, :, lanes] = even.astype(extinct_ref.dtype)
-            extinct_ref[0, 1, :, lanes] = odd.astype(extinct_ref.dtype)
-            miss_even = counts_ref[0, :, lanes] * (even - stars_ref[0, :, lanes])
-            miss_odd = counts_ref[1, :, lanes] * (odd - stars_ref[1, :, lanes])
-            behind = running(miss_even + miss_odd, False)
-            back_even = behind + past
-            back_odd = (shifted(behind, 1, False) + miss_odd) + past
-            flow[0, q] = density_ref[0, 0, :, lanes] * back_even
-            flow[1, q] = density_ref[0, 1, :, lanes] * back_odd
-        for u in range(2):
+            low = local_ref[0, pl.ds(0, 8), lanes] + into
+            high = local_ref[0, pl.ds(8, 8), lanes] + into
+            extinct_ref[0, pl.ds(0, 8), lanes] = low.astype(extinct_ref.dtype)
+            extinct_ref[0, pl.ds(8, 8), lanes] = high.astype(extinct_ref.dtype)
+            miss_low = counts_ref[pl.ds(0, 8), lanes] * (low - stars_ref[pl.ds(0, 8), lanes])
+            miss_high = counts_ref[pl.ds(8, 8), lanes] * (high - stars_ref[pl.ds(8, 8), lanes])
+            behind_high = running(miss_high, False)
+            behind_low = running(miss_low, False) + jnp.broadcast_to(behind_high[0:1], behind_high.shape)
+            for h, behind in ((0, behind_low), (1, behind_high)):
+                moving = density_ref[0, pl.ds(8 * h, 8), lanes] * (behind + past)
+                flow[h, q, 0] = paired(moving, True)
+                flow[h, q, 1] = paired(moving, False)
+        for h in range(2):
             for r in range(4):
                 total = None
                 for t in range(2):
                     for q in range(4):
-                        term = sqrt_ref[((t * 4 + q) * 2 + u) * 4 + r] * flow[t, q]
+                        term = sqrt_tiles[(t * 4 + q) * 4 + r] * flow[h, q, t]
                         total = term if total is None else total + term
-                lanes = pl.ds(pl.multiple_of(r * tile + b * LANES, LANES), LANES)
-                grad_ref[0, u, :, lanes] = total
-        return carry
-
-    lax.fori_loop(0, blocks, one_block, 0, unroll=8)
+                grad_ref[0, pl.ds(8 * h, 8), pl.ds(r * tile + b * LANES, LANES)] = total
 
 
 def by_parity(values):
@@ -223,15 +240,15 @@
     windows = jnp.stack(
         [extended[:, :, b * BAND : b * BAND + window] for b in range(blocks)], axis=1
     )
-    pieces = split_three(windows)
-    pieces = jnp.pad(pieces, ((0, 0), (0, 0), (0, 0), (0, 16 - shells), (0, 0)))
-    pieces = pieces.transpose(1, 2, 0, 3, 4).reshape(samples, blocks, 3 * 16, window)
+    rows = 2 * (fine_shells // 2 + 4)
+    windows = jnp.pad(windows, ((0, 0), (0, 0), (0, rows // 2 - shells), (0, 0)))
+    pieces = split_three(jnp.repeat(windows, 2, axis=2))
+    pieces = pieces.transpose(1, 2, 0, 3, 4).reshape(samples, blocks, 3 * rows, window)
     starts = (jnp.arange(blocks, dtype=jnp.int32) * BAND)[None, :, None]
     local = halo_index.reshape(slots, blocks, BAND) - starts
     spots = jnp.arange(window, dtype=jnp.int32)[None, :, None, None]
     onehot = (local.transpose(1, 0, 2)[:, None] == spots).astype(jnp.bfloat16)
     onehot = onehot.reshape(blocks, window, slots * BAND)
-    excite = by_parity(excitations)
     half = fine_shells // 2
     smem = pl.BlockSpec(memory_space=pltpu.SMEM)
     whole = lambda shape: pl.BlockSpec(shape, lambda k: (0,) * len(shape))
@@ -242,27 +259,27 @@
         in_specs=[
             smem,
             smem,
-            per_sample((1, blocks, 48, window)),
+            per_sample((1, blocks, 3 * rows, window)),
             whole((blocks, window, slots * BAND)),
-            per_sample((1, 2, half, fine_pixels)),
-            whole((2, half, fine_pixels)),
-            whole((2, half, fine_pixels)),
+            per_sample((1, fine_shells, fine_pixels)),
+            whole((fine_shells, fine_pixels)),
+            whole((fine_shells, fine_pixels)),
             smem,
         ],
         out_specs=[
-            per_sample((1, 2, half, fine_pixels)),
-            per_sample((1, 2, half, fine_pixels)),
+            per_sample((1, fine_shells, fine_pixels)),
+            per_sample((1, fine_shells, fine_pixels)),
             per_sample((1, 2, fine_pixels)),
         ],
         out_shape=[
-            jax.ShapeDtypeStruct((samples, 2, half, fine_pixels), jnp.float32),
-            jax.ShapeDtypeStruct((samples, 2, half, fine_pixels), jnp.float32),
+            jax.ShapeDtypeStruct((samples, fine_shells, fine_pixels), jnp.float32),
+            jax.ShapeDtypeStruct((samples, fine_shells, fine_pixels), jnp.float32),
             jax.ShapeDtypeStruct((samples, 2, fine_pixels), jnp.float32),
         ],
         scratch_shapes=[
-            pltpu.VMEM((16, slots * BAND), jnp.float32),
-            pltpu.VMEM((2 * 4 * 3 * slots, 8, LANES), jnp.float32),
-            pltpu.VMEM((2 * 4 * 2 * 4, 8, LANES), jnp.float32),
+            pltpu.VMEM((rows, slots * BAND), jnp.float32),
+            pltpu.VMEM((4 * 3 * slots, 8, LANES), jnp.float32),
+            pltpu.VMEM((4 * 2 * 4, 8, LANES), jnp.float32),
             pltpu.VMEM((2, 8, LANES), jnp.float32),
         ],
         interpret=INTERPRET,
@@ -271,40 +288,40 @@
         refine_sqrt.astype(jnp.float32).reshape(-1),
         pieces,
         onehot,
-        excite,
-        by_parity(counts),
-        by_parity(stars),
+        excitations,
+        counts,
+        stars,
         widths,
     )
 
 
 def local_backward(refine_sqrt, density, local_cum, carries, counts, stars):
-    samples, _, half, fine_pixels = density.shape
+    samples, fine_shells, fine_pixels = density.shape
     smem = pl.BlockSpec(memory_space=pltpu.SMEM)
     whole = lambda shape: pl.BlockSpec(shape, lambda k: (0,) * len(shape))
     per_sample = lambda shape: pl.BlockSpec(shape, lambda k: (k,) + (0,) * (len(shape) - 1))
-    extinct, grad = pl.pallas_call(
+    return pl.pallas_call(
         backward_kernel,
         grid=(samples,),
         in_specs=[
             smem,
-            per_sample((1, 2, half, fine_pixels)),
-            per_sample((1, 2, half, fine_pixels)),
+            per_sample((1, fine_shells, fine_pixels)),
+            per_sample((1, fine_shells, fine_pixels)),
             per_sample((1, 2, fine_pixels)),
-            whole((2, half, fine_pixels)),
-            whole((2, half, fine_pixels)),
+            whole((fine_shells, fine_pixels)),
+            whole((fine_shells, fine_pixels)),
         ],
         out_specs=[
-            per_sample((1, 2, half, fine_pixels)),
-            per_sample((1, 2, half, fine_pixels)),
+            per_sample((1, fine_shells, fine_pixels)),
+            per_sample((1, fine_shells, fine_pixels)),
         ],
         out_shape=[
-            jax.ShapeDtypeStruct((samples, 2, half, fine_pixels), jnp.bfloat16),
-            jax.ShapeDtypeStruct((samples, 2, half, fine_pixels), jnp.float32),
-        ],
+            jax.ShapeDtypeStruct((samples, fine_shells, fine_pixels), jnp.bfloat16),
+            jax.ShapeDtypeStruct((samples, fine_shells, fine_pixels), jnp.float32),
+        ],
+        scratch_shapes=[pltpu.VMEM((2 * 4 * 4, 8, LANES), jnp.float32)],
         interpret=INTERPRET,
-    )(refine_sqrt.astype(jnp.float32).reshape(-1), density, local_cum, carries, by_parity(counts), by_parity(stars))
-    return from_parity(extinct), from_parity(grad)
+    )(refine_sqrt.astype(jnp.float32).reshape(-1), density, local_cum, carries, counts, stars)
 
 
 def shards(

time: 117 us -> 115 us (0.983)
  local copies, waits for them, and re-layouts: 22.6 us -> 12.8 us
  other arithmetic: 11.8 us -> 15.4 us
  Pallas kernels: 23.6 us -> 26.5 us
    transpose x4 -> x0, local copies, waits for them, and re-layouts: 6.24 us -> none  [the longest x2 3.39 us: from_parity(): return jnp.swapaxes(values, -2, -3).reshape(lead + (2 * shells, width))]
    unnamed x31 -> x25, local copies, waits for them, and re-layouts: 7.65 us -> 3.22 us
    another operation x1 -> x2, other arithmetic: 0.24 us -> 4.5 us
    pallas_call x1, Pallas kernels: 16.1 us -> 18.8 us  [local_forward(): pl.pallas_call(forward_kernel, grid=(samples,), in_specs=[smem, smem, per...]
    reshape x3 -> x1, local copies, waits for them, and re-layouts: 2.81 us -> 2.75 us  [local_forward(): pieces = split_three(jnp.repeat(windows, 2, axis=2))]
  transfers between devices with their start and end apart: 4 -> 4, of which waited for: 0 -> 1; matrix products, arithmetic and copies ran while one was open for 12% -> 8% of each run, Pallas kernels for 0% -> 0%
where the time goes in v9:
time: 115 us; the launch traced here: 114 us
  blocking collectives  45.7 us (40%)
  Pallas kernels  26.5 us (23%)
  other arithmetic  15.4 us (13%)
  local copies, waits for them, and re-layouts  12.8 us (11%)
  starting transfers between devices  10.9 us (9%)
    all_to_all x1, blocking collectives, block_carries(): mine = lax.all_to_all(packed, axis, 0, 0, tiled=True)  27.9 us
    pallas_call x1, Pallas kernels, local_forward(): pl.pallas_call(forward_kernel, grid=(samples,), in_specs=[smem, smem, per...  18.8 us
    all_to_all x1, blocking collectives, block_carries(): lax.all_to_all(jnp.concatenate([carry_in, carry_out], axis=1), axis, 0, 0...  17.8 us
    pallas_call x1, Pallas kernels, local_backward(): pl.pallas_call(backward_kernel, grid=(samples,), in_specs=[smem, per_samp...  7.71 us
    ppermute x2, starting transfers between devices, with_halo(): lax.ppermute(lax.slice_in_dim(block, block.shape[dim] - width, None, axis...  7.7 us
    convert_element_type x1, other arithmetic, local_forward(): onehot = (local.transpose(1, 0, 2)[:, None] == spots).astype(jnp.bfloat16)  5.75 us
    ppermute x2, starting transfers between devices, with_halo(): lax.ppermute(lax.slice_in_dim(block, 0, width, axis=dim), axis, backward)  3.22 us
    unnamed x25, local copies, waits for them, and re-layouts  3.22 us
  transfers between devices with their start and end apart: 4, of which 1 were waited for; matrix products, arithmetic and copies ran while one was open for 8% of the time, Pallas kernels for 0%

profile of v9, /device:TPU:1, one launch (start us, length us, event | category | flops | bytes accessed | tf_op | source)
XLA Modules:
  0.0 114.3 jit_solution(10186671497886900924)
XLA Ops:
  0.6 1.0 copy.58
  1.6 4.5 %collective-permute-start = (f32[8,1,8,128]{3,2,1,0:T(8,128)S(1)}, f32[8,1,8,128]{3,2,1,0:T(8,128)S(1)}, u32[]{:S(2)}, u32[]{:S(2)}) collective-permute-start(f32[8,1,8,128]{3,2,1,0:T(8,128)S(1)} %get-tuple-element.20), channel_id=1, source_target_pairs={{0,4},{4,8},{8,12},{12,16},{16,20},{20,24},{24,28},{28,32},{32,36}... | collective-permute-start | bytes 98312 | tf_op jit(solution)/shard_map/ppermute | solution.py:19
  6.2 1.9 %collective-permute-start.1 = (f32[8,1,8,128]{3,2,1,0:T(8,128)S(1)}, f32[8,1,8,128]{3,2,1,0:T(8,128)S(1)}, u32[]{:S(2)}, u32[]{:S(2)}) collective-permute-start(f32[8,1,8,128]{3,2,1,0:T(8,128)S(1)} %get-tuple-element.19), channel_id=1, source_target_pairs={{4,0},{8,4},{12,8},{16,12},{20,16},{24,20},{28,24},{32,28},{36,32}... | collective-permute-start | bytes 98312 | tf_op jit(solution)/shard_map/ppermute | solution.py:22
  8.1 0.9 copy.51
  9.0 0.1 fusion.10
  9.0 0.0 copy-start.1
  9.1 0.0 copy-start.2
  9.1 5.7 %fusion.onehot_ref = bf16[8,384,1152]{2,1,0:T(8,128)(2,1)} fusion(s32[8,1152]{1,0:T(8,128)S(1)} %fusion.10), kind=kLoop, calls=%fused_computation.1 | loop fusion | flops 7077888 | bytes 7114752 | tf_op jit(solution)/shard_map/convert_element_type | solution.py:250
  14.8 0.0 copy-done.1
  14.9 0.0 collective-permute-done
  14.9 0.0 copy-done
  14.9 0.1 constant_dynamic-update-slice_fusion.1
  15.0 0.0 collective-permute-done.1
  15.0 0.1 fusion.19
  15.0 3.2 %collective-permute-start.2 = (f32[8,10,1,128]{3,2,1,0:T(1,128)S(1)}, f32[8,10,1,128]{3,2,1,0:T(1,128)S(1)}, u32[]{:S(2)}, u32[]{:S(2)}) collective-permute-start(f32[8,10,1,128]{3,2,1,0:T(1,128)S(1)} %get-tuple-element.17), channel_id=1, source_target_pairs={{0,1},{1,2},{2,3},{4,5},{5,6},{6,7},{8,9},{9,10},{10,11},{12,13},{... | collective-permute-start | bytes 122888 | tf_op jit(solution)/shard_map/ppermute | solution.py:19
  18.2 1.3 %collective-permute-start.3 = (f32[8,10,1,128]{3,2,1,0:T(1,128)S(1)}, f32[8,10,1,128]{3,2,1,0:T(1,128)S(1)}, u32[]{:S(2)}, u32[]{:S(2)}) collective-permute-start(f32[8,10,1,128]{3,2,1,0:T(1,128)S(1)} %get-tuple-element.18), channel_id=1, source_target_pairs={{1,0},{2,1},{3,2},{5,4},{6,5},{7,6},{9,8},{10,9},{11,10},{13,12},{... | collective-permute-start | bytes 122888 | tf_op jit(solution)/shard_map/ppermute | solution.py:22
  19.5 0.6 exponential_multiply_fusion.widths_ref
  20.1 0.7 convert_element_type.17.counts_ref
  20.8 0.0 copy-done.3
  20.8 0.6 reshape.105.sqrt_ref
  21.4 0.0 copy-done.2
  21.5 0.7 reshape.96.weights_ref
  22.1 0.1 concatenate.23
  22.2 0.0 collective-permute-done.2
  22.2 0.8 collective-permute-done.3
  23.0 0.1 pad_maximum_fusion.1
  23.1 0.2 copy.57
  23.5 0.3 copy.49
  23.8 0.1 pad.4.clone
  23.9 0.8 broadcast_in_dim.2
  24.7 2.8 %reshape.99 = f32[1,8,8,24,384]{4,3,0,2,1:T(8,128)} reshape(f32[8,8,12,2,384]{4,3,2,1,0:T(2,128)S(1)} %broadcast_in_dim.2) | data formatting | bytes 4718592 | tf_op jit(solution)/shard_map/reshape | solution.py:245
  27.5 2.4 %reduce-precision_convert_fusion.1 = (bf16[1,8,8,24,384]{4,3,0,2,1:T(8,128)(2,1)S(1)}, bf16[1,8,8,24,384]{4,3,0,2,1:T(8,128)(2,1)S(1)}, bf16[1,8,8,24,384]{4,3,0,2,1:T(8,128)(2,1)S(1)}) fusion(f32[1,8,8,24,384]{4,3,0,2,1:T(8,128)} %reshape.99), kind=kLoop, calls=%fused_computation.6 | loop fusion | flops 4128768 | bytes 5898240 | tf_op jit(solution)/shard_map/convert.1
  29.9 2.1 %pad_maximum_fusion = bf16[3,8,8,24,384]{4,3,0,2,1:T(8,128)(2,1)} fusion(bf16[1,8,8,24,384]{4,3,0,2,1:T(8,128)(2,1)S(1)} %get-tuple-element.11, bf16[1,8,8,24,384]{4,3,0,2,1:T(8,128)(2,1)S(1)} %get-tuple-element.12, bf16[1,8,8,24,384]{4,3,0,2,1:T(8,128)(2,1)S(1)} %get-tuple-element.10), kind=kLoop, calls=%fused_computation.2 | loop fusion | flops 3538944 | bytes 7077888 | tf_op jit(solution)/shard_map/stack | solution.py:54
  32.0 18.8 %shard_map.86 = (f32[8,16,4096]{2,1,0:T(8,128)}, f32[8,16,4096]{2,1,0:T(8,128)}, f32[8,2,4096]{2,1,0:T(2,128)}) custom-call(f32[216]{0:T(256)} %reshape.96.weights_ref, f32[64]{0:T(128)} %reshape.105.sqrt_ref, bf16[8,8,72,384]{3,2,1,0:T(8,128)(2,1)} %bitcast.72, bf16[8,384,1152]{2,1,0:T(8,128)(2,1)} %fusion.onehot_ref, bf16[8,16,4096]{2,1,0:T(8,128)(2,1)} %excite_ref.1, ...), custom_call_target="tpu_custom_call" | custom-call | tf_op jit(solution)/shard_map/pallas_call | solution.py:256
  50.8 1.7 %slice_reduce_fusion.1 = (f32[8,4096]{1,0:T(8,128)S(1)}, f32[8,4096]{1,0:T(8,128)S(1)}) fusion(f32[8,2,4096]{2,1,0:T(2,128)} %get-tuple-element.7), kind=kLoop, calls=%fused_computation.16 | loop fusion | bytes 524288 | tf_op jit(solution)/shard_map/slice | solution.py:347
  52.5 0.1 concatenate.21
  52.7 0.2 copy.35
  52.8 0.1 concatenate.22
  52.9 0.2 copy.36
  53.1 0.1 maximum_bitcast_fusion
  53.2 0.4 reshape.110
  53.5 27.9 %all_to_all.10 = f32[64,1,1088]{2,1,0:T(1,128)S(1)} all-to-all(f32[64,1,1088]{2,1,0:T(1,128)S(1)} %reshape.110), channel_id=1, replica_groups=mesh['dist'=64,'sky'=4] {'dist'}, dimensions={0} | all-to-all | bytes 557056 | tf_op jit(solution)/shard_map/all_to_all | solution.py:33
  81.5 0.5 broadcast.31
  82.0 1.3 %reduce.4 = f32[64,1088]{1,0:T(8,128)S(1)} reduce(f32[64,1,1088]{2,1,0:T(1,128)S(1)} %all_to_all.10, f32[]{:T(128)} %broadcast.31), dimensions={1}, to_apply=%all_to_all.6.reduce_sub_computation | reduce | bytes 557060 | tf_op jit(solution)/shard_map/all_to_all | solution.py:33
  83.3 0.1 reshape.111
  83.5 0.1 reshape.102
  83.7 0.1 copy.37
  83.8 0.5 copy_add_fusion
  84.3 0.2 copy.40
  84.5 0.1 reshape.103
  84.6 0.1 copy.47
  84.7 0.5 fusion.12
  85.2 0.1 pad_maximum_fusion.2
  85.3 0.3 copy.42
  85.6 0.3 reshape.112
  85.9 17.8 %all_to_all.11 = f32[64,1,1024]{2,1,0:T(1,128)S(1)} all-to-all(f32[64,1,1024]{2,1,0:T(1,128)S(1)} %reshape.112), channel_id=1, replica_groups=mesh['dist'=64,'sky'=4] {'dist'}, dimensions={0} | all-to-all | bytes 524288 | tf_op jit(solution)/shard_map/all_to_all | solution.py:44
  103.8 1.3 %reduce.5 = f32[64,1024]{1,0:T(8,128)S(1)} reduce(f32[64,1,1024]{2,1,0:T(1,128)S(1)} %all_to_all.11, f32[]{:T(128)} %broadcast.31), dimensions={1}, to_apply=%all_to_all.7.reduce_sub_computation | reduce | bytes 524292 | tf_op jit(solution)/shard_map/all_to_all | solution.py:44
  105.0 0.1 reshape.113
  105.2 0.1 copy.43
  105.3 0.2 stack.53
  105.4 0.1 copy.44
  105.5 0.2 stack.54
  105.7 0.9 pad_maximum_fusion.3.carries_ref
  106.6 7.7 %shard_map.87 = (bf16[8,16,4096]{2,1,0:T(8,128)(2,1)}, f32[8,16,4096]{2,1,0:T(8,128)}) custom-call(f32[64]{0:T(128)} %reshape.105.sqrt_ref, f32[8,16,4096]{2,1,0:T(8,128)} %get-tuple-element.5.density_ref, f32[8,16,4096]{2,1,0:T(8,128)} %get-tuple-element.6.local_ref, f32[8,2,4096]{2,1,0:T(2,128)} %pad_maximum_fusion.3.carries_ref, ...), custom_call_target="tpu_custom_call" | custom-call | tf_op jit(solution)/shard_map/pallas_call | solution.py:303
  (19 shorter events, 0.3 us)
Async XLA Ops:
  1.6 13.2 %collective-permute-start = (f32[8,1,8,128]{3,2,1,0:T(8,128)S(1)}, f32[8,1,8,128]{3,2,1,0:T(8,128)S(1)}, u32[]{:S(2)}, u32[]{:S(2)}) collective-permute-start(f32[8,1,8,128]{3,2,1,0:T(8,128)S(1)} %get-tuple-element.20), channel_id=1, source_target_pairs={{0,4},{4,8},{8,12},{12,16},{16,20},{20,24},{24,28},{28,32},{32,36}... | collective-permute-start | bytes 98312 | tf_op jit(solution)/shard_map/ppermute | solution.py:19
  6.2 8.8 %collective-permute-start.1 = (f32[8,1,8,128]{3,2,1,0:T(8,128)S(1)}, f32[8,1,8,128]{3,2,1,0:T(8,128)S(1)}, u32[]{:S(2)}, u32[]{:S(2)}) collective-permute-start(f32[8,1,8,128]{3,2,1,0:T(8,128)S(1)} %get-tuple-element.19), channel_id=1, source_target_pairs={{4,0},{8,4},{12,8},{16,12},{20,16},{24,20},{28,24},{32,28},{36,32}... | collective-permute-start | bytes 98312 | tf_op jit(solution)/shard_map/ppermute | solution.py:22
  9.0 5.8 %copy-start.1 = (s32[16,4096]{1,0:T(8,128)S(1)}, s32[16,4096]{1,0:T(8,128)}, u32[]{:S(2)}) copy-start(s32[16,4096]{1,0:T(8,128)} %param.13) | copy-start | bytes 786436
  9.0 5.9 %copy-start = (f32[8,8,1024]{2,1,0:T(8,128)S(1)}, f32[8,8,1024]{2,1,0:T(8,128)}, u32[]{:S(2)}) copy-start(f32[8,8,1024]{2,1,0:T(8,128)} %param.7) | copy-start | bytes 786436
  9.1 11.8 %copy-start.3 = (bf16[2,4,2,4]{3,2,1,0:T(2,128)(2,1)S(1)}, bf16[2,4,2,4]{3,2,1,0:T(2,128)(2,1)}, u32[]{:S(2)}) copy-start(bf16[2,4,2,4]{3,2,1,0:T(2,128)(2,1)} %param.10) | copy-start | bytes 388
  9.1 12.4 %copy-start.2 = (f32[2,4,3,9]{3,1,2,0:T(4,128)S(1)}, f32[2,4,3,9]{3,1,2,0:T(4,128)}, u32[]{:S(2)}) copy-start(f32[2,4,3,9]{3,1,2,0:T(4,128)} %param.9) | copy-start | bytes 2596
  15.0 7.2 %collective-permute-start.2 = (f32[8,10,1,128]{3,2,1,0:T(1,128)S(1)}, f32[8,10,1,128]{3,2,1,0:T(1,128)S(1)}, u32[]{:S(2)}, u32[]{:S(2)}) collective-permute-start(f32[8,10,1,128]{3,2,1,0:T(1,128)S(1)} %get-tuple-element.17), channel_id=1, source_target_pairs={{0,1},{1,2},{2,3},{4,5},{5,6},{6,7},{8,9},{9,10},{10,11},{12,13},{... | collective-permute-start | bytes 122888 | tf_op jit(solution)/shard_map/ppermute | solution.py:19
  18.2 4.7 %collective-permute-start.3 = (f32[8,10,1,128]{3,2,1,0:T(1,128)S(1)}, f32[8,10,1,128]{3,2,1,0:T(1,128)S(1)}, u32[]{:S(2)}, u32[]{:S(2)}) collective-permute-start(f32[8,10,1,128]{3,2,1,0:T(1,128)S(1)} %get-tuple-element.18), channel_id=1, source_target_pairs={{1,0},{2,1},{3,2},{5,4},{6,5},{7,6},{9,8},{10,9},{11,10},{13,12},{... | collective-permute-start | bytes 122888 | tf_op jit(solution)/shard_map/ppermute | solution.py:22

commit v10 on v9

--- a/solution.py
+++ b/solution.py
@@ -237,12 +237,11 @@
     window = 3 * BAND
     fine_shells = excitations.shape[1]
     fine_pixels = excitations.shape[2]
-    windows = jnp.stack(
-        [extended[:, :, b * BAND : b * BAND + window] for b in range(blocks)], axis=1
-    )
     rows = 2 * (fine_shells // 2 + 4)
-    windows = jnp.pad(windows, ((0, 0), (0, 0), (0, rows // 2 - shells), (0, 0)))
-    pieces = split_three(jnp.repeat(windows, 2, axis=2))
+    split = split_three(extended)
+    split = jnp.pad(split, ((0, 0), (0, 0), (0, rows // 2 - shells), (0, 0)))
+    split = jnp.repeat(split, 2, axis=2)
+    pieces = jnp.stack([split[:, :, :, b * BAND : b * BAND + window] for b in range(blocks)], axis=2)
     pieces = pieces.transpose(1, 2, 0, 3, 4).reshape(samples, blocks, 3 * rows, window)
     starts = (jnp.arange(blocks, dtype=jnp.int32) * BAND)[None, :, None]
     local = halo_index.reshape(slots, blocks, BAND) - starts

time: 115 us -> 110 us (0.957)
  other arithmetic: 15.4 us -> 11.3 us
    unnamed x25 -> x27, local copies, waits for them, and re-layouts: 3.22 us -> 5.42 us
    another operation x1, other arithmetic: 2.43 us -> 0.25 us
    reshape x1, local copies, waits for them, and re-layouts: 2.75 us -> 0.6 us  [local_forward(): split = jnp.repeat(split, 2, axis=2)]
    another operation x1, other arithmetic: 2.07 us -> 0.07 us  [split_three(): return jnp.stack([high, middle, low]).astype(jnp.bfloat16)]
  transfers between devices with their start and end apart: 4 -> 4, of which waited for: 1 -> 1; matrix products, arithmetic and copies ran while one was open for 8% -> 9% of each run, Pallas kernels for 0% -> 0%
where the time goes in v10:
time: 110 us
  blocking collectives  45.7 us (42%)
  Pallas kernels  26.5 us (24%)
  local copies, waits for them, and re-layouts  12.7 us (12%)
  other arithmetic  11.3 us (10%)
  starting transfers between devices  10.9 us (10%)
    all_to_all x1, blocking collectives, block_carries(): mine = lax.all_to_all(packed, axis, 0, 0, tiled=True)  27.9 us
    pallas_call x1, Pallas kernels, local_forward(): pl.pallas_call(forward_kernel, grid=(samples,), in_specs=[smem, smem, per...  18.8 us
    all_to_all x1, blocking collectives, block_carries(): lax.all_to_all(jnp.concatenate([carry_in, carry_out], axis=1), axis, 0, 0...  17.8 us
    pallas_call x1, Pallas kernels, local_backward(): pl.pallas_call(backward_kernel, grid=(samples,), in_specs=[smem, per_samp...  7.71 us
    ppermute x2, starting transfers between devices, with_halo(): lax.ppermute(lax.slice_in_dim(block, block.shape[dim] - width, None, axis...  7.7 us
    convert_element_type x1, other arithmetic, local_forward(): onehot = (local.transpose(1, 0, 2)[:, None] == spots).astype(jnp.bfloat16)  5.74 us
    unnamed x27, local copies, waits for them, and re-layouts  5.42 us
    ppermute x2, starting transfers between devices, with_halo(): lax.ppermute(lax.slice_in_dim(block, 0, width, axis=dim), axis, backward)  3.22 us
  transfers between devices with their start and end apart: 4, of which 1 were waited for; matrix products, arithmetic and copies ran while one was open for 9% of the time, Pallas kernels for 0%

profile of v10, /device:TPU:1, one launch (start us, length us, event | category | flops | bytes accessed | tf_op | source)
XLA Modules:
  0.0 110.0 jit_solution(12858643440364703138)
XLA Ops:
  0.6 1.0 copy.80
  1.6 4.5 %collective-permute-start = (f32[8,1,8,128]{3,2,1,0:T(8,128)S(1)}, f32[8,1,8,128]{3,2,1,0:T(8,128)S(1)}, u32[]{:S(2)}, u32[]{:S(2)}) collective-permute-start(f32[8,1,8,128]{3,2,1,0:T(8,128)S(1)} %get-tuple-element.20), channel_id=1, source_target_pairs={{0,4},{4,8},{8,12},{12,16},{16,20},{20,24},{24,28},{28,32},{32,36}... | collective-permute-start | bytes 98312 | tf_op jit(solution)/shard_map/ppermute | solution.py:19
  6.2 1.9 %collective-permute-start.1 = (f32[8,1,8,128]{3,2,1,0:T(8,128)S(1)}, f32[8,1,8,128]{3,2,1,0:T(8,128)S(1)}, u32[]{:S(2)}, u32[]{:S(2)}) collective-permute-start(f32[8,1,8,128]{3,2,1,0:T(8,128)S(1)} %get-tuple-element.19), channel_id=1, source_target_pairs={{4,0},{8,4},{12,8},{16,12},{20,16},{24,20},{28,24},{32,28},{36,32}... | collective-permute-start | bytes 98312 | tf_op jit(solution)/shard_map/ppermute | solution.py:22
  8.1 0.9 copy.72
  9.0 0.1 fusion.10
  9.1 0.0 copy-start.3
  9.1 5.7 %fusion.onehot_ref = bf16[8,384,1152]{2,1,0:T(8,128)(2,1)} fusion(s32[8,1152]{1,0:T(8,128)S(1)} %fusion.10), kind=kLoop, calls=%fused_computation.1 | loop fusion | flops 7077888 | bytes 7114752 | tf_op jit(solution)/shard_map/convert_element_type | solution.py:249
  14.9 0.1 constant_dynamic-update-slice_fusion.1
  15.0 0.1 fusion.19
  15.0 3.2 %collective-permute-start.2 = (f32[8,10,1,128]{3,2,1,0:T(1,128)S(1)}, f32[8,10,1,128]{3,2,1,0:T(1,128)S(1)}, u32[]{:S(2)}, u32[]{:S(2)}) collective-permute-start(f32[8,10,1,128]{3,2,1,0:T(1,128)S(1)} %get-tuple-element.17), channel_id=1, source_target_pairs={{0,1},{1,2},{2,3},{4,5},{5,6},{6,7},{8,9},{9,10},{10,11},{12,13},{... | collective-permute-start | bytes 122888 | tf_op jit(solution)/shard_map/ppermute | solution.py:19
  18.2 1.3 %collective-permute-start.3 = (f32[8,10,1,128]{3,2,1,0:T(1,128)S(1)}, f32[8,10,1,128]{3,2,1,0:T(1,128)S(1)}, u32[]{:S(2)}, u32[]{:S(2)}) collective-permute-start(f32[8,10,1,128]{3,2,1,0:T(1,128)S(1)} %get-tuple-element.18), channel_id=1, source_target_pairs={{1,0},{2,1},{3,2},{5,4},{6,5},{7,6},{9,8},{10,9},{11,10},{13,12},{... | collective-permute-start | bytes 122888 | tf_op jit(solution)/shard_map/ppermute | solution.py:22
  19.5 0.6 exponential_multiply_fusion.widths_ref
  20.2 0.7 convert_element_type.17.counts_ref
  20.9 0.6 reshape.105.sqrt_ref
  21.5 0.7 reshape.96.weights_ref
  22.2 0.1 concatenate.23
  22.3 0.7 collective-permute-done.3
  23.0 0.1 pad_maximum_fusion
  23.1 0.2 reduce-precision_convert_fusion.1
  23.4 0.1 pad_maximum_fusion.1
  23.4 0.1 copy.70
  23.6 0.1 pad.4.clone
  23.7 0.8 broadcast_in_dim.2
  24.5 0.6 reshape.99
  25.1 0.1 fusion.8
  25.1 0.1 fusion.7
  25.2 0.1 fusion.6
  25.3 0.1 fusion.5
  25.4 0.1 fusion.4
  25.5 0.1 fusion.3
  25.6 0.1 fusion.2
  25.7 0.1 fusion.1
  25.8 1.8 %copy-done = bf16[3,8,8,24,384]{4,3,0,2,1:T(8,128)(2,1)} copy-done((bf16[3,8,8,24,384]{4,3,0,2,1:T(8,128)(2,1)}, bf16[3,8,8,24,384]{4,3,0,2,1:T(8,128)(2,1)S(1)}, u32[]{:S(2)}) %copy-start) | copy-done | bytes 3538968
  27.6 18.8 %shard_map.86 = (f32[8,16,4096]{2,1,0:T(8,128)}, f32[8,16,4096]{2,1,0:T(8,128)}, f32[8,2,4096]{2,1,0:T(2,128)}) custom-call(f32[216]{0:T(256)} %reshape.96.weights_ref, f32[64]{0:T(128)} %reshape.105.sqrt_ref, bf16[8,8,72,384]{3,2,1,0:T(8,128)(2,1)} %bitcast.92, bf16[8,384,1152]{2,1,0:T(8,128)(2,1)} %fusion.onehot_ref, bf16[8,16,4096]{2,1,0:T(8,128)(2,1)} %excite_ref.1, ...), custom_call_target="tpu_custom_call" | custom-call | tf_op jit(solution)/shard_map/pallas_call | solution.py:255
  46.4 1.7 %slice_reduce_fusion.1 = (f32[8,4096]{1,0:T(8,128)S(1)}, f32[8,4096]{1,0:T(8,128)S(1)}) fusion(f32[8,2,4096]{2,1,0:T(2,128)} %get-tuple-element.7), kind=kLoop, calls=%fused_computation.31 | loop fusion | bytes 524288 | tf_op jit(solution)/shard_map/slice | solution.py:346
  48.2 0.1 concatenate.21
  48.3 0.2 copy.56
  48.5 0.1 concatenate.22
  48.6 0.2 copy.57
  48.7 0.1 maximum_bitcast_fusion
  48.8 0.4 reshape.110
  49.2 27.9 %all_to_all.10 = f32[64,1,1088]{2,1,0:T(1,128)S(1)} all-to-all(f32[64,1,1088]{2,1,0:T(1,128)S(1)} %reshape.110), channel_id=1, replica_groups=mesh['dist'=64,'sky'=4] {'dist'}, dimensions={0} | all-to-all | bytes 557056 | tf_op jit(solution)/shard_map/all_to_all | solution.py:33
  77.1 0.5 broadcast.31
  77.6 1.3 %reduce.4 = f32[64,1088]{1,0:T(8,128)S(1)} reduce(f32[64,1,1088]{2,1,0:T(1,128)S(1)} %all_to_all.10, f32[]{:T(128)} %broadcast.31), dimensions={1}, to_apply=%all_to_all.6.reduce_sub_computation | reduce | bytes 557060 | tf_op jit(solution)/shard_map/all_to_all | solution.py:33
  79.0 0.1 reshape.111
  79.2 0.1 reshape.102
  79.3 0.1 copy.58
  79.4 0.5 copy_add_fusion
  79.9 0.2 copy.61
  80.1 0.1 reshape.103
  80.2 0.1 copy.68
  80.3 0.5 fusion.12
  80.9 0.1 pad_maximum_fusion.2
  80.9 0.3 copy.63
  81.2 0.3 reshape.112
  81.6 17.8 %all_to_all.11 = f32[64,1,1024]{2,1,0:T(1,128)S(1)} all-to-all(f32[64,1,1024]{2,1,0:T(1,128)S(1)} %reshape.112), channel_id=1, replica_groups=mesh['dist'=64,'sky'=4] {'dist'}, dimensions={0} | all-to-all | bytes 524288 | tf_op jit(solution)/shard_map/all_to_all | solution.py:44
  99.4 1.3 %reduce.5 = f32[64,1024]{1,0:T(8,128)S(1)} reduce(f32[64,1,1024]{2,1,0:T(1,128)S(1)} %all_to_all.11, f32[]{:T(128)} %broadcast.31), dimensions={1}, to_apply=%all_to_all.7.reduce_sub_computation | reduce | bytes 524292 | tf_op jit(solution)/shard_map/all_to_all | solution.py:44
  100.6 0.1 reshape.113
  100.8 0.1 copy.64
  100.9 0.2 stack.53
  101.1 0.1 copy.65
  101.1 0.2 stack.54
  101.3 0.9 pad_maximum_fusion.3.carries_ref
  102.2 7.7 %shard_map.87 = (bf16[8,16,4096]{2,1,0:T(8,128)(2,1)}, f32[8,16,4096]{2,1,0:T(8,128)}) custom-call(f32[64]{0:T(128)} %reshape.105.sqrt_ref, f32[8,16,4096]{2,1,0:T(8,128)} %get-tuple-element.5.density_ref, f32[8,16,4096]{2,1,0:T(8,128)} %get-tuple-element.6.local_ref, f32[8,2,4096]{2,1,0:T(2,128)} %pad_maximum_fusion.3.carries_ref, ...), custom_call_target="tpu_custom_call" | custom-call | tf_op jit(solution)/shard_map/pallas_call | solution.py:302
  (20 shorter events, 0.2 us)
Async XLA Ops:
  1.6 13.2 %collective-permute-start = (f32[8,1,8,128]{3,2,1,0:T(8,128)S(1)}, f32[8,1,8,128]{3,2,1,0:T(8,128)S(1)}, u32[]{:S(2)}, u32[]{:S(2)}) collective-permute-start(f32[8,1,8,128]{3,2,1,0:T(8,128)S(1)} %get-tuple-element.20), channel_id=1, source_target_pairs={{0,4},{4,8},{8,12},{12,16},{16,20},{20,24},{24,28},{28,32},{32,36}... | collective-permute-start | bytes 98312 | tf_op jit(solution)/shard_map/ppermute | solution.py:19
  6.2 8.8 %collective-permute-start.1 = (f32[8,1,8,128]{3,2,1,0:T(8,128)S(1)}, f32[8,1,8,128]{3,2,1,0:T(8,128)S(1)}, u32[]{:S(2)}, u32[]{:S(2)}) collective-permute-start(f32[8,1,8,128]{3,2,1,0:T(8,128)S(1)} %get-tuple-element.19), channel_id=1, source_target_pairs={{4,0},{8,4},{12,8},{16,12},{20,16},{24,20},{28,24},{32,28},{36,32}... | collective-permute-start | bytes 98312 | tf_op jit(solution)/shard_map/ppermute | solution.py:22
  9.0 5.8 %copy-start.2 = (s32[16,4096]{1,0:T(8,128)S(1)}, s32[16,4096]{1,0:T(8,128)}, u32[]{:S(2)}) copy-start(s32[16,4096]{1,0:T(8,128)} %param.13) | copy-start | bytes 786436
  9.0 5.8 %copy-start.1 = (f32[8,8,1024]{2,1,0:T(8,128)S(1)}, f32[8,8,1024]{2,1,0:T(8,128)}, u32[]{:S(2)}) copy-start(f32[8,8,1024]{2,1,0:T(8,128)} %param.7) | copy-start | bytes 786436
  9.1 11.8 %copy-start.4 = (bf16[2,4,2,4]{3,2,1,0:T(2,128)(2,1)S(1)}, bf16[2,4,2,4]{3,2,1,0:T(2,128)(2,1)}, u32[]{:S(2)}) copy-start(bf16[2,4,2,4]{3,2,1,0:T(2,128)(2,1)} %param.10) | copy-start | bytes 388
  9.1 12.5 %copy-start.3 = (f32[2,4,3,9]{3,1,2,0:T(4,128)S(1)}, f32[2,4,3,9]{3,1,2,0:T(4,128)}, u32[]{:S(2)}) copy-start(f32[2,4,3,9]{3,1,2,0:T(4,128)} %param.9) | copy-start | bytes 2596
  15.0 7.2 %collective-permute-start.2 = (f32[8,10,1,128]{3,2,1,0:T(1,128)S(1)}, f32[8,10,1,128]{3,2,1,0:T(1,128)S(1)}, u32[]{:S(2)}, u32[]{:S(2)}) collective-permute-start(f32[8,10,1,128]{3,2,1,0:T(1,128)S(1)} %get-tuple-element.17), channel_id=1, source_target_pairs={{0,1},{1,2},{2,3},{4,5},{5,6},{6,7},{8,9},{9,10},{10,11},{12,13},{... | collective-permute-start | bytes 122888 | tf_op jit(solution)/shard_map/ppermute | solution.py:19
  18.2 4.7 %collective-permute-start.3 = (f32[8,10,1,128]{3,2,1,0:T(1,128)S(1)}, f32[8,10,1,128]{3,2,1,0:T(1,128)S(1)}, u32[]{:S(2)}, u32[]{:S(2)}) collective-permute-start(f32[8,10,1,128]{3,2,1,0:T(1,128)S(1)} %get-tuple-element.18), channel_id=1, source_target_pairs={{1,0},{2,1},{3,2},{5,4},{6,5},{7,6},{9,8},{10,9},{11,10},{13,12},{... | collective-permute-start | bytes 122888 | tf_op jit(solution)/shard_map/ppermute | solution.py:22
  25.8 1.8 %copy-start = (bf16[3,8,8,24,384]{4,3,0,2,1:T(8,128)(2,1)}, bf16[3,8,8,24,384]{4,3,0,2,1:T(8,128)(2,1)S(1)}, u32[]{:S(2)}) copy-start(bf16[3,8,8,24,384]{4,3,0,2,1:T(8,128)(2,1)S(1)} %fusion.1) | copy-start | bytes 10616836

commit v11 on v10

--- a/solution.py
+++ b/solution.py
@@ -81,15 +81,9 @@
 def shifted(values, amount, toward_end):
     rows = values.shape[0]
     row = lax.broadcasted_iota(jnp.int32, values.shape, 0)
-    forward = pltpu.roll(values, amount, 0)
-    backward = pltpu.roll(values, rows - amount, 0)
-    probe = pltpu.roll(row, amount, 0)
-    plain = probe == jnp.where(row >= amount, row - amount, row + rows - amount)
     if toward_end:
-        moved = jnp.where(plain, forward, backward)
-        return jnp.where(row >= amount, moved, 0.0)
-    moved = jnp.where(plain, backward, forward)
-    return jnp.where(row < rows - amount, moved, 0.0)
+        return jnp.where(row >= amount, pltpu.roll(values, amount, 0), 0.0)
+    return jnp.where(row < rows - amount, pltpu.roll(values, rows - amount, 0), 0.0)
 
 
 def running(values, toward_end):

time: 110 us -> 110 us (level)
  no operation moved by 1% of the time
where the time goes in v11:
time: 110 us; the launch traced here: 109 us
  blocking collectives  45.7 us (42%)
  Pallas kernels  26 us (24%)
  local copies, waits for them, and re-layouts  12.7 us (12%)
  other arithmetic  11.3 us (10%)
  starting transfers between devices  10.9 us (10%)
    all_to_all x1, blocking collectives, block_carries(): mine = lax.all_to_all(packed, axis, 0, 0, tiled=True)  27.9 us
    pallas_call x1, Pallas kernels, local_forward(): pl.pallas_call(forward_kernel, grid=(samples,), in_specs=[smem, smem, per...  18.4 us
    all_to_all x1, blocking collectives, block_carries(): lax.all_to_all(jnp.concatenate([carry_in, carry_out], axis=1), axis, 0, 0...  17.8 us
    ppermute x2, starting transfers between devices, with_halo(): lax.ppermute(lax.slice_in_dim(block, block.shape[dim] - width, None, axis...  7.7 us
    pallas_call x1, Pallas kernels, local_backward(): pl.pallas_call(backward_kernel, grid=(samples,), in_specs=[smem, per_samp...  7.53 us
    convert_element_type x1, other arithmetic, local_forward(): onehot = (local.transpose(1, 0, 2)[:, None] == spots).astype(jnp.bfloat16)  5.74 us
    unnamed x27, local copies, waits for them, and re-layouts  5.42 us
    ppermute x2, starting transfers between devices, with_halo(): lax.ppermute(lax.slice_in_dim(block, 0, width, axis=dim), axis, backward)  3.22 us
  transfers between devices with their start and end apart: 4, of which 1 were waited for; matrix products, arithmetic and copies ran while one was open for 9% of the time, Pallas kernels for 0%

profile of v11, /device:TPU:1, one launch (start us, length us, event | category | flops | bytes accessed | tf_op | source)
XLA Modules:
  0.0 109.4 jit_solution(8587683307193453990)
XLA Ops:
  0.6 1.0 copy.80
  1.6 4.5 %collective-permute-start = (f32[8,1,8,128]{3,2,1,0:T(8,128)S(1)}, f32[8,1,8,128]{3,2,1,0:T(8,128)S(1)}, u32[]{:S(2)}, u32[]{:S(2)}) collective-permute-start(f32[8,1,8,128]{3,2,1,0:T(8,128)S(1)} %get-tuple-element.20), channel_id=1, source_target_pairs={{0,4},{4,8},{8,12},{12,16},{16,20},{20,24},{24,28},{28,32},{32,36}... | collective-permute-start | bytes 98312 | tf_op jit(solution)/shard_map/ppermute | solution.py:19
  6.2 1.9 %collective-permute-start.1 = (f32[8,1,8,128]{3,2,1,0:T(8,128)S(1)}, f32[8,1,8,128]{3,2,1,0:T(8,128)S(1)}, u32[]{:S(2)}, u32[]{:S(2)}) collective-permute-start(f32[8,1,8,128]{3,2,1,0:T(8,128)S(1)} %get-tuple-element.19), channel_id=1, source_target_pairs={{4,0},{8,4},{12,8},{16,12},{20,16},{24,20},{28,24},{32,28},{36,32}... | collective-permute-start | bytes 98312 | tf_op jit(solution)/shard_map/ppermute | solution.py:22
  8.1 0.9 copy.72
  9.0 0.1 fusion.10
  9.1 0.0 copy-start.3
  9.1 5.7 %fusion.onehot_ref = bf16[8,384,1152]{2,1,0:T(8,128)(2,1)} fusion(s32[8,1152]{1,0:T(8,128)S(1)} %fusion.10), kind=kLoop, calls=%fused_computation.1 | loop fusion | flops 7077888 | bytes 7114752 | tf_op jit(solution)/shard_map/convert_element_type | solution.py:243
  14.9 0.1 constant_dynamic-update-slice_fusion.1
  15.0 0.1 fusion.19
  15.0 3.2 %collective-permute-start.2 = (f32[8,10,1,128]{3,2,1,0:T(1,128)S(1)}, f32[8,10,1,128]{3,2,1,0:T(1,128)S(1)}, u32[]{:S(2)}, u32[]{:S(2)}) collective-permute-start(f32[8,10,1,128]{3,2,1,0:T(1,128)S(1)} %get-tuple-element.17), channel_id=1, source_target_pairs={{0,1},{1,2},{2,3},{4,5},{5,6},{6,7},{8,9},{9,10},{10,11},{12,13},{... | collective-permute-start | bytes 122888 | tf_op jit(solution)/shard_map/ppermute | solution.py:19
  18.2 1.3 %collective-permute-start.3 = (f32[8,10,1,128]{3,2,1,0:T(1,128)S(1)}, f32[8,10,1,128]{3,2,1,0:T(1,128)S(1)}, u32[]{:S(2)}, u32[]{:S(2)}) collective-permute-start(f32[8,10,1,128]{3,2,1,0:T(1,128)S(1)} %get-tuple-element.18), channel_id=1, source_target_pairs={{1,0},{2,1},{3,2},{5,4},{6,5},{7,6},{9,8},{10,9},{11,10},{13,12},{... | collective-permute-start | bytes 122888 | tf_op jit(solution)/shard_map/ppermute | solution.py:22
  19.5 0.6 exponential_multiply_fusion.widths_ref
  20.2 0.7 convert_element_type.17.counts_ref
  20.9 0.6 reshape.105.sqrt_ref
  21.5 0.7 reshape.96.weights_ref
  22.2 0.1 concatenate.23
  22.3 0.7 collective-permute-done.3
  23.0 0.1 pad_maximum_fusion
  23.1 0.2 reduce-precision_convert_fusion.1
  23.4 0.1 pad_maximum_fusion.1
  23.4 0.1 copy.70
  23.6 0.1 pad.4.clone
  23.7 0.8 broadcast_in_dim.2
  24.5 0.6 reshape.99
  25.1 0.1 fusion.8
  25.1 0.1 fusion.7
  25.2 0.1 fusion.6
  25.3 0.1 fusion.5
  25.4 0.1 fusion.4
  25.5 0.1 fusion.3
  25.6 0.1 fusion.2
  25.7 0.1 fusion.1
  25.8 1.8 %copy-done = bf16[3,8,8,24,384]{4,3,0,2,1:T(8,128)(2,1)} copy-done((bf16[3,8,8,24,384]{4,3,0,2,1:T(8,128)(2,1)}, bf16[3,8,8,24,384]{4,3,0,2,1:T(8,128)(2,1)S(1)}, u32[]{:S(2)}) %copy-start) | copy-done | bytes 3538968
  27.6 18.4 %shard_map.86 = (f32[8,16,4096]{2,1,0:T(8,128)}, f32[8,16,4096]{2,1,0:T(8,128)}, f32[8,2,4096]{2,1,0:T(2,128)}) custom-call(f32[216]{0:T(256)} %reshape.96.weights_ref, f32[64]{0:T(128)} %reshape.105.sqrt_ref, bf16[8,8,72,384]{3,2,1,0:T(8,128)(2,1)} %bitcast.92, bf16[8,384,1152]{2,1,0:T(8,128)(2,1)} %fusion.onehot_ref, bf16[8,16,4096]{2,1,0:T(8,128)(2,1)} %excite_ref.1, ...), custom_call_target="tpu_custom_call" | custom-call | tf_op jit(solution)/shard_map/pallas_call | solution.py:249
  46.0 1.7 %slice_reduce_fusion.1 = (f32[8,4096]{1,0:T(8,128)S(1)}, f32[8,4096]{1,0:T(8,128)S(1)}) fusion(f32[8,2,4096]{2,1,0:T(2,128)} %get-tuple-element.7), kind=kLoop, calls=%fused_computation.31 | loop fusion | bytes 524288 | tf_op jit(solution)/shard_map/slice | solution.py:340
  47.8 0.1 concatenate.21
  47.9 0.2 copy.56
  48.0 0.1 concatenate.22
  48.1 0.2 copy.57
  48.3 0.1 maximum_bitcast_fusion
  48.4 0.4 reshape.110
  48.8 27.9 %all_to_all.10 = f32[64,1,1088]{2,1,0:T(1,128)S(1)} all-to-all(f32[64,1,1088]{2,1,0:T(1,128)S(1)} %reshape.110), channel_id=1, replica_groups=mesh['dist'=64,'sky'=4] {'dist'}, dimensions={0} | all-to-all | bytes 557056 | tf_op jit(solution)/shard_map/all_to_all | solution.py:33
  76.7 0.5 broadcast.31
  77.2 1.3 %reduce.4 = f32[64,1088]{1,0:T(8,128)S(1)} reduce(f32[64,1,1088]{2,1,0:T(1,128)S(1)} %all_to_all.10, f32[]{:T(128)} %broadcast.31), dimensions={1}, to_apply=%all_to_all.6.reduce_sub_computation | reduce | bytes 557060 | tf_op jit(solution)/shard_map/all_to_all | solution.py:33
  78.5 0.1 reshape.111
  78.7 0.1 reshape.102
  78.9 0.1 copy.58
  79.0 0.5 copy_add_fusion
  79.5 0.2 copy.61
  79.7 0.1 reshape.103
  79.8 0.1 copy.68
  79.9 0.5 fusion.12
  80.5 0.1 pad_maximum_fusion.2
  80.5 0.3 copy.63
  80.8 0.3 reshape.112
  81.2 17.8 %all_to_all.11 = f32[64,1,1024]{2,1,0:T(1,128)S(1)} all-to-all(f32[64,1,1024]{2,1,0:T(1,128)S(1)} %reshape.112), channel_id=1, replica_groups=mesh['dist'=64,'sky'=4] {'dist'}, dimensions={0} | all-to-all | bytes 524288 | tf_op jit(solution)/shard_map/all_to_all | solution.py:44
  99.0 1.3 %reduce.5 = f32[64,1024]{1,0:T(8,128)S(1)} reduce(f32[64,1,1024]{2,1,0:T(1,128)S(1)} %all_to_all.11, f32[]{:T(128)} %broadcast.31), dimensions={1}, to_apply=%all_to_all.7.reduce_sub_computation | reduce | bytes 524292 | tf_op jit(solution)/shard_map/all_to_all | solution.py:44
  100.2 0.1 reshape.113
  100.4 0.1 copy.64
  100.5 0.2 stack.53
  100.7 0.1 copy.65
  100.7 0.2 stack.54
  100.9 0.9 pad_maximum_fusion.3.carries_ref
  101.8 7.5 %shard_map.87 = (bf16[8,16,4096]{2,1,0:T(8,128)(2,1)}, f32[8,16,4096]{2,1,0:T(8,128)}) custom-call(f32[64]{0:T(128)} %reshape.105.sqrt_ref, f32[8,16,4096]{2,1,0:T(8,128)} %get-tuple-element.5.density_ref, f32[8,16,4096]{2,1,0:T(8,128)} %get-tuple-element.6.local_ref, f32[8,2,4096]{2,1,0:T(2,128)} %pad_maximum_fusion.3.carries_ref, ...), custom_call_target="tpu_custom_call" | custom-call | tf_op jit(solution)/shard_map/pallas_call | solution.py:296
  (20 shorter events, 0.2 us)
Async XLA Ops:
  1.6 13.2 %collective-permute-start = (f32[8,1,8,128]{3,2,1,0:T(8,128)S(1)}, f32[8,1,8,128]{3,2,1,0:T(8,128)S(1)}, u32[]{:S(2)}, u32[]{:S(2)}) collective-permute-start(f32[8,1,8,128]{3,2,1,0:T(8,128)S(1)} %get-tuple-element.20), channel_id=1, source_target_pairs={{0,4},{4,8},{8,12},{12,16},{16,20},{20,24},{24,28},{28,32},{32,36}... | collective-permute-start | bytes 98312 | tf_op jit(solution)/shard_map/ppermute | solution.py:19
  6.2 8.8 %collective-permute-start.1 = (f32[8,1,8,128]{3,2,1,0:T(8,128)S(1)}, f32[8,1,8,128]{3,2,1,0:T(8,128)S(1)}, u32[]{:S(2)}, u32[]{:S(2)}) collective-permute-start(f32[8,1,8,128]{3,2,1,0:T(8,128)S(1)} %get-tuple-element.19), channel_id=1, source_target_pairs={{4,0},{8,4},{12,8},{16,12},{20,16},{24,20},{28,24},{32,28},{36,32}... | collective-permute-start | bytes 98312 | tf_op jit(solution)/shard_map/ppermute | solution.py:22
  9.0 5.8 %copy-start.2 = (s32[16,4096]{1,0:T(8,128)S(1)}, s32[16,4096]{1,0:T(8,128)}, u32[]{:S(2)}) copy-start(s32[16,4096]{1,0:T(8,128)} %param.13) | copy-start | bytes 786436
  9.0 5.8 %copy-start.1 = (f32[8,8,1024]{2,1,0:T(8,128)S(1)}, f32[8,8,1024]{2,1,0:T(8,128)}, u32[]{:S(2)}) copy-start(f32[8,8,1024]{2,1,0:T(8,128)} %param.7) | copy-start | bytes 786436
  9.1 11.8 %copy-start.4 = (bf16[2,4,2,4]{3,2,1,0:T(2,128)(2,1)S(1)}, bf16[2,4,2,4]{3,2,1,0:T(2,128)(2,1)}, u32[]{:S(2)}) copy-start(bf16[2,4,2,4]{3,2,1,0:T(2,128)(2,1)} %param.10) | copy-start | bytes 388
  9.1 12.5 %copy-start.3 = (f32[2,4,3,9]{3,1,2,0:T(4,128)S(1)}, f32[2,4,3,9]{3,1,2,0:T(4,128)}, u32[]{:S(2)}) copy-start(f32[2,4,3,9]{3,1,2,0:T(4,128)} %param.9) | copy-start | bytes 2596
  15.0 7.2 %collective-permute-start.2 = (f32[8,10,1,128]{3,2,1,0:T(1,128)S(1)}, f32[8,10,1,128]{3,2,1,0:T(1,128)S(1)}, u32[]{:S(2)}, u32[]{:S(2)}) collective-permute-start(f32[8,10,1,128]{3,2,1,0:T(1,128)S(1)} %get-tuple-element.17), channel_id=1, source_target_pairs={{0,1},{1,2},{2,3},{4,5},{5,6},{6,7},{8,9},{9,10},{10,11},{12,13},{... | collective-permute-start | bytes 122888 | tf_op jit(solution)/shard_map/ppermute | solution.py:19
  18.2 4.7 %collective-permute-start.3 = (f32[8,10,1,128]{3,2,1,0:T(1,128)S(1)}, f32[8,10,1,128]{3,2,1,0:T(1,128)S(1)}, u32[]{:S(2)}, u32[]{:S(2)}) collective-permute-start(f32[8,10,1,128]{3,2,1,0:T(1,128)S(1)} %get-tuple-element.18), channel_id=1, source_target_pairs={{1,0},{2,1},{3,2},{5,4},{6,5},{7,6},{9,8},{10,9},{11,10},{13,12},{... | collective-permute-start | bytes 122888 | tf_op jit(solution)/shard_map/ppermute | solution.py:22
  25.8 1.8 %copy-start = (bf16[3,8,8,24,384]{4,3,0,2,1:T(8,128)(2,1)}, bf16[3,8,8,24,384]{4,3,0,2,1:T(8,128)(2,1)S(1)}, u32[]{:S(2)}) copy-start(bf16[3,8,8,24,384]{4,3,0,2,1:T(8,128)(2,1)S(1)} %fusion.1) | copy-start | bytes 10616836

commit v12 on v11

--- a/solution.py
+++ b/solution.py
@@ -161,11 +161,14 @@
             high = running(second, True) + jnp.broadcast_to(low[7:8], low.shape)
             local_ref[0, pl.ds(0, 8), lanes] = low
             local_ref[0, pl.ds(8, 8), lanes] = high
-            misfit = counts_ref[pl.ds(0, 8), lanes] * (low - stars_ref[pl.ds(0, 8), lanes]) + counts_ref[
-                pl.ds(8, 8), lanes
-            ] * (high - stars_ref[pl.ds(8, 8), lanes])
+            counts_low = counts_ref[pl.ds(0, 8), lanes]
+            counts_high = counts_ref[pl.ds(8, 8), lanes]
+            misfit = counts_low * (low - stars_ref[pl.ds(0, 8), lanes]) + counts_high * (
+                high - stars_ref[pl.ds(8, 8), lanes]
+            )
             sums_ref[0, 0:1, lanes] = high[7:8]
             sums_ref[0, 1:2, lanes] = jnp.sum(misfit, axis=0, keepdims=True)
+            sums_ref[0, 2:3, lanes] = jnp.sum(counts_low + counts_high, axis=0, keepdims=True)
 
 
 def backward_kernel(
@@ -262,12 +265,12 @@
         out_specs=[
             per_sample((1, fine_shells, fine_pixels)),
             per_sample((1, fine_shells, fine_pixels)),
-            per_sample((1, 2, fine_pixels)),
+            per_sample((1, 3, fine_pixels)),
         ],
         out_shape=[
             jax.ShapeDtypeStruct((samples, fine_shells, fine_pixels), jnp.float32),
             jax.ShapeDtypeStruct((samples, fine_shells, fine_pixels), jnp.float32),
-            jax.ShapeDtypeStruct((samples, 2, fine_pixels), jnp.float32),
+            jax.ShapeDtypeStruct((samples, 3, fine_pixels), jnp.float32),
         ],
         scratch_shapes=[
             pltpu.VMEM((rows, slots * BAND), jnp.float32),
@@ -336,8 +339,7 @@
     density, local_cum, sums = local_forward(
         extended, halo_index, excitations, refine_weights, refine_sqrt, counts, star_extinction, widths
     )
-    weight = jnp.sum(counts, axis=0, keepdims=True)
-    carry_in, carry_out = block_carries(sums[:, 0], sums[:, 1], weight, "dist")
+    carry_in, carry_out = block_carries(sums[:, 0], sums[:, 1], sums[:1, 2], "dist")
     carries = jnp.stack([carry_in, carry_out], axis=1)
     return local_backward(refine_sqrt, density, local_cum, carries, counts, star_extinction)
 

time: 110 us -> 111 us (level)
    slice x1 -> x2, local copies, waits for them, and re-layouts: 1.74 us -> 2.92 us  [the longest x1 2.03 us: shards(): sums[:, 0]]
  transfers between devices with their start and end apart: 4 -> 4, of which waited for: 1 -> 1; matrix products, arithmetic and copies ran while one was open for 9% -> 8% of each run, Pallas kernels for 0% -> 0%
where the time goes in v12:
time: 111 us
  blocking collectives  45.7 us (41%)
  Pallas kernels  26.1 us (24%)
  local copies, waits for them, and re-layouts  13.8 us (12%)
  other arithmetic  11.2 us (10%)
  starting transfers between devices  10.9 us (10%)
    all_to_all x1, blocking collectives, block_carries(): mine = lax.all_to_all(packed, axis, 0, 0, tiled=True)  27.9 us
    pallas_call x1, Pallas kernels, local_forward(): pl.pallas_call(forward_kernel, grid=(samples,), in_specs=[smem, smem, per...  18.6 us
    all_to_all x1, blocking collectives, block_carries(): lax.all_to_all(jnp.concatenate([carry_in, carry_out], axis=1), axis, 0, 0...  17.8 us
    ppermute x2, starting transfers between devices, with_halo(): lax.ppermute(lax.slice_in_dim(block, block.shape[dim] - width, None, axis...  7.7 us
    pallas_call x1, Pallas kernels, local_backward(): pl.pallas_call(backward_kernel, grid=(samples,), in_specs=[smem, per_samp...  7.53 us
    convert_element_type x1, other arithmetic, local_forward(): onehot = (local.transpose(1, 0, 2)[:, None] == spots).astype(jnp.bfloat16)  5.74 us
    unnamed x27, local copies, waits for them, and re-layouts  5.41 us
    ppermute x2, starting transfers between devices, with_halo(): lax.ppermute(lax.slice_in_dim(block, 0, width, axis=dim), axis, backward)  3.22 us
  transfers between devices with their start and end apart: 4, of which 1 were waited for; matrix products, arithmetic and copies ran while one was open for 8% of the time, Pallas kernels for 0%

profile of v12, /device:TPU:1, one launch (start us, length us, event | category | flops | bytes accessed | tf_op | source)
XLA Modules:
  0.0 110.7 jit_solution(685958376379652068)
XLA Ops:
  0.6 1.0 copy.81
  1.6 4.5 %collective-permute-start = (f32[8,1,8,128]{3,2,1,0:T(8,128)S(1)}, f32[8,1,8,128]{3,2,1,0:T(8,128)S(1)}, u32[]{:S(2)}, u32[]{:S(2)}) collective-permute-start(f32[8,1,8,128]{3,2,1,0:T(8,128)S(1)} %get-tuple-element.20), channel_id=1, source_target_pairs={{0,4},{4,8},{8,12},{12,16},{16,20},{20,24},{24,28},{28,32},{32,36}... | collective-permute-start | bytes 98312 | tf_op jit(solution)/shard_map/ppermute | solution.py:19
  6.2 1.9 %collective-permute-start.1 = (f32[8,1,8,128]{3,2,1,0:T(8,128)S(1)}, f32[8,1,8,128]{3,2,1,0:T(8,128)S(1)}, u32[]{:S(2)}, u32[]{:S(2)}) collective-permute-start(f32[8,1,8,128]{3,2,1,0:T(8,128)S(1)} %get-tuple-element.19), channel_id=1, source_target_pairs={{4,0},{8,4},{12,8},{16,12},{20,16},{24,20},{28,24},{32,28},{36,32}... | collective-permute-start | bytes 98312 | tf_op jit(solution)/shard_map/ppermute | solution.py:22
  8.1 0.9 copy.73
  9.0 0.1 fusion.10
  9.1 5.7 %fusion.onehot_ref = bf16[8,384,1152]{2,1,0:T(8,128)(2,1)} fusion(s32[8,1152]{1,0:T(8,128)S(1)} %fusion.10), kind=kLoop, calls=%fused_computation.1 | loop fusion | flops 7077888 | bytes 7114752 | tf_op jit(solution)/shard_map/convert_element_type | solution.py:246
  14.8 0.1 constant_dynamic-update-slice_fusion.1
  14.9 0.1 fusion.19
  15.0 3.2 %collective-permute-start.2 = (f32[8,10,1,128]{3,2,1,0:T(1,128)S(1)}, f32[8,10,1,128]{3,2,1,0:T(1,128)S(1)}, u32[]{:S(2)}, u32[]{:S(2)}) collective-permute-start(f32[8,10,1,128]{3,2,1,0:T(1,128)S(1)} %get-tuple-element.17), channel_id=1, source_target_pairs={{0,1},{1,2},{2,3},{4,5},{5,6},{6,7},{8,9},{9,10},{10,11},{12,13},{... | collective-permute-start | bytes 122888 | tf_op jit(solution)/shard_map/ppermute | solution.py:19
  18.2 1.3 %collective-permute-start.3 = (f32[8,10,1,128]{3,2,1,0:T(1,128)S(1)}, f32[8,10,1,128]{3,2,1,0:T(1,128)S(1)}, u32[]{:S(2)}, u32[]{:S(2)}) collective-permute-start(f32[8,10,1,128]{3,2,1,0:T(1,128)S(1)} %get-tuple-element.18), channel_id=1, source_target_pairs={{1,0},{2,1},{3,2},{5,4},{6,5},{7,6},{9,8},{10,9},{11,10},{13,12},{... | collective-permute-start | bytes 122888 | tf_op jit(solution)/shard_map/ppermute | solution.py:22
  19.5 0.6 exponential_multiply_fusion.widths_ref
  20.1 0.7 convert_element_type.17.counts_ref
  20.8 0.6 reshape.105.sqrt_ref
  21.5 0.7 reshape.96.weights_ref
  22.1 0.8 collective-permute-done.3
  22.9 0.1 pad_maximum_fusion
  23.0 0.2 reduce-precision_convert_fusion.1
  23.3 0.1 pad_maximum_fusion.1
  23.4 0.1 copy.71
  23.5 0.1 pad.4.clone
  23.6 0.8 broadcast_in_dim.2
  24.4 0.6 reshape.99
  25.0 0.1 fusion.8
  25.1 0.1 fusion.7
  25.1 0.1 fusion.6
  25.2 0.1 fusion.5
  25.3 0.1 fusion.4
  25.4 0.1 fusion.3
  25.5 0.1 fusion.2
  25.6 0.1 fusion.1
  25.7 1.8 %copy-done = bf16[3,8,8,24,384]{4,3,0,2,1:T(8,128)(2,1)} copy-done((bf16[3,8,8,24,384]{4,3,0,2,1:T(8,128)(2,1)}, bf16[3,8,8,24,384]{4,3,0,2,1:T(8,128)(2,1)S(1)}, u32[]{:S(2)}) %copy-start) | copy-done | bytes 3538968
  27.5 18.6 %shard_map.86 = (f32[8,16,4096]{2,1,0:T(8,128)}, f32[8,16,4096]{2,1,0:T(8,128)}, f32[8,3,4096]{2,1,0:T(4,128)}) custom-call(f32[216]{0:T(256)} %reshape.96.weights_ref, f32[64]{0:T(128)} %reshape.105.sqrt_ref, bf16[8,8,72,384]{3,2,1,0:T(8,128)(2,1)} %bitcast.93, bf16[8,384,1152]{2,1,0:T(8,128)(2,1)} %fusion.onehot_ref, bf16[8,16,4096]{2,1,0:T(8,128)(2,1)} %excite_ref.1, ...), custom_call_target="tpu_custom_call" | custom-call | tf_op jit(solution)/shard_map/pallas_call | solution.py:252
  46.1 2.0 %slice_reduce_fusion.1 = (f32[8,4096]{1,0:T(8,128)S(1)}, f32[8,4096]{1,0:T(8,128)S(1)}) fusion(f32[8,3,4096]{2,1,0:T(4,128)} %get-tuple-element.7), kind=kLoop, calls=%fused_computation.31 | loop fusion | bytes 524288 | tf_op jit(solution)/shard_map/slice | solution.py:342
  48.2 0.9 slice_reduce_fusion.2
  49.0 0.1 concatenate.21
  49.2 0.2 copy.56
  49.3 0.1 concatenate.22
  49.4 0.2 copy.57
  49.6 0.1 concatenate.23
  49.7 0.1 maximum_bitcast_fusion
  49.7 0.4 reshape.117
  50.1 27.9 %all_to_all.10 = f32[64,1,1088]{2,1,0:T(1,128)S(1)} all-to-all(f32[64,1,1088]{2,1,0:T(1,128)S(1)} %reshape.117), channel_id=1, replica_groups=mesh['dist'=64,'sky'=4] {'dist'}, dimensions={0} | all-to-all | bytes 557056 | tf_op jit(solution)/shard_map/all_to_all | solution.py:33
  78.0 0.5 broadcast.34
  78.5 1.3 %reduce.8 = f32[64,1088]{1,0:T(8,128)S(1)} reduce(f32[64,1,1088]{2,1,0:T(1,128)S(1)} %all_to_all.10, f32[]{:T(128)} %broadcast.34), dimensions={1}, to_apply=%all_to_all.6.reduce_sub_computation | reduce | bytes 557060 | tf_op jit(solution)/shard_map/all_to_all | solution.py:33
  79.9 0.1 reshape.118
  80.1 0.1 reshape.102
  80.2 0.1 copy.59
  80.3 0.5 copy_add_fusion
  80.9 0.2 copy.62
  81.0 0.1 reshape.103
  81.1 0.1 copy.69
  81.3 0.5 fusion.12
  81.8 0.1 pad_maximum_fusion.2
  81.9 0.3 copy.64
  82.2 0.3 reshape.119
  82.5 17.8 %all_to_all.11 = f32[64,1,1024]{2,1,0:T(1,128)S(1)} all-to-all(f32[64,1,1024]{2,1,0:T(1,128)S(1)} %reshape.119), channel_id=1, replica_groups=mesh['dist'=64,'sky'=4] {'dist'}, dimensions={0} | all-to-all | bytes 524288 | tf_op jit(solution)/shard_map/all_to_all | solution.py:44
  100.3 1.3 %reduce.9 = f32[64,1024]{1,0:T(8,128)S(1)} reduce(f32[64,1,1024]{2,1,0:T(1,128)S(1)} %all_to_all.11, f32[]{:T(128)} %broadcast.34), dimensions={1}, to_apply=%all_to_all.7.reduce_sub_computation | reduce | bytes 524292 | tf_op jit(solution)/shard_map/all_to_all | solution.py:44
  101.6 0.1 reshape.120
  101.8 0.1 copy.65
  101.8 0.2 stack.53
  102.0 0.1 copy.66
  102.1 0.2 stack.54
  102.2 0.9 pad_maximum_fusion.3.carries_ref
  103.2 7.5 %shard_map.87 = (bf16[8,16,4096]{2,1,0:T(8,128)(2,1)}, f32[8,16,4096]{2,1,0:T(8,128)}) custom-call(f32[64]{0:T(128)} %reshape.105.sqrt_ref, f32[8,16,4096]{2,1,0:T(8,128)} %get-tuple-element.5.density_ref, f32[8,16,4096]{2,1,0:T(8,128)} %get-tuple-element.6.local_ref, f32[8,2,4096]{2,1,0:T(2,128)} %pad_maximum_fusion.3.carries_ref, ...), custom_call_target="tpu_custom_call" | custom-call | tf_op jit(solution)/shard_map/pallas_call | solution.py:299
  (20 shorter events, 0.1 us)
Async XLA Ops:
  1.6 13.2 %collective-permute-start = (f32[8,1,8,128]{3,2,1,0:T(8,128)S(1)}, f32[8,1,8,128]{3,2,1,0:T(8,128)S(1)}, u32[]{:S(2)}, u32[]{:S(2)}) collective-permute-start(f32[8,1,8,128]{3,2,1,0:T(8,128)S(1)} %get-tuple-element.20), channel_id=1, source_target_pairs={{0,4},{4,8},{8,12},{12,16},{16,20},{20,24},{24,28},{28,32},{32,36}... | collective-permute-start | bytes 98312 | tf_op jit(solution)/shard_map/ppermute | solution.py:19
  6.2 8.7 %collective-permute-start.1 = (f32[8,1,8,128]{3,2,1,0:T(8,128)S(1)}, f32[8,1,8,128]{3,2,1,0:T(8,128)S(1)}, u32[]{:S(2)}, u32[]{:S(2)}) collective-permute-start(f32[8,1,8,128]{3,2,1,0:T(8,128)S(1)} %get-tuple-element.19), channel_id=1, source_target_pairs={{4,0},{8,4},{12,8},{16,12},{20,16},{24,20},{28,24},{32,28},{36,32}... | collective-permute-start | bytes 98312 | tf_op jit(solution)/shard_map/ppermute | solution.py:22
  9.0 5.8 %copy-start.1 = (f32[8,8,1024]{2,1,0:T(8,128)S(1)}, f32[8,8,1024]{2,1,0:T(8,128)}, u32[]{:S(2)}) copy-start(f32[8,8,1024]{2,1,0:T(8,128)} %param.7) | copy-start | bytes 786436
  9.0 11.0 %copy-start.2 = (s32[16,4096]{1,0:T(8,128)S(1)}, s32[16,4096]{1,0:T(8,128)}, u32[]{:S(2)}) copy-start(s32[16,4096]{1,0:T(8,128)} %param.13) | copy-start | bytes 786436
  9.1 11.8 %copy-start.4 = (bf16[2,4,2,4]{3,2,1,0:T(2,128)(2,1)S(1)}, bf16[2,4,2,4]{3,2,1,0:T(2,128)(2,1)}, u32[]{:S(2)}) copy-start(bf16[2,4,2,4]{3,2,1,0:T(2,128)(2,1)} %param.10) | copy-start | bytes 388
  9.1 12.4 %copy-start.3 = (f32[2,4,3,9]{3,1,2,0:T(4,128)S(1)}, f32[2,4,3,9]{3,1,2,0:T(4,128)}, u32[]{:S(2)}) copy-start(f32[2,4,3,9]{3,1,2,0:T(4,128)} %param.9) | copy-start | bytes 2596
  15.0 7.2 %collective-permute-start.2 = (f32[8,10,1,128]{3,2,1,0:T(1,128)S(1)}, f32[8,10,1,128]{3,2,1,0:T(1,128)S(1)}, u32[]{:S(2)}, u32[]{:S(2)}) collective-permute-start(f32[8,10,1,128]{3,2,1,0:T(1,128)S(1)} %get-tuple-element.17), channel_id=1, source_target_pairs={{0,1},{1,2},{2,3},{4,5},{5,6},{6,7},{8,9},{9,10},{10,11},{12,13},{... | collective-permute-start | bytes 122888 | tf_op jit(solution)/shard_map/ppermute | solution.py:19
  18.2 4.7 %collective-permute-start.3 = (f32[8,10,1,128]{3,2,1,0:T(1,128)S(1)}, f32[8,10,1,128]{3,2,1,0:T(1,128)S(1)}, u32[]{:S(2)}, u32[]{:S(2)}) collective-permute-start(f32[8,10,1,128]{3,2,1,0:T(1,128)S(1)} %get-tuple-element.18), channel_id=1, source_target_pairs={{1,0},{2,1},{3,2},{5,4},{6,5},{7,6},{9,8},{10,9},{11,10},{13,12},{... | collective-permute-start | bytes 122888 | tf_op jit(solution)/shard_map/ppermute | solution.py:22
  25.7 1.8 %copy-start = (bf16[3,8,8,24,384]{4,3,0,2,1:T(8,128)(2,1)}, bf16[3,8,8,24,384]{4,3,0,2,1:T(8,128)(2,1)S(1)}, u32[]{:S(2)}) copy-start(bf16[3,8,8,24,384]{4,3,0,2,1:T(8,128)(2,1)S(1)} %fusion.1) | copy-start | bytes 10616836

commit v13 on v11

--- a/solution.py
+++ b/solution.py
@@ -41,9 +41,9 @@
     carry_in = jnp.dot(earlier, flat(block_totals), precision=exact_mode).reshape(blocks, height, width)
     block_misfit = block_partial + block_weight * carry_in
     carry_out = jnp.dot(earlier.T, flat(block_misfit), precision=exact_mode).reshape(blocks, height, width)
-    back = lax.all_to_all(jnp.concatenate([carry_in, carry_out], axis=1), axis, 0, 0, tiled=True)
-    back = back.transpose(1, 0, 2).reshape(2 * rows, pixels)
-    return back[:rows], back[rows:]
+    paired_carries = jnp.stack([carry_in, carry_out], axis=2).reshape(blocks, 2 * rows, width)
+    back = lax.all_to_all(paired_carries, axis, 0, 0, tiled=True)
+    return back.transpose(1, 0, 2).reshape(rows, 2, pixels)
 
 
 def split_three(values):
@@ -337,8 +337,7 @@
         extended, halo_index, excitations, refine_weights, refine_sqrt, counts, star_extinction, widths
     )
     weight = jnp.sum(counts, axis=0, keepdims=True)
-    carry_in, carry_out = block_carries(sums[:, 0], sums[:, 1], weight, "dist")
-    carries = jnp.stack([carry_in, carry_out], axis=1)
+    carries = block_carries(sums[:, 0], sums[:, 1], weight, "dist")
     return local_backward(refine_sqrt, density, local_cum, carries, counts, star_extinction)
 
 

time: 110 us -> 109 us (level)
    reshape x0 -> x3, local copies, waits for them, and re-layouts: none -> 1.37 us  [the longest x1 0.95 us: block_carries(): return back.transpose(1, 0, 2).reshape(rows, 2, pixels)]
where the time goes in v13:
time: 109 us
  blocking collectives  45.7 us (42%)
  Pallas kernels  25.9 us (24%)
  local copies, waits for them, and re-layouts  13.3 us (12%)
  starting transfers between devices  10.9 us (10%)
  other arithmetic  10.4 us (10%)
    all_to_all x1, blocking collectives, block_carries(): mine = lax.all_to_all(packed, axis, 0, 0, tiled=True)  27.9 us
    pallas_call x1, Pallas kernels, local_forward(): pl.pallas_call(forward_kernel, grid=(samples,), in_specs=[smem, smem, per...  18.4 us
    all_to_all x1, blocking collectives, block_carries(): back = lax.all_to_all(paired_carries, axis, 0, 0, tiled=True)  17.8 us
    ppermute x2, starting transfers between devices, with_halo(): lax.ppermute(lax.slice_in_dim(block, block.shape[dim] - width, None, axis...  7.7 us
    pallas_call x1, Pallas kernels, local_backward(): pl.pallas_call(backward_kernel, grid=(samples,), in_specs=[smem, per_samp...  7.53 us
    convert_element_type x1, other arithmetic, local_forward(): onehot = (local.transpose(1, 0, 2)[:, None] == spots).astype(jnp.bfloat16)  5.74 us
    unnamed x27, local copies, waits for them, and re-layouts  5.41 us
    ppermute x2, starting transfers between devices, with_halo(): lax.ppermute(lax.slice_in_dim(block, 0, width, axis=dim), axis, backward)  3.22 us
  transfers between devices with their start and end apart: 4, of which 1 were waited for; matrix products, arithmetic and copies ran while one was open for 9% of the time, Pallas kernels for 0%

profile of v13, /device:TPU:1, one launch (start us, length us, event | category | flops | bytes accessed | tf_op | source)
XLA Modules:
  0.0 108.8 jit_solution(8208898409839342951)
XLA Ops:
  0.6 1.0 copy.74
  1.6 4.5 %collective-permute-start = (f32[8,1,8,128]{3,2,1,0:T(8,128)S(1)}, f32[8,1,8,128]{3,2,1,0:T(8,128)S(1)}, u32[]{:S(2)}, u32[]{:S(2)}) collective-permute-start(f32[8,1,8,128]{3,2,1,0:T(8,128)S(1)} %get-tuple-element.16), channel_id=1, source_target_pairs={{0,4},{4,8},{8,12},{12,16},{16,20},{20,24},{24,28},{28,32},{32,36}... | collective-permute-start | bytes 98312 | tf_op jit(solution)/shard_map/ppermute | solution.py:19
  6.2 1.9 %collective-permute-start.1 = (f32[8,1,8,128]{3,2,1,0:T(8,128)S(1)}, f32[8,1,8,128]{3,2,1,0:T(8,128)S(1)}, u32[]{:S(2)}, u32[]{:S(2)}) collective-permute-start(f32[8,1,8,128]{3,2,1,0:T(8,128)S(1)} %get-tuple-element.15), channel_id=1, source_target_pairs={{4,0},{8,4},{12,8},{16,12},{20,16},{24,20},{28,24},{32,28},{36,32}... | collective-permute-start | bytes 98312 | tf_op jit(solution)/shard_map/ppermute | solution.py:22
  8.1 0.9 copy.67
  9.0 0.1 fusion.10
  9.1 0.0 copy-start.3
  9.1 5.7 %fusion.onehot_ref = bf16[8,384,1152]{2,1,0:T(8,128)(2,1)} fusion(s32[8,1152]{1,0:T(8,128)S(1)} %fusion.10), kind=kLoop, calls=%fused_computation.1 | loop fusion | flops 7077888 | bytes 7114752 | tf_op jit(solution)/shard_map/convert_element_type | solution.py:243
  14.9 0.0 collective-permute-done
  14.9 0.1 constant_dynamic-update-slice_fusion.1
  15.0 0.0 collective-permute-done.1
  15.0 0.1 fusion.14
  15.0 3.2 %collective-permute-start.2 = (f32[8,10,1,128]{3,2,1,0:T(1,128)S(1)}, f32[8,10,1,128]{3,2,1,0:T(1,128)S(1)}, u32[]{:S(2)}, u32[]{:S(2)}) collective-permute-start(f32[8,10,1,128]{3,2,1,0:T(1,128)S(1)} %get-tuple-element.13), channel_id=1, source_target_pairs={{0,1},{1,2},{2,3},{4,5},{5,6},{6,7},{8,9},{9,10},{10,11},{12,13},{... | collective-permute-start | bytes 122888 | tf_op jit(solution)/shard_map/ppermute | solution.py:19
  18.2 1.3 %collective-permute-start.3 = (f32[8,10,1,128]{3,2,1,0:T(1,128)S(1)}, f32[8,10,1,128]{3,2,1,0:T(1,128)S(1)}, u32[]{:S(2)}, u32[]{:S(2)}) collective-permute-start(f32[8,10,1,128]{3,2,1,0:T(1,128)S(1)} %get-tuple-element.14), channel_id=1, source_target_pairs={{1,0},{2,1},{3,2},{5,4},{6,5},{7,6},{9,8},{10,9},{11,10},{13,12},{... | collective-permute-start | bytes 122888 | tf_op jit(solution)/shard_map/ppermute | solution.py:22
  19.5 0.6 exponential_multiply_fusion.widths_ref
  20.1 0.7 convert_element_type.17.counts_ref
  20.9 0.6 reshape.115.sqrt_ref
  21.5 0.7 reshape.102.weights_ref
  22.2 0.1 concatenate.20
  22.3 0.0 collective-permute-done.2
  22.3 0.7 collective-permute-done.3
  23.0 0.1 pad_maximum_fusion
  23.1 0.2 reduce-precision_convert_fusion.1
  23.4 0.1 pad_maximum_fusion.1
  23.4 0.1 copy.65
  23.6 0.1 pad.4.clone
  23.7 0.8 broadcast_in_dim.2
  24.5 0.6 reshape.105
  25.1 0.1 fusion.8
  25.1 0.1 fusion.7
  25.2 0.1 fusion.6
  25.3 0.1 fusion.5
  25.4 0.1 fusion.4
  25.5 0.1 fusion.3
  25.6 0.1 fusion.2
  25.7 0.1 fusion.1
  25.8 1.8 %copy-done = bf16[3,8,8,24,384]{4,3,0,2,1:T(8,128)(2,1)} copy-done((bf16[3,8,8,24,384]{4,3,0,2,1:T(8,128)(2,1)}, bf16[3,8,8,24,384]{4,3,0,2,1:T(8,128)(2,1)S(1)}, u32[]{:S(2)}) %copy-start) | copy-done | bytes 3538968
  27.6 18.4 %shard_map.86 = (f32[8,16,4096]{2,1,0:T(8,128)}, f32[8,16,4096]{2,1,0:T(8,128)}, f32[8,2,4096]{2,1,0:T(2,128)}) custom-call(f32[216]{0:T(256)} %reshape.102.weights_ref, f32[64]{0:T(128)} %reshape.115.sqrt_ref, bf16[8,8,72,384]{3,2,1,0:T(8,128)(2,1)} %bitcast.87, bf16[8,384,1152]{2,1,0:T(8,128)(2,1)} %fusion.onehot_ref, bf16[8,16,4096]{2,1,0:T(8,128)(2,1)} %excite_ref.1, ...), custom_call_target="tpu_custom_call" | custom-call | tf_op jit(solution)/shard_map/pallas_call | solution.py:249
  46.0 1.7 %slice_reduce_fusion.1 = (f32[8,4096]{1,0:T(8,128)S(1)}, f32[8,4096]{1,0:T(8,128)S(1)}) fusion(f32[8,2,4096]{2,1,0:T(2,128)} %get-tuple-element.7), kind=kLoop, calls=%fused_computation.31 | loop fusion | bytes 524288 | tf_op jit(solution)/shard_map/slice | solution.py:340
  47.7 0.1 concatenate.18
  47.8 0.2 copy.57
  48.0 0.1 concatenate.19
  48.1 0.2 copy.58
  48.3 0.1 maximum_bitcast_fusion
  48.3 0.4 reshape.119
  48.7 27.9 %all_to_all.10 = f32[64,1,1088]{2,1,0:T(1,128)S(1)} all-to-all(f32[64,1,1088]{2,1,0:T(1,128)S(1)} %reshape.119), channel_id=1, replica_groups=mesh['dist'=64,'sky'=4] {'dist'}, dimensions={0} | all-to-all | bytes 557056 | tf_op jit(solution)/shard_map/all_to_all | solution.py:33
  76.7 0.5 broadcast.31
  77.2 1.3 %reduce.4 = f32[64,1088]{1,0:T(8,128)S(1)} reduce(f32[64,1,1088]{2,1,0:T(1,128)S(1)} %all_to_all.10, f32[]{:T(128)} %broadcast.31), dimensions={1}, to_apply=%all_to_all.6.reduce_sub_computation | reduce | bytes 557060 | tf_op jit(solution)/shard_map/all_to_all | solution.py:33
  78.5 0.1 reshape.120
  78.7 0.1 reshape.108
  78.8 0.3 fusion.12
  79.1 0.1 reshape.109
  79.2 0.1 stack_reshape.4
  79.3 0.1 reshape.110
  79.5 0.1 copy.64
  79.6 0.5 convolution_bitcast_fusion
  80.1 0.1 copy.60
  80.3 0.3 copy.62
  80.6 0.3 reshape.121
  80.9 17.8 %all_to_all.11 = f32[64,1,1024]{2,1,0:T(1,128)S(1)} all-to-all(f32[64,1,1024]{2,1,0:T(1,128)S(1)} %reshape.121), channel_id=1, replica_groups=mesh['dist'=64,'sky'=4] {'dist'}, dimensions={0} | all-to-all | bytes 524288 | tf_op jit(solution)/shard_map/all_to_all | solution.py:45
  98.7 1.3 %reduce.5 = f32[64,1024]{1,0:T(8,128)S(1)} reduce(f32[64,1,1024]{2,1,0:T(1,128)S(1)} %all_to_all.11, f32[]{:T(128)} %broadcast.31), dimensions={1}, to_apply=%all_to_all.7.reduce_sub_computation | reduce | bytes 524292 | tf_op jit(solution)/shard_map/all_to_all | solution.py:45
  100.0 0.1 reshape.122
  100.1 0.2 copy.63
  100.3 1.0 reshape.113.carries_ref
  101.2 7.5 %shard_map.87 = (bf16[8,16,4096]{2,1,0:T(8,128)(2,1)}, f32[8,16,4096]{2,1,0:T(8,128)}) custom-call(f32[64]{0:T(128)} %reshape.115.sqrt_ref, f32[8,16,4096]{2,1,0:T(8,128)} %get-tuple-element.5.density_ref, f32[8,16,4096]{2,1,0:T(8,128)} %get-tuple-element.6.local_ref, f32[8,2,4096]{2,1,0:T(2,128)} %reshape.113.carries_ref, ...), custom_call_target="tpu_custom_call" | custom-call | tf_op jit(solution)/shard_map/pallas_call | solution.py:296
  (19 shorter events, 0.3 us)
Async XLA Ops:
  1.6 13.2 %collective-permute-start = (f32[8,1,8,128]{3,2,1,0:T(8,128)S(1)}, f32[8,1,8,128]{3,2,1,0:T(8,128)S(1)}, u32[]{:S(2)}, u32[]{:S(2)}) collective-permute-start(f32[8,1,8,128]{3,2,1,0:T(8,128)S(1)} %get-tuple-element.16), channel_id=1, source_target_pairs={{0,4},{4,8},{8,12},{12,16},{16,20},{20,24},{24,28},{28,32},{32,36}... | collective-permute-start | bytes 98312 | tf_op jit(solution)/shard_map/ppermute | solution.py:19
  6.2 8.8 %collective-permute-start.1 = (f32[8,1,8,128]{3,2,1,0:T(8,128)S(1)}, f32[8,1,8,128]{3,2,1,0:T(8,128)S(1)}, u32[]{:S(2)}, u32[]{:S(2)}) collective-permute-start(f32[8,1,8,128]{3,2,1,0:T(8,128)S(1)} %get-tuple-element.15), channel_id=1, source_target_pairs={{4,0},{8,4},{12,8},{16,12},{20,16},{24,20},{28,24},{32,28},{36,32}... | collective-permute-start | bytes 98312 | tf_op jit(solution)/shard_map/ppermute | solution.py:22
  9.0 5.8 %copy-start.2 = (s32[16,4096]{1,0:T(8,128)S(1)}, s32[16,4096]{1,0:T(8,128)}, u32[]{:S(2)}) copy-start(s32[16,4096]{1,0:T(8,128)} %param.13) | copy-start | bytes 786436
  9.0 5.8 %copy-start.1 = (f32[8,8,1024]{2,1,0:T(8,128)S(1)}, f32[8,8,1024]{2,1,0:T(8,128)}, u32[]{:S(2)}) copy-start(f32[8,8,1024]{2,1,0:T(8,128)} %param.7) | copy-start | bytes 786436
  9.1 11.8 %copy-start.4 = (bf16[2,4,2,4]{3,2,1,0:T(2,128)(2,1)S(1)}, bf16[2,4,2,4]{3,2,1,0:T(2,128)(2,1)}, u32[]{:S(2)}) copy-start(bf16[2,4,2,4]{3,2,1,0:T(2,128)(2,1)} %param.10) | copy-start | bytes 388
  9.1 12.4 %copy-start.3 = (f32[2,4,3,9]{3,1,2,0:T(4,128)S(1)}, f32[2,4,3,9]{3,1,2,0:T(4,128)}, u32[]{:S(2)}) copy-start(f32[2,4,3,9]{3,1,2,0:T(4,128)} %param.9) | copy-start | bytes 2596
  15.0 7.2 %collective-permute-start.2 = (f32[8,10,1,128]{3,2,1,0:T(1,128)S(1)}, f32[8,10,1,128]{3,2,1,0:T(1,128)S(1)}, u32[]{:S(2)}, u32[]{:S(2)}) collective-permute-start(f32[8,10,1,128]{3,2,1,0:T(1,128)S(1)} %get-tuple-element.13), channel_id=1, source_target_pairs={{0,1},{1,2},{2,3},{4,5},{5,6},{6,7},{8,9},{9,10},{10,11},{12,13},{... | collective-permute-start | bytes 122888 | tf_op jit(solution)/shard_map/ppermute | solution.py:19
  18.2 4.7 %collective-permute-start.3 = (f32[8,10,1,128]{3,2,1,0:T(1,128)S(1)}, f32[8,10,1,128]{3,2,1,0:T(1,128)S(1)}, u32[]{:S(2)}, u32[]{:S(2)}) collective-permute-start(f32[8,10,1,128]{3,2,1,0:T(1,128)S(1)} %get-tuple-element.14), channel_id=1, source_target_pairs={{1,0},{2,1},{3,2},{5,4},{6,5},{7,6},{9,8},{10,9},{11,10},{13,12},{... | collective-permute-start | bytes 122888 | tf_op jit(solution)/shard_map/ppermute | solution.py:22
  25.8 1.8 %copy-start = (bf16[3,8,8,24,384]{4,3,0,2,1:T(8,128)(2,1)}, bf16[3,8,8,24,384]{4,3,0,2,1:T(8,128)(2,1)S(1)}, u32[]{:S(2)}) copy-start(bf16[3,8,8,24,384]{4,3,0,2,1:T(8,128)(2,1)S(1)} %fusion.1) | copy-start | bytes 10616836

commit v14 on v13

--- a/solution.py
+++ b/solution.py
@@ -161,9 +161,9 @@
             high = running(second, True) + jnp.broadcast_to(low[7:8], low.shape)
             local_ref[0, pl.ds(0, 8), lanes] = low
             local_ref[0, pl.ds(8, 8), lanes] = high
-            misfit = counts_ref[pl.ds(0, 8), lanes] * (low - stars_ref[pl.ds(0, 8), lanes]) + counts_ref[
+            misfit = counts_ref[pl.ds(0, 8), lanes].astype(jnp.float32) * (low - stars_ref[pl.ds(0, 8), lanes]) + counts_ref[
                 pl.ds(8, 8), lanes
-            ] * (high - stars_ref[pl.ds(8, 8), lanes])
+            ].astype(jnp.float32) * (high - stars_ref[pl.ds(8, 8), lanes])
             sums_ref[0, 0:1, lanes] = high[7:8]
             sums_ref[0, 1:2, lanes] = jnp.sum(misfit, axis=0, keepdims=True)
 
@@ -188,8 +188,8 @@
             high = local_ref[0, pl.ds(8, 8), lanes] + into
             extinct_ref[0, pl.ds(0, 8), lanes] = low.astype(extinct_ref.dtype)
             extinct_ref[0, pl.ds(8, 8), lanes] = high.astype(extinct_ref.dtype)
-            miss_low = counts_ref[pl.ds(0, 8), lanes] * (low - stars_ref[pl.ds(0, 8), lanes])
-            miss_high = counts_ref[pl.ds(8, 8), lanes] * (high - stars_ref[pl.ds(8, 8), lanes])
+            miss_low = counts_ref[pl.ds(0, 8), lanes].astype(jnp.float32) * (low - stars_ref[pl.ds(0, 8), lanes])
+            miss_high = counts_ref[pl.ds(8, 8), lanes].astype(jnp.float32) * (high - stars_ref[pl.ds(8, 8), lanes])
             behind_high = running(miss_high, False)
             behind_low = running(miss_low, False) + jnp.broadcast_to(behind_high[0:1], behind_high.shape)
             for h, behind in ((0, behind_low), (1, behind_high)):
@@ -332,11 +332,11 @@
     shells = dist_rank * fine_shells + jnp.arange(fine_shells, dtype=jnp.int32)
     middle = (shells.astype(jnp.float32) + 0.5) / all_shells
     widths = 3.0 * jnp.exp(3.0 * middle - 3.0) / all_shells
-    counts = star_counts.astype(jnp.float32)
+    counts = star_counts
     density, local_cum, sums = local_forward(
         extended, halo_index, excitations, refine_weights, refine_sqrt, counts, star_extinction, widths
     )
-    weight = jnp.sum(counts, axis=0, keepdims=True)
+    weight = jnp.sum(counts, axis=0, keepdims=True).astype(jnp.float32)
     carries = block_carries(sums[:, 0], sums[:, 1], weight, "dist")
     return local_backward(refine_sqrt, density, local_cum, carries, counts, star_extinction)
 

time: 109 us -> 109 us (level)
  transfers between devices with their start and end apart: 4 -> 4, of which waited for: 1 -> 1; matrix products, arithmetic and copies ran while one was open for 9% -> 8% of each run, Pallas kernels for 0% -> 0%
where the time goes in v14:
time: 109 us
  blocking collectives  45.7 us (42%)
  Pallas kernels  26.1 us (24%)
  local copies, waits for them, and re-layouts  13.3 us (12%)
  starting transfers between devices  10.9 us (10%)
  other arithmetic  9.66 us (9%)
  waiting for transfers between devices  1.37 us (1%)
    all_to_all x1, blocking collectives, block_carries(): mine = lax.all_to_all(packed, axis, 0, 0, tiled=True)  27.9 us
    pallas_call x1, Pallas kernels, local_forward(): pl.pallas_call(forward_kernel, grid=(samples,), in_specs=[smem, smem, per...  18.5 us
    all_to_all x1, blocking collectives, block_carries(): back = lax.all_to_all(paired_carries, axis, 0, 0, tiled=True)  17.8 us
    ppermute x2, starting transfers between devices, with_halo(): lax.ppermute(lax.slice_in_dim(block, block.shape[dim] - width, None, axis...  7.7 us
    pallas_call x1, Pallas kernels, local_backward(): pl.pallas_call(backward_kernel, grid=(samples,), in_specs=[smem, per_samp...  7.56 us
    convert_element_type x1, other arithmetic, local_forward(): onehot = (local.transpose(1, 0, 2)[:, None] == spots).astype(jnp.bfloat16)  5.74 us
    unnamed x27, local copies, waits for them, and re-layouts  5.41 us
    ppermute x2, starting transfers between devices, with_halo(): lax.ppermute(lax.slice_in_dim(block, 0, width, axis=dim), axis, backward)  3.22 us
  transfers between devices with their start and end apart: 4, of which 1 were waited for; matrix products, arithmetic and copies ran while one was open for 8% of the time, Pallas kernels for 0%

profile of v14, /device:TPU:1, one launch (start us, length us, event | category | flops | bytes accessed | tf_op | source)
XLA Modules:
  0.0 108.8 jit_solution(17034640345315032923)
XLA Ops:
  0.6 1.0 copy.74
  1.6 4.5 %collective-permute-start = (f32[8,1,8,128]{3,2,1,0:T(8,128)S(1)}, f32[8,1,8,128]{3,2,1,0:T(8,128)S(1)}, u32[]{:S(2)}, u32[]{:S(2)}) collective-permute-start(f32[8,1,8,128]{3,2,1,0:T(8,128)S(1)} %get-tuple-element.16), channel_id=1, source_target_pairs={{0,4},{4,8},{8,12},{12,16},{16,20},{20,24},{24,28},{28,32},{32,36}... | collective-permute-start | bytes 98312 | tf_op jit(solution)/shard_map/ppermute | solution.py:19
  6.2 1.9 %collective-permute-start.1 = (f32[8,1,8,128]{3,2,1,0:T(8,128)S(1)}, f32[8,1,8,128]{3,2,1,0:T(8,128)S(1)}, u32[]{:S(2)}, u32[]{:S(2)}) collective-permute-start(f32[8,1,8,128]{3,2,1,0:T(8,128)S(1)} %get-tuple-element.15), channel_id=1, source_target_pairs={{4,0},{8,4},{12,8},{16,12},{20,16},{24,20},{28,24},{32,28},{36,32}... | collective-permute-start | bytes 98312 | tf_op jit(solution)/shard_map/ppermute | solution.py:22
  8.1 0.9 copy.67
  9.0 0.1 fusion.10
  9.1 0.0 copy-start.1
  9.1 5.7 %fusion.onehot_ref = bf16[8,384,1152]{2,1,0:T(8,128)(2,1)} fusion(s32[8,1152]{1,0:T(8,128)S(1)} %fusion.10), kind=kLoop, calls=%fused_computation.1 | loop fusion | flops 7077888 | bytes 7114752 | tf_op jit(solution)/shard_map/convert_element_type | solution.py:243
  14.8 0.0 collective-permute-done
  14.8 0.0 copy-done.2
  14.8 0.1 constant_dynamic-update-slice_fusion.1
  14.9 0.0 collective-permute-done.1
  14.9 0.1 fusion.14
  15.0 3.2 %collective-permute-start.2 = (f32[8,10,1,128]{3,2,1,0:T(1,128)S(1)}, f32[8,10,1,128]{3,2,1,0:T(1,128)S(1)}, u32[]{:S(2)}, u32[]{:S(2)}) collective-permute-start(f32[8,10,1,128]{3,2,1,0:T(1,128)S(1)} %get-tuple-element.13), channel_id=1, source_target_pairs={{0,1},{1,2},{2,3},{4,5},{5,6},{6,7},{8,9},{9,10},{10,11},{12,13},{... | collective-permute-start | bytes 122888 | tf_op jit(solution)/shard_map/ppermute | solution.py:19
  18.2 1.3 %collective-permute-start.3 = (f32[8,10,1,128]{3,2,1,0:T(1,128)S(1)}, f32[8,10,1,128]{3,2,1,0:T(1,128)S(1)}, u32[]{:S(2)}, u32[]{:S(2)}) collective-permute-start(f32[8,10,1,128]{3,2,1,0:T(1,128)S(1)} %get-tuple-element.14), channel_id=1, source_target_pairs={{1,0},{2,1},{3,2},{5,4},{6,5},{7,6},{9,8},{10,9},{11,10},{13,12},{... | collective-permute-start | bytes 122888 | tf_op jit(solution)/shard_map/ppermute | solution.py:22
  19.5 0.6 exponential_multiply_fusion.widths_ref
  20.1 0.6 reshape.127.sqrt_ref
  20.7 0.7 reshape.114.weights_ref
  21.4 0.1 convert_element_type.31
  21.5 0.0 collective-permute-done.2
  21.5 1.4 %collective-permute-done.3 = f32[8,10,1,128]{3,2,1,0:T(1,128)S(1)} collective-permute-done((f32[8,10,1,128]{3,2,1,0:T(1,128)S(1)}, f32[8,10,1,128]{3,2,1,0:T(1,128)S(1)}, u32[]{:S(2)}, u32[]{:S(2)}) %collective-permute-start.3) | collective-permute-done | bytes 40992 | tf_op jit(solution)/shard_map/ppermute | solution.py:22
  22.9 0.1 pad_maximum_fusion
  23.0 0.2 reduce-precision_convert_fusion.1
  23.3 0.1 pad_maximum_fusion.1
  23.4 0.1 copy.65
  23.5 0.1 pad.4.clone
  23.6 0.8 broadcast_in_dim.2
  24.4 0.6 reshape.117
  25.0 0.1 fusion.8
  25.0 0.1 fusion.7
  25.1 0.1 fusion.6
  25.2 0.1 fusion.5
  25.3 0.1 fusion.4
  25.4 0.1 fusion.3
  25.5 0.1 fusion.2
  25.6 0.1 fusion.1
  25.7 1.8 %copy-done = bf16[3,8,8,24,384]{4,3,0,2,1:T(8,128)(2,1)} copy-done((bf16[3,8,8,24,384]{4,3,0,2,1:T(8,128)(2,1)}, bf16[3,8,8,24,384]{4,3,0,2,1:T(8,128)(2,1)S(1)}, u32[]{:S(2)}) %copy-start) | copy-done | bytes 3538968
  27.5 18.5 %shard_map.86 = (f32[8,16,4096]{2,1,0:T(8,128)}, f32[8,16,4096]{2,1,0:T(8,128)}, f32[8,2,4096]{2,1,0:T(2,128)}) custom-call(f32[216]{0:T(256)} %reshape.114.weights_ref, f32[64]{0:T(128)} %reshape.127.sqrt_ref, bf16[8,8,72,384]{3,2,1,0:T(8,128)(2,1)} %bitcast.87, bf16[8,384,1152]{2,1,0:T(8,128)(2,1)} %fusion.onehot_ref, bf16[8,16,4096]{2,1,0:T(8,128)(2,1)} %excite_ref.1, ...), custom_call_target="tpu_custom_call" | custom-call | tf_op jit(solution)/shard_map/pallas_call | solution.py:249
  46.0 1.7 %slice_reduce_fusion.1 = (f32[8,4096]{1,0:T(8,128)S(1)}, f32[8,4096]{1,0:T(8,128)S(1)}) fusion(f32[8,2,4096]{2,1,0:T(2,128)} %get-tuple-element.7), kind=kLoop, calls=%fused_computation.31 | loop fusion | bytes 524288 | tf_op jit(solution)/shard_map/slice | solution.py:340
  47.8 0.1 concatenate.16
  47.9 0.2 copy.57
  48.0 0.1 concatenate.17
  48.1 0.2 copy.58
  48.3 0.1 maximum_bitcast_fusion
  48.4 0.4 reshape.131
  48.7 27.9 %all_to_all.10 = f32[64,1,1088]{2,1,0:T(1,128)S(1)} all-to-all(f32[64,1,1088]{2,1,0:T(1,128)S(1)} %reshape.131), channel_id=1, replica_groups=mesh['dist'=64,'sky'=4] {'dist'}, dimensions={0} | all-to-all | bytes 557056 | tf_op jit(solution)/shard_map/all_to_all | solution.py:33
  76.7 0.5 broadcast.31
  77.2 1.3 %reduce.4 = f32[64,1088]{1,0:T(8,128)S(1)} reduce(f32[64,1,1088]{2,1,0:T(1,128)S(1)} %all_to_all.10, f32[]{:T(128)} %broadcast.31), dimensions={1}, to_apply=%all_to_all.6.reduce_sub_computation | reduce | bytes 557060 | tf_op jit(solution)/shard_map/all_to_all | solution.py:33
  78.5 0.1 reshape.132
  78.7 0.1 reshape.120
  78.8 0.2 fusion.12
  79.1 0.1 reshape.121
  79.2 0.1 stack_reshape.4
  79.4 0.1 reshape.122
  79.5 0.1 copy.64
  79.6 0.5 convolution_bitcast_fusion
  80.1 0.1 copy.60
  80.3 0.3 copy.62
  80.6 0.3 reshape.133
  80.9 17.8 %all_to_all.11 = f32[64,1,1024]{2,1,0:T(1,128)S(1)} all-to-all(f32[64,1,1024]{2,1,0:T(1,128)S(1)} %reshape.133), channel_id=1, replica_groups=mesh['dist'=64,'sky'=4] {'dist'}, dimensions={0} | all-to-all | bytes 524288 | tf_op jit(solution)/shard_map/all_to_all | solution.py:45
  98.7 1.3 %reduce.5 = f32[64,1024]{1,0:T(8,128)S(1)} reduce(f32[64,1,1024]{2,1,0:T(1,128)S(1)} %all_to_all.11, f32[]{:T(128)} %broadcast.31), dimensions={1}, to_apply=%all_to_all.7.reduce_sub_computation | reduce | bytes 524292 | tf_op jit(solution)/shard_map/all_to_all | solution.py:45
  100.0 0.1 reshape.134
  100.1 0.2 copy.63
  100.3 1.0 reshape.125.carries_ref
  101.3 7.6 %shard_map.87 = (bf16[8,16,4096]{2,1,0:T(8,128)(2,1)}, f32[8,16,4096]{2,1,0:T(8,128)}) custom-call(f32[64]{0:T(128)} %reshape.127.sqrt_ref, f32[8,16,4096]{2,1,0:T(8,128)} %get-tuple-element.5.density_ref, f32[8,16,4096]{2,1,0:T(8,128)} %get-tuple-element.6.local_ref, f32[8,2,4096]{2,1,0:T(2,128)} %reshape.125.carries_ref, s32[16,4096]{1,0:T(8,128)} %counts_ref.3, ...), custom_call_target="tpu_custom_call" | custom-call | tf_op jit(solution)/shard_map/pallas_call | solution.py:296
  (19 shorter events, 0.2 us)
Async XLA Ops:
  1.6 13.2 %collective-permute-start = (f32[8,1,8,128]{3,2,1,0:T(8,128)S(1)}, f32[8,1,8,128]{3,2,1,0:T(8,128)S(1)}, u32[]{:S(2)}, u32[]{:S(2)}) collective-permute-start(f32[8,1,8,128]{3,2,1,0:T(8,128)S(1)} %get-tuple-element.16), channel_id=1, source_target_pairs={{0,4},{4,8},{8,12},{12,16},{16,20},{20,24},{24,28},{28,32},{32,36}... | collective-permute-start | bytes 98312 | tf_op jit(solution)/shard_map/ppermute | solution.py:19
  6.2 8.7 %collective-permute-start.1 = (f32[8,1,8,128]{3,2,1,0:T(8,128)S(1)}, f32[8,1,8,128]{3,2,1,0:T(8,128)S(1)}, u32[]{:S(2)}, u32[]{:S(2)}) collective-permute-start(f32[8,1,8,128]{3,2,1,0:T(8,128)S(1)} %get-tuple-element.15), channel_id=1, source_target_pairs={{4,0},{8,4},{12,8},{16,12},{20,16},{24,20},{28,24},{32,28},{36,32}... | collective-permute-start | bytes 98312 | tf_op jit(solution)/shard_map/ppermute | solution.py:22
  9.0 5.8 %copy-start.2 = (f32[8,8,1024]{2,1,0:T(8,128)S(1)}, f32[8,8,1024]{2,1,0:T(8,128)}, u32[]{:S(2)}) copy-start(f32[8,8,1024]{2,1,0:T(8,128)} %param.7) | copy-start | bytes 786436
  9.0 11.0 %copy-start.4 = (bf16[2,4,2,4]{3,2,1,0:T(2,128)(2,1)S(1)}, bf16[2,4,2,4]{3,2,1,0:T(2,128)(2,1)}, u32[]{:S(2)}) copy-start(bf16[2,4,2,4]{3,2,1,0:T(2,128)(2,1)} %param.10) | copy-start | bytes 388
  9.1 11.7 %copy-start.3 = (f32[2,4,3,9]{3,1,2,0:T(4,128)S(1)}, f32[2,4,3,9]{3,1,2,0:T(4,128)}, u32[]{:S(2)}) copy-start(f32[2,4,3,9]{3,1,2,0:T(4,128)} %param.9) | copy-start | bytes 2596
  9.1 12.3 %copy-start.1 = (s32[16,4096]{1,0:T(8,128)S(1)}, s32[16,4096]{1,0:T(8,128)}, u32[]{:S(2)}) copy-start(s32[16,4096]{1,0:T(8,128)} %counts_ref.3) | copy-start | bytes 786436
  15.0 6.6 %collective-permute-start.2 = (f32[8,10,1,128]{3,2,1,0:T(1,128)S(1)}, f32[8,10,1,128]{3,2,1,0:T(1,128)S(1)}, u32[]{:S(2)}, u32[]{:S(2)}) collective-permute-start(f32[8,10,1,128]{3,2,1,0:T(1,128)S(1)} %get-tuple-element.13), channel_id=1, source_target_pairs={{0,1},{1,2},{2,3},{4,5},{5,6},{6,7},{8,9},{9,10},{10,11},{12,13},{... | collective-permute-start | bytes 122888 | tf_op jit(solution)/shard_map/ppermute | solution.py:19
  18.2 4.7 %collective-permute-start.3 = (f32[8,10,1,128]{3,2,1,0:T(1,128)S(1)}, f32[8,10,1,128]{3,2,1,0:T(1,128)S(1)}, u32[]{:S(2)}, u32[]{:S(2)}) collective-permute-start(f32[8,10,1,128]{3,2,1,0:T(1,128)S(1)} %get-tuple-element.14), channel_id=1, source_target_pairs={{1,0},{2,1},{3,2},{5,4},{6,5},{7,6},{9,8},{10,9},{11,10},{13,12},{... | collective-permute-start | bytes 122888 | tf_op jit(solution)/shard_map/ppermute | solution.py:22
  25.7 1.8 %copy-start = (bf16[3,8,8,24,384]{4,3,0,2,1:T(8,128)(2,1)}, bf16[3,8,8,24,384]{4,3,0,2,1:T(8,128)(2,1)S(1)}, u32[]{:S(2)}) copy-start(bf16[3,8,8,24,384]{4,3,0,2,1:T(8,128)(2,1)S(1)} %fusion.1) | copy-start | bytes 10616836
